TPU v7x, 128 devices: a whole 4x4x4 slice. The times are simulated.
128 devices in a mesh: seq: 32 (over y, x, z_lo), chan: 4 (over z_hi, core).
Axes of the slice: x: 4, y: 4, z: 4 (z_hi: 2, z_lo: 2; z = z_hi * 2 + z_lo), core: 2. Of those that a mesh axis runs over, the one named last changes fastest.
Arguments:
- tokens: bfloat16 [24576, 4096], P('seq', 'chan'), may hold values from -4 to 4
- w_in: bfloat16 [8, 4096, 1296], P('chan', 'seq'), may hold values from -1 to 1
- conv_w: float32 [8, 4, 1280], P('chan'), may hold values from -3 to 3
- conv_b: float32 [8, 1280], P('chan'), may hold values from -3 to 3
- dt_bias: float32 [8, 16], P('chan'), may hold values from -8 to 2
- a_log: float32 [8, 16], P('chan'), may hold values from -4.6 to -3.7
- d_skip: float32 [8, 16], P('chan'), may hold values from 0.3 to 3
- norm_gain: float32 [8, 1024], P('chan'), may hold values from 0.5 to 1.5
Outputs:
- mixer_out: bfloat16 [24576, 8192], P('seq', 'chan')
All inputs are finite; a program needn't handle non-finite values.
Results may differ from a plain program's by a relative error of at most 0.0076.
Values may be sent and summed in bfloat16 or wider, within the bound.
No kernel may reach another device: no remote copies, remote signals or barrier semaphores. Data moves between devices by JAX's collectives and lax.ppermute only.
A program may use at most 128 MiB of HBM per device.

v0:
```python
import jax
import jax.numpy as jnp
from jax import lax
from jax.sharding import PartitionSpec as P

P_SIZE = 64
N = 128
KCONV = 4
Q = 128
HG = 16
GW = 1024
CW = 1280


epsilon = 1e-05


def shifted(block, axis, distance):
    devices = range(lax.axis_size(axis))
    route = [(i - distance, i) for i in devices if i - distance in devices]
    return lax.ppermute(block, axis, route)


def entering(part, axis, combine, identity):
    place = lax.axis_index(axis)
    gathered = jax.tree.map(lambda a: lax.all_gather(a, axis), part)
    state = jax.tree.map(lambda a, e: jnp.zeros_like(a) + jnp.asarray(e, a.dtype), part, identity)

    def one(step, state):
        return combine(
            state, jax.tree.map(lambda a: lax.dynamic_index_in_dim(a, step, 0, False), gathered)
        )

    return lax.fori_loop(0, place, one, state)


def combine_states(earlier, later_one):
    return (earlier[0] * later_one[0], later_one[0][..., None, None] * earlier[1] + later_one[1])


def mix_groups(gathered, w_in, conv_w, conv_b, dt_bias, a_log, d_skip, norm_gain):
    groups = w_in.shape[0]
    row_count = gathered.shape[0]
    projected = jnp.einsum(
        "td,gdc->tgc",
        gathered,
        lax.all_gather(w_in, "seq", axis=1, tiled=True),
        preferred_element_type=jnp.float32,
    )
    conv_in = projected[:, :, :CW].astype(jnp.bfloat16)
    raw_dt = projected[gathered.shape[0] - row_count :, :, CW:]
    rim_rows = shifted(conv_in[row_count - (KCONV - 1) :], "seq", 1)
    padded = jnp.concatenate([rim_rows, conv_in], axis=0)
    pre_act = jnp.broadcast_to(conv_b[None], (row_count, groups, CW))
    for offset in range(KCONV):
        pre_act = pre_act + conv_w[None, :, offset] * padded[offset : offset + row_count]
    inputs = jax.nn.silu(pre_act).astype(jnp.bfloat16)
    block_count = row_count // Q
    blocked = inputs.reshape(block_count, Q, groups, CW)
    x_all = blocked[..., :GW].reshape(block_count, Q, groups, HG, P_SIZE)
    b_all = blocked[..., GW : GW + N]
    c_all = blocked[..., GW + N :]
    step_dt = jax.nn.softplus(raw_dt + dt_bias[None]).reshape(block_count, Q, groups, HG)
    decay_rate = -jnp.exp(a_log)
    cumulative = jnp.cumsum(decay_rate[None, None] * step_dt, axis=1)
    causal = lax.broadcasted_iota(jnp.int32, (Q, Q), 0) >= lax.broadcasted_iota(
        jnp.int32, (Q, Q), 1
    )

    def local_block(carried, block_in):
        state_now, factor = carried
        x_blk, b_blk, c_blk, dt_blk, cum_blk = block_in
        scores = jnp.einsum("ign,jgn->gij", c_blk, b_blk, preferred_element_type=jnp.float32)
        cum_cols = jnp.transpose(cum_blk, (1, 2, 0))
        dt_cols = jnp.transpose(dt_blk, (1, 2, 0))
        spread = cum_cols[..., :, None] - cum_cols[..., None, :]
        damping = jnp.where(causal, jnp.exp(jnp.minimum(spread, 0.0)), 0.0)
        weights = (scores[:, None] * damping * dt_cols[..., None, :]).astype(jnp.bfloat16)
        partial_y = jnp.einsum(
            "ghij,jghp->ighp", weights, x_blk, preferred_element_type=jnp.float32
        )
        partial_y = partial_y + d_skip[None, :, :, None] * x_blk
        last_cum = cum_blk[-1]
        tail_factor = jnp.exp(last_cum[None] - cum_blk) * dt_blk
        scaled = (x_blk * tail_factor[..., None]).astype(jnp.bfloat16)
        fresh_state = jnp.einsum(
            "jghp,jgn->ghpn", scaled, b_blk, preferred_element_type=jnp.float32
        )
        keep_blk = jnp.exp(last_cum)
        carried_next = (keep_blk[..., None, None] * state_now + fresh_state, factor * keep_blk)
        return (carried_next, (partial_y, fresh_state, keep_blk))

    zero_state = jnp.zeros((groups, HG, P_SIZE, N), jnp.float32)
    unit_keep = jnp.ones((groups, HG), jnp.float32)
    (local_end, local_keep), (partial_all, fresh_all, keep_all) = lax.scan(
        local_block, (zero_state, unit_keep), (x_all, b_all, c_all, step_dt, cumulative)
    )
    _, incoming = entering((local_keep, local_end), "seq", combine_states, (unit_keep, zero_state))

    def finish_block(state_now, block_in):
        partial_y, fresh_state, keep_blk, c_blk, cum_blk = block_in
        across = jnp.einsum(
            "ign,ghpn->ighp",
            c_blk,
            state_now.astype(jnp.bfloat16),
            preferred_element_type=jnp.float32,
        )
        activity = partial_y + jnp.exp(cum_blk)[..., None] * across
        flat_act = activity.reshape(Q, groups, GW)
        inv_rms = lax.rsqrt(jnp.mean(flat_act * flat_act, axis=-1, keepdims=True) + epsilon)
        normed = (flat_act * inv_rms * norm_gain[None]).astype(jnp.bfloat16)
        return (keep_blk[..., None, None] * state_now + fresh_state, normed)

    _, outputs = lax.scan(
        finish_block, incoming, (partial_all, fresh_all, keep_all, c_all, cumulative)
    )
    return outputs.reshape(row_count, groups * GW)


def per_device(tokens, w_in, conv_w, conv_b, dt_bias, a_log, d_skip, norm_gain):
    gathered = lax.all_gather(tokens, "chan", axis=1, tiled=True)
    return mix_groups(gathered, w_in, conv_w, conv_b, dt_bias, a_log, d_skip, norm_gain)


def solution(mesh):
    return jax.shard_map(
        per_device,
        mesh=mesh,
        in_specs=(
            P("seq", "chan"),
            P("chan", "seq", None),
            P("chan", None, None),
            P("chan", None),
            P("chan", None),
            P("chan", None),
            P("chan", None),
            P("chan", None),
        ),
        out_specs=P("seq", "chan"),
        check_vma=False,
    )
```

profile of v0, /device:TPU:22, one launch (start us, length us, event | category | flops | bytes accessed | tf_op | source)
XLA Modules:
  0.0 1470.4 jit_solution(51003138211059274)
XLA Ops:
  9.8 51.9 %all-gather.7.cloned.1.call-done = bf16[768,4096]{1,0:T(8,128)(2,1)} async-done(((bf16[768,1024]{1,0:T(8,128)(2,1)}), bf16[768,4096]{1,0:T(8,128)(2,1)}) %all-gather.7.cloned.1.call-update) | async-done | bytes 6291472 | tf_op jit(solution)/shard_map/all_gather | solution.py:121
  61.8 510.8 %all-gather.9.cloned.1.call-done = bf16[2,4096,1296]{1,2,0:T(8,128)(2,1)} async-done(((bf16[2,128,1296]{1,2,0:T(8,128)(2,1)}), bf16[2,4096,1296]{1,2,0:T(8,128)(2,1)}) %all-gather.9.cloned.1.call-update) | async-done | bytes 21233680 | tf_op jit(solution)/shard_map/all_gather | solution.py:47
  572.5 23.0 %fusion.48 = (bf16[768,2,1296]{0,2,1:T(8,128)(2,1)S(1)}, f32[768,2,1296]{0,2,1:T(8,128)}) fusion(bf16[2,4096,1296]{1,2,0:T(8,128)(2,1)} %all-gather.9.cloned.1.call-done, bf16[768,4096]{1,0:T(8,128)(2,1)} %all-gather.7.cloned.1.call-done), kind=kOutput, calls=%fused_computation.84 | convolution fusion | flops 16309444608 | bytes 39469056 | tf_op jit(solution)/shard_map/td,gdc->tgc/dot_general | solution.py:44
  595.5 1.9 copy-done.1
  597.9 1.9 collective-permute-start
  601.7 4.2 slice.61
  606.7 14.2 multiply_convert_fusion.2
  620.9 6.1 copy.40
  628.2 3.9 slice.66
  632.1 4.7 copy.41
  636.8 37.4 %while.45 = (s32[]{:T(128)}, f32[2,16,64,128]{3,2,1,0:T(8,128)S(1)}, f32[2,16]{1,0:T(2,128)S(1)}, f32[6,128,2,16,64]{1,4,3,2,0:T(8,128)}, f32[6,2,16,64,128]{4,3...) while((s32[]{:T(128)}, ...), condition=%wide.region_2.3_spmd.clone, body=%wide.region_1.2_spmd.clone.sunk | while | flops 148136000 | bytes 8544956 | solution.py:95
  639.9 3.1 fusion.69
  643.3 1.5 fusion.67
  646.1 3.2 fusion.69
  649.6 1.5 fusion.67
  652.4 3.2 fusion.69
  655.9 1.5 fusion.67
  658.7 3.2 fusion.69
  662.1 1.5 fusion.67
  664.9 3.1 fusion.69
  671.1 3.2 fusion.69
  675.2 79.1 %all-gather.2 = f32[32,2,16]{2,1,0:T(2,128)S(1)} all-gather(f32[1,2,16]{2,1,0:T(2,128)S(1)} %bitcast.159), channel_id=2, replica_groups=mesh['seq'=32,'chan'=4] {'seq'}, dimensions={0}, use_global_device_ids=true | all-gather | bytes 4224 | tf_op jit(solution)/shard_map/all_gather | solution.py:26
  754.3 641.2 %all-gather.11.cloned.1.call-done = f32[64,16,64,128]{3,2,1,0:T(8,128)} async-done(((f32[2,16,64,128]{3,2,1,0:T(8,128)}), f32[64,16,64,128]{3,2,1,0:T(8,128)}) %all-gather.11.cloned.1.call-update) | async-done | bytes 33554448 | tf_op jit(solution)/shard_map/all_gather | solution.py:26
  1395.6 33.1 %while.43 = (s32[]{:T(128)}, f32[2,16,64,128]{3,2,1,0:T(8,128)S(1)}, s32[]{:T(128)}, f32[32,2,16]{2,1,0:T(2,128)S(1)}, f32[32,2,16,64,128]{4,3,2,1,0:T(8,128)}, /*index=5*/s32[]{:T(128)}, s32[]{:T(128)}, s32[]{:T(128)}) while((s32[]{:T(128)}, f32[2,16,64,128]{3,2,1,0:T(8,128)S(1)}, s32[]{:T(128)}, f32[32,2,16]{2,1,0:T(2,128)S(1)}, ...), condition=%wide.region_4.5_spmd, body=%wide.region_3.4_spmd.sunk | while | flops 524293 | bytes 3146239 | solution.py:34
  1428.7 30.6 %while.44 = (s32[]{:T(128)}, f32[2,16,64,128]{3,2,1,0:T(8,128)S(1)}, bf16[6,128,2,1024]{3,2,1,0:T(2,128)(2,1)}, f32[6,2,16]{2,1,0:T(2,128)S(1)}, f32[6,2,16,64,1...) while((s32[]{:T(128)}, ...), condition=%wide.region_7.8_spmd, body=%wide.region_5.7_spmd.sunk | while | flops 69730560 | bytes 10090481 | solution.py:114
  1428.8 1.6 multiply_reduce_fusion.2
  1433.9 1.6 multiply_reduce_fusion.2
  1439.0 1.6 multiply_reduce_fusion.2
  1444.1 1.6 multiply_reduce_fusion.2
  1449.1 1.5 multiply_reduce_fusion.2
  1454.2 1.6 multiply_reduce_fusion.2
  1459.3 4.6 copy.59
  (182 shorter events, 73.8 us)
Async XLA Ops:
  6.5 55.2 %all-gather.7.cloned.1.call-start = ((), (), s32[]{:S(2)}) async-start(), calls=%async_computation | async-start | bytes 7864320 | tf_op jit(solution)/shard_map/all_gather | solution.py:121
  7.3 565.3 %all-gather.9.cloned.1.call-start = ((), (), s32[]{:S(2)}) async-start(), calls=%async_computation.1 | async-start | bytes 21897216 | tf_op jit(solution)/shard_map/all_gather | solution.py:47
  8.0 1387.5 %all-gather.11.cloned.1.call-start = ((), (), s32[]{:S(2)}) async-start(), calls=%async_computation.2 | async-start | bytes 34603008 | tf_op jit(solution)/shard_map/all_gather | solution.py:26
  9.8 590.1 %copy-start.4 = (f32[2,16]{1,0:T(2,128)S(1)}, f32[2,16]{1,0:T(2,128)}, u32[]{:S(2)}) copy-start(f32[2,16]{1,0:T(2,128)} %param.18) | copy-start | bytes 388
  595.5 1.9 copy-start.1
  597.9 8.3 collective-permute-start
  599.9 6.8 copy-start.3
  628.2 8.6 copy-start.5
  674.2 1.0 copy-start
  1395.6 33.1 %copy-start.2 = (f32[2,1024]{1,0:T(2,128)S(1)}, f32[2,1024]{1,0:T(2,128)}, u32[]{:S(2)}) copy-start(f32[2,1024]{1,0:T(2,128)} %param.21) | copy-start | bytes 24580
Sparse Core Ops, SparseCore 0:
  9.0 52.6 all-gather.6
  63.3 509.1 all-gather.8
  675.4 720.1 all-gather.10
where the time goes:
time: 1490 us; the launch traced here: 1470 us
  waiting for transfers between devices  1210 us (81%)
  blocking collectives  79.1 us (5%)
  matrix products  61.1 us (4%)
  other arithmetic  59.5 us (4%)
  local copies, waits for them, and re-layouts  48.4 us (3%)
    all_gather x1, waiting for transfers between devices, entering(): gathered = jax.tree.map(lambda a: lax.all_gather(a, axis), part)  641 us
    all_gather x1, waiting for transfers between devices, mix_groups(): lax.all_gather(w_in, 'seq', axis=1, tiled=True)  511 us
    all_gather x1, blocking collectives, entering(): gathered = jax.tree.map(lambda a: lax.all_gather(a, axis), part)  79.1 us
    all_gather x1, waiting for transfers between devices, per_device(): gathered = lax.all_gather(tokens, 'chan', axis=1, tiled=True)  51.9 us
    add x22, other arithmetic, combine_states(): later_one[0][..., None, None] * earlier[1] + later_one[1]  31.8 us
  transfers between devices with their start and end apart: 4, of which 3 were waited for; matrix products, arithmetic and copies ran while one was open for 1% of the time, Pallas kernels for 0%

commit v1 on v0

v1 whole, which is shorter than its diff:
```python
import jax
import jax.numpy as jnp
from jax import lax
from jax.sharding import PartitionSpec as P

P_SIZE = 64
N = 128
KCONV = 4
Q = 128
HG = 16
GW = 1024
CW = 1280


epsilon = 1e-05


def shifted(block, axis, distance):
    devices = range(lax.axis_size(axis))
    route = [(i - distance, i) for i in devices if i - distance in devices]
    return lax.ppermute(block, axis, route)


def entering(keep, end, axis):
    place = lax.axis_index(axis)
    size = lax.axis_size(axis)
    keep = jnp.where(place == 0, 1.0, shifted(keep, axis, 1))
    end = shifted(end, axis, 1)
    distance = 1
    while distance < size:
        earlier_end = shifted(end, axis, distance)
        reach = place >= distance
        end = jnp.where(reach, keep[..., None, None] * earlier_end + end, end)
        if distance * 2 < size:
            earlier_keep = shifted(keep, axis, distance)
            keep = jnp.where(reach, keep * earlier_keep, keep)
        distance *= 2
    return end


def mix_groups(gathered, w_in, conv_w, conv_b, dt_bias, a_log, d_skip, norm_gain):
    groups = w_in.shape[0]
    row_count = gathered.shape[0]
    rows_first = jnp.transpose(w_in, (1, 0, 2))
    full_w = lax.all_gather(rows_first, "seq", axis=0, tiled=True)
    projected = jnp.einsum(
        "td,dgc->tgc",
        gathered,
        full_w,
        preferred_element_type=jnp.float32,
    )
    conv_in = projected[:, :, :CW].astype(jnp.bfloat16)
    raw_dt = projected[:, :, CW:]
    rim_rows = shifted(conv_in[row_count - (KCONV - 1) :], "seq", 1)
    padded = jnp.concatenate([rim_rows, conv_in], axis=0)
    pre_act = jnp.broadcast_to(conv_b[None], (row_count, groups, CW))
    for offset in range(KCONV):
        pre_act = pre_act + conv_w[None, :, offset] * padded[offset : offset + row_count]
    inputs = jax.nn.silu(pre_act).astype(jnp.bfloat16)
    block_count = row_count // Q
    blocked = inputs.reshape(block_count, Q, groups, CW)
    x_all = blocked[..., :GW].reshape(block_count, Q, groups, HG, P_SIZE)
    b_all = blocked[..., GW : GW + N]
    c_all = blocked[..., GW + N :]
    step_dt = jax.nn.softplus(raw_dt + dt_bias[None]).reshape(block_count, Q, groups, HG)
    decay_rate = -jnp.exp(a_log)
    cumulative = jnp.cumsum(decay_rate[None, None] * step_dt, axis=1)
    causal = lax.broadcasted_iota(jnp.int32, (Q, Q), 0) >= lax.broadcasted_iota(
        jnp.int32, (Q, Q), 1
    )

    last_cum = cumulative[:, -1]
    keep_all = jnp.exp(last_cum)
    tail_factor = jnp.exp(last_cum[:, None] - cumulative) * step_dt
    scaled = (x_all * tail_factor[..., None]).astype(jnp.bfloat16)
    fresh_all = jnp.einsum(
        "qjghp,qjgn->qghpn", scaled, b_all, preferred_element_type=jnp.float32
    )

    local_states = []
    state_now = jnp.zeros(fresh_all.shape[1:], jnp.float32)
    keep_now = jnp.ones(keep_all.shape[1:], jnp.float32)
    keep_before = []
    for q in range(block_count):
        local_states.append(state_now)
        keep_before.append(keep_now)
        state_now = keep_all[q][..., None, None] * state_now + fresh_all[q]
        keep_now = keep_now * keep_all[q]
    incoming = entering(keep_now, state_now, "seq")
    states = jnp.stack(local_states) + jnp.stack(keep_before)[..., None, None] * incoming[None]

    scores = jnp.einsum("qign,qjgn->qgij", c_all, b_all, preferred_element_type=jnp.float32)
    cum_cols = jnp.transpose(cumulative, (0, 2, 3, 1))
    dt_cols = jnp.transpose(step_dt, (0, 2, 3, 1))
    spread = cum_cols[..., :, None] - cum_cols[..., None, :]
    damping = jnp.where(causal, jnp.exp(jnp.minimum(spread, 0.0)), 0.0)
    weights = (scores[:, :, None] * damping * dt_cols[..., None, :]).astype(jnp.bfloat16)
    partial_y = jnp.einsum(
        "qghij,qjghp->qighp", weights, x_all, preferred_element_type=jnp.float32
    )
    partial_y = partial_y + d_skip[None, None, :, :, None] * x_all

    across = jnp.einsum(
        "qign,qghpn->qighp",
        c_all,
        states.astype(jnp.bfloat16),
        preferred_element_type=jnp.float32,
    )
    activity = partial_y + jnp.exp(cumulative)[..., None] * across
    flat_act = activity.reshape(row_count, groups, GW)
    inv_rms = lax.rsqrt(jnp.mean(flat_act * flat_act, axis=-1, keepdims=True) + epsilon)
    normed = (flat_act * inv_rms * norm_gain[None]).astype(jnp.bfloat16)
    return normed.reshape(row_count, groups * GW)


def per_device(tokens, w_in, conv_w, conv_b, dt_bias, a_log, d_skip, norm_gain):
    gathered = lax.all_gather(tokens, "chan", axis=1, tiled=True)
    return mix_groups(gathered, w_in, conv_w, conv_b, dt_bias, a_log, d_skip, norm_gain)


def solution(mesh):
    return jax.shard_map(
        per_device,
        mesh=mesh,
        in_specs=(
            P("seq", "chan"),
            P("chan", "seq", None),
            P("chan", None, None),
            P("chan", None),
            P("chan", None),
            P("chan", None),
            P("chan", None),
            P("chan", None),
        ),
        out_specs=P("seq", "chan"),
        check_vma=False,
    )
```

time: 1490 us -> 844 us (0.57)
  waiting for transfers between devices: 1210 us -> 654 us
  blocking collectives: 79.1 us -> 0 us
  starting transfers between devices: 2 us -> 44.4 us
  matrix products: 61.1 us -> 38.1 us
  other arithmetic: 59.5 us -> 38.9 us
    all_gather x2 -> x1, waiting for transfers between devices: 1150 us -> 511 us  [mix_groups(): full_w = lax.all_gather(rows_first, 'seq', axis=0, tiled=True)]
    ppermute x1 -> x12, waiting for transfers between devices: 0.01 us -> 89.7 us  [shifted(): return lax.ppermute(block, axis, route)]
    all_gather x1 -> x0, blocking collectives: 79.1 us -> none  [entering(): gathered = jax.tree.map(lambda a: lax.all_gather(a, axis), part)]
    ppermute x1 -> x12, starting transfers between devices: 1.92 us -> 44.4 us  [shifted(): return lax.ppermute(block, axis, route)]
    add x28 -> x1, other arithmetic: 40.5 us -> 0.48 us  [mix_groups(): state_now = keep_all[q][..., None, None] * state_now + fresh_all[q]]
    dot_general x25 -> x5, matrix products: 61.1 us -> 38.1 us  [the longest x1 22.6 us: mix_groups(): jnp.einsum('td,dgc->tgc', gathered, full_w, preferred_element_type=jnp.fl...]
    dynamic_update_slice x24 -> x0, local copies, waits for them, and re-layouts: 16.7 us -> none  [the longest x12 10.2 us: mix_groups(): lax.scan(finish_block, incoming, (partial_all, fresh_all, keep_all, c_all...]
  transfers between devices with their start and end apart: 4 -> 14, of which waited for: 3 -> 11; matrix products, arithmetic and copies ran while one was open for 1% -> 5% of each run, Pallas kernels for 0% -> 0%
where the time goes in v1:
time: 844 us; the launch traced here: 832 us
  waiting for transfers between devices  654 us (77%)
  starting transfers between devices  44.4 us (5%)
  local copies, waits for them, and re-layouts  43 us (5%)
  other arithmetic  38.9 us (5%)
  matrix products  38.1 us (5%)
  between operations  14 us (2%)
    all_gather x1, waiting for transfers between devices, mix_groups(): full_w = lax.all_gather(rows_first, 'seq', axis=0, tiled=True)  511 us
    ppermute x12, waiting for transfers between devices, shifted(): return lax.ppermute(block, axis, route)  89.7 us
    all_gather x1, waiting for transfers between devices, per_device(): gathered = lax.all_gather(tokens, 'chan', axis=1, tiled=True)  52 us
    ppermute x12, starting transfers between devices, shifted(): return lax.ppermute(block, axis, route)  44.4 us
    dot_general x1, matrix products, mix_groups(): jnp.einsum('td,dgc->tgc', gathered, full_w, preferred_element_type=jnp.fl...  22.6 us
  transfers between devices with their start and end apart: 14, of which 11 were waited for; matrix products, arithmetic and copies ran while one was open for 5% of the time, Pallas kernels for 0%

profile of v1, /device:TPU:22, one launch (start us, length us, event | category | flops | bytes accessed | tf_op | source)
XLA Modules:
  0.0 832.3 jit_solution(2859440067428863867)
XLA Ops:
  9.7 52.0 %all-gather.3.cloned.1.call-done = bf16[768,4096]{1,0:T(8,128)(2,1)} async-done(((bf16[768,1024]{1,0:T(8,128)(2,1)}), bf16[768,4096]{1,0:T(8,128)(2,1)}) %all-gather.3.cloned.1.call-update) | async-done | bytes 6291472 | tf_op jit(solution)/shard_map/all_gather | solution.py:117
  61.8 510.8 %all-gather.5.cloned.1.call-done = bf16[4096,2,1296]{0,2,1:T(8,128)(2,1)} async-done(((bf16[128,2,1296]{0,2,1:T(8,128)(2,1)}), bf16[4096,2,1296]{0,2,1:T(8,128)(2,1)}) %all-gather.5.cloned.1.call-update) | async-done | bytes 21233680 | tf_op jit(solution)/shard_map/all_gather | solution.py:45
  572.5 22.6 %fusion.45 = (bf16[768,2,1296]{0,2,1:T(8,128)(2,1)}, f32[768,2,1296]{0,2,1:T(8,128)S(1)}) fusion(bf16[4096,2,1296]{0,2,1:T(8,128)(2,1)} %all-gather.5.cloned.1.call-done, bf16[768,4096]{1,0:T(8,128)(2,1)} %all-gather.3.cloned.1.call-done), kind=kOutput, calls=%fused_computation.110 | convolution fusion | flops 16309444608 | bytes 39469056 | tf_op jit(solution)/shard_map/td,dgc->tgc/dot_general | solution.py:46
  598.8 2.1 collective-permute-start
  603.2 4.3 slice.113
  608.8 14.2 %multiply_convert_fusion.1 = bf16[768,2,1280]{0,2,1:T(8,128)(2,1)} fusion(bf16[768,2,1280]{0,2,1:T(8,128)(2,1)} %slice.113, bf16[3,2,1280]{0,2,1:T(8,128)(2,1)S(1)} %copy.46, f32[2,1280]{1,0:T(2,128)S(1)} %get-tuple-element.31, f32[2,1280]{1,0:T(2,128)S(1)} %get-tuple-element.32, f32[2,1280]{1,0:T(2,128)S(1)} %get-tuple-element.33, ...), kind=kLoop, calls=%fused_computation.3 | loop fusion | flops 51118080 | bytes 7930880 | tf_op jit(solution)/shard_map/convert_element_type | solution.py:59
  623.0 6.3 copy.47
  629.3 3.9 slice.118
  635.1 3.5 copy.48
  638.7 2.0 fusion.17
  640.7 2.7 copy-done
  643.8 6.9 collective-permute-start.6
  650.8 16.2 %collective-permute-done.6 = f32[2,16,64,128]{3,2,1,0:T(8,128)} collective-permute-done((f32[2,16,64,128]{3,2,1,0:T(8,128)S(1)}, f32[2,16,64,128]{3,2,1,0:T(8,128)}, u32[]{:S(2)}, u32[]{:S(2)}) %collective-permute-start.6) | collective-permute-done | bytes 1048608 | tf_op jit(solution)/shard_map/ppermute | solution.py:21
  667.0 3.5 collective-permute-start.7
  670.5 6.4 collective-permute-start.1
  676.9 12.8 %collective-permute-done.1 = f32[2,16]{1,0:T(2,128)S(1)} collective-permute-done((f32[2,16]{1,0:T(2,128)}, f32[2,16]{1,0:T(2,128)S(1)}, u32[]{:S(2)}, u32[]{:S(2)}) %collective-permute-start.1) | collective-permute-done | bytes 160 | tf_op jit(solution)/shard_map/ppermute | solution.py:21
  691.7 7.3 collective-permute-start.8
  702.8 7.2 collective-permute-done.2
  711.3 11.3 %collective-permute-done.8 = f32[2,16,64,128]{3,2,1,0:T(8,128)} collective-permute-done((f32[2,16,64,128]{3,2,1,0:T(8,128)S(1)}, f32[2,16,64,128]{3,2,1,0:T(8,128)}, u32[]{:S(2)}, u32[]{:S(2)}) %collective-permute-start.8) | collective-permute-done | bytes 1048608 | tf_op jit(solution)/shard_map/ppermute | solution.py:21
  726.9 6.7 collective-permute-start.3
  735.6 9.0 %collective-permute-done.3 = f32[2,16]{1,0:T(2,128)} collective-permute-done((f32[2,16]{1,0:T(2,128)}, f32[2,16]{1,0:T(2,128)}, u32[]{:S(2)}, u32[]{:S(2)}) %collective-permute-start.3) | collective-permute-done | bytes 160 | tf_op jit(solution)/shard_map/ppermute | solution.py:21
  745.2 2.5 collective-permute-start.4
  749.3 2.9 collective-permute-done.4
  756.6 3.3 collective-permute-done.5
  760.5 2.6 fusion.28
  766.4 2.7 constant_dynamic-update-slice_fusion.1
  772.9 19.3 %collective-permute-done.10 = f32[2,16,64,128]{3,2,1,0:T(8,128)S(1)} collective-permute-done((f32[2,16,64,128]{3,2,1,0:T(8,128)S(1)}, f32[2,16,64,128]{3,2,1,0:T(8,128)S(1)}, u32[]{:S(2)}, u32[]{:S(2)}) %collective-permute-start.10) | collective-permute-done | bytes 1048608 | tf_op jit(solution)/shard_map/ppermute | solution.py:21
  794.8 8.7 %fusion = f32[6,2,16,64,128]{4,3,2,1,0:T(8,128)} fusion(bf16[6,128,2,16,64]{1,4,3,2,0:T(8,128)(2,1)S(1)} %bitcast.132, f32[6,2,16,128]{3,2,1,0:T(8,128)S(1)} %copy-done.9, f32[6,2,16,128]{3,2,1,0:T(8,128)S(1)} %copy-done.8, f32[6,2,128,128]{3,2,1,0:T(8,128)S(1)} %fusion.32, pred[128,128]{1,0:T(8,128)(4,1)S(1)} %copy-done.10), kind=kOutput, calls=%fused_computation.4 | convolution fusion | flops 421527552 | bytes 10436608 | tf_op jit(solution)/shard_map/qghij,qjghp->qighp/dot_general | solution.py:98
  803.6 7.7 collective-permute-done.11
  811.5 4.4 multiply_reduce_fusion
  815.9 5.6 copy.58
  822.6 2.9 copy.59
  (117 shorter events, 44.2 us)
Async XLA Ops:
  6.5 55.2 %all-gather.3.cloned.1.call-start = ((), (), s32[]{:S(2)}) async-start(), calls=%async_computation | async-start | bytes 7864320 | tf_op jit(solution)/shard_map/all_gather | solution.py:117
  7.3 565.3 %all-gather.5.cloned.1.call-start = ((), (), s32[]{:S(2)}) async-start(), calls=%async_computation.1 | async-start | bytes 21897216 | tf_op jit(solution)/shard_map/all_gather | solution.py:45
  9.7 585.4 %copy-start.22 = (f32[2,16]{1,0:T(2,128)S(1)}, f32[2,16]{1,0:T(2,128)}, u32[]{:S(2)}) copy-start(f32[2,16]{1,0:T(2,128)} %param.12) | copy-start | bytes 388
  596.1 11.3 %copy-start.3 = (f32[6,128,2,16]{3,2,1,0:T(2,128)}, f32[6,128,2,16]{3,2,1,0:T(2,128)S(1)}, u32[]{:S(2)}) copy-start(f32[6,128,2,16]{3,2,1,0:T(2,128)S(1)} %fusion.46) | copy-start | bytes 294916
  598.8 9.6 %collective-permute-start = (bf16[3,2,1280]{2,1,0:T(2,128)(2,1)S(1)}, bf16[3,2,1280]{2,1,0:T(2,128)(2,1)S(1)}, u32[]{:S(2)}, u32[]{:S(2)}) collective-permute-start(bf16[3,2,1280]{2,1,0:T(2,128)(2,1)S(1)} %copy.45), channel_id=1, source_target_pairs={{0,4},{4,8},{8,12},{12,16},{16,20},{20,24},{24,28},{28,32},{32,36}... | collective-permute-start | bytes 46088 | tf_op jit(solution)/shard_map/ppermute | solution.py:21
  603.1 19.8 %copy-start.18 = (f32[6,2,16]{2,1,0:T(2,128)}, f32[6,2,16]{2,1,0:T(2,128)S(1)}, u32[]{:S(2)}) copy-start(f32[6,2,16]{2,1,0:T(2,128)S(1)} %get-tuple-element.19) | copy-start | bytes 2308
  603.2 37.5 %copy-start.13 = (f32[2,16]{1,0:T(2,128)}, f32[2,16]{1,0:T(2,128)S(1)}, u32[]{:S(2)}) copy-start(f32[2,16]{1,0:T(2,128)S(1)} %get-tuple-element.21) | copy-start | bytes 388
  603.2 37.5 %copy-start.15 = (f32[2,16]{1,0:T(2,128)}, f32[2,16]{1,0:T(2,128)S(1)}, u32[]{:S(2)}) copy-start(f32[2,16]{1,0:T(2,128)S(1)} %get-tuple-element.22) | copy-start | bytes 388
  643.8 23.1 %collective-permute-start.6 = (f32[2,16,64,128]{3,2,1,0:T(8,128)S(1)}, f32[2,16,64,128]{3,2,1,0:T(8,128)}, u32[]{:S(2)}, u32[]{:S(2)}) collective-permute-start(f32[2,16,64,128]{3,2,1,0:T(8,128)S(1)} %fusion.22), channel_id=1, source_target_pairs={{0,4},{4,8},{8,12},{12,16},{16,20},{20,24},{24,28},{28,32},{32,36}... | collective-permute-start | bytes 3145736 | tf_op jit(solution)/shard_map/ppermute | solution.py:21
  667.0 23.3 %collective-permute-start.7 = (f32[2,16,64,128]{3,2,1,0:T(8,128)}, f32[2,16,64,128]{3,2,1,0:T(8,128)S(1)}, u32[]{:S(2)}, u32[]{:S(2)}) collective-permute-start(f32[2,16,64,128]{3,2,1,0:T(8,128)} %collective-permute-done.6), channel_id=1, source_target_pairs={{0,4},{4,8},{8,12},{12,16},{16,20},{20,24},{24,28},{28,32},{32,36}... | collective-permute-start | bytes 3145736 | tf_op jit(solution)/shard_map/ppermute | solution.py:21
  670.5 19.2 %collective-permute-start.1 = (f32[2,16]{1,0:T(2,128)}, f32[2,16]{1,0:T(2,128)S(1)}, u32[]{:S(2)}, u32[]{:S(2)}) collective-permute-start(f32[2,16]{1,0:T(2,128)} %get-tuple-element.25), channel_id=1, source_target_pairs={{0,4},{4,8},{8,12},{12,16},{16,20},{20,24},{24,28},{28,32},{32,36}... | collective-permute-start | bytes 392 | tf_op jit(solution)/shard_map/ppermute | solution.py:21
  689.7 12.4 %copy-start.20 = (f32[2,16]{1,0:T(2,128)}, f32[2,16]{1,0:T(2,128)S(1)}, u32[]{:S(2)}) copy-start(f32[2,16]{1,0:T(2,128)S(1)} %collective-permute-done.1) | copy-start | bytes 388
  691.7 19.6 %copy-start.4 = (f32[2,16,64,128]{3,2,1,0:T(8,128)}, f32[2,16,64,128]{3,2,1,0:T(8,128)S(1)}, u32[]{:S(2)}) copy-start(f32[2,16,64,128]{3,2,1,0:T(8,128)S(1)} %add_select_fusion.4) | copy-start | bytes 3145732
  691.7 30.9 %collective-permute-start.8 = (f32[2,16,64,128]{3,2,1,0:T(8,128)S(1)}, f32[2,16,64,128]{3,2,1,0:T(8,128)}, u32[]{:S(2)}, u32[]{:S(2)}) collective-permute-start(f32[2,16,64,128]{3,2,1,0:T(8,128)S(1)} %add_select_fusion.4), channel_id=1, source_target_pairs={{0,8},{4,12},{8,16},{12,20},{16,24},{20,28},{24,32},{28,36},{32,40... | collective-permute-start | bytes 3145736 | tf_op jit(solution)/shard_map/ppermute | solution.py:21
  699.1 70.1 %slice-start = ((s8[6291456]{0:T(1024)(128)(4,1)}), s8[2097152]{0:T(1024)(128)(4,1)S(1)}, s32[]{:S(2)}) async-start(s8[6291456]{0:T(1024)(128)(4,1)} %bitcast.128), calls=%async_computation.2 | async-start | bytes 4194304
  700.2 9.9 %collective-permute-start.2 = (f32[2,16]{1,0:T(2,128)}, f32[2,16]{1,0:T(2,128)S(1)}, u32[]{:S(2)}, u32[]{:S(2)}) collective-permute-start(f32[2,16]{1,0:T(2,128)} %broadcast_select_fusion), channel_id=1, source_target_pairs={{0,4},{4,8},{8,12},{12,16},{16,20},{20,24},{24,28},{28,32},{32,36}... | collective-permute-start | bytes 392 | tf_op jit(solution)/shard_map/ppermute | solution.py:21
  724.4 38.7 %collective-permute-start.9 = (f32[2,16,64,128]{3,2,1,0:T(8,128)S(1)}, f32[2,16,64,128]{3,2,1,0:T(8,128)}, u32[]{:S(2)}, u32[]{:S(2)}) collective-permute-start(f32[2,16,64,128]{3,2,1,0:T(8,128)S(1)} %add_select_fusion.3), channel_id=1, source_target_pairs={{0,16},{4,20},{8,24},{12,28},{16,32},{20,36},{24,40},{28,44},{32,4... | collective-permute-start | bytes 3145736 | tf_op jit(solution)/shard_map/ppermute | solution.py:21
  726.9 17.6 %collective-permute-start.3 = (f32[2,16]{1,0:T(2,128)}, f32[2,16]{1,0:T(2,128)}, u32[]{:S(2)}, u32[]{:S(2)}) collective-permute-start(f32[2,16]{1,0:T(2,128)} %multiply_select_fusion.3), channel_id=1, source_target_pairs={{0,8},{4,12},{8,16},{12,20},{16,24},{20,28},{24,32},{28,36},{32,40... | collective-permute-start | bytes 392 | tf_op jit(solution)/shard_map/ppermute | solution.py:21
  745.2 7.0 collective-permute-start.4
  752.8 7.1 collective-permute-start.5
  764.5 27.7 %collective-permute-start.10 = (f32[2,16,64,128]{3,2,1,0:T(8,128)S(1)}, f32[2,16,64,128]{3,2,1,0:T(8,128)S(1)}, u32[]{:S(2)}, u32[]{:S(2)}) collective-permute-start(f32[2,16,64,128]{3,2,1,0:T(8,128)S(1)} %add_select_fusion.2), channel_id=1, source_target_pairs={{0,32},{4,36},{8,40},{12,44},{16,48},{20,52},{24,56},{28,60},{32,6... | collective-permute-start | bytes 3145736 | tf_op jit(solution)/shard_map/ppermute | solution.py:21
  770.4 24.0 %copy-start.5 = (bf16[6,128,2,128]{3,1,0,2:T(8,128)(2,1)S(1)}, bf16[6,128,2,128]{3,1,0,2:T(8,128)(2,1)}, u32[]{:S(2)}) copy-start(bf16[6,128,2,128]{3,1,0,2:T(8,128)(2,1)} %get-tuple-element.11) | copy-start | bytes 1179652
  770.4 24.4 %copy-start.2 = (bf16[6,128,2,1024]{1,3,2,0:T(8,128)(2,1)S(1)}, bf16[6,128,2,1024]{1,3,2,0:T(8,128)(2,1)}, u32[]{:S(2)}) copy-start(bf16[6,128,2,1024]{1,3,2,0:T(8,128)(2,1)} %copy-done.1) | copy-start | bytes 9437188
  770.4 24.4 %copy-start.8 = (f32[6,2,16,128]{3,2,1,0:T(8,128)S(1)}, f32[6,2,16,128]{3,2,1,0:T(8,128)}, u32[]{:S(2)}) copy-start(f32[6,2,16,128]{3,2,1,0:T(8,128)} %copy.52) | copy-start | bytes 294916
  770.4 24.4 %copy-start.9 = (f32[6,2,16,128]{3,2,1,0:T(8,128)S(1)}, f32[6,2,16,128]{3,2,1,0:T(8,128)}, u32[]{:S(2)}) copy-start(f32[6,2,16,128]{3,2,1,0:T(8,128)} %copy.54) | copy-start | bytes 294916
  770.4 24.4 %copy-start.10 = (pred[128,128]{1,0:T(8,128)(4,1)S(1)}, pred[128,128]{1,0:T(8,128)(4,1)}, u32[]{:S(2)}) copy-start(pred[128,128]{1,0:T(8,128)(4,1)} %iota_compare_fusion) | copy-start | bytes 49156
  793.0 18.2 %collective-permute-start.11 = (f32[2,16,64,128]{3,2,1,0:T(8,128)S(1)}, f32[2,16,64,128]{3,2,1,0:T(8,128)S(1)}, u32[]{:S(2)}, u32[]{:S(2)}) collective-permute-start(f32[2,16,64,128]{3,2,1,0:T(8,128)S(1)} %add_select_fusion.1), channel_id=1, source_target_pairs={{0,64},{4,68},{8,72},{12,76},{16,80},{20,84},{24,88},{28,92},{32,9... | collective-permute-start | bytes 3145736 | tf_op jit(solution)/shard_map/ppermute | solution.py:21
  794.4 17.1 %slice-start.2 = ((s8[6291456]{0:T(1024)(128)(4,1)}), s8[4194304]{0:T(1024)(128)(4,1)S(1)}, s32[]{:S(2)}) async-start(s8[6291456]{0:T(1024)(128)(4,1)} %bitcast.136), calls=%async_computation.4 | async-start | bytes 8388608
  794.8 16.7 %slice-start.3 = ((s8[6291456]{0:T(1024)(128)(4,1)}), s8[2097152]{0:T(1024)(128)(4,1)S(1)}, s32[]{:S(2)}) async-start(s8[6291456]{0:T(1024)(128)(4,1)} %bitcast.136), calls=%async_computation.5 | async-start | bytes 4194304
  794.8 16.7 %copy-start.7 = (f32[6,128,2,16]{1,3,2,0:T(8,128)S(1)}, f32[6,128,2,16]{1,3,2,0:T(8,128)}, u32[]{:S(2)}) copy-start(f32[6,128,2,16]{1,3,2,0:T(8,128)} %copy.55) | copy-start | bytes 294916
  794.8 16.7 %copy-start.19 = (f32[6,2,16]{2,1,0:T(2,128)S(1)}, f32[6,2,16]{2,1,0:T(2,128)}, u32[]{:S(2)}) copy-start(f32[6,2,16]{2,1,0:T(2,128)} %copy-done.18) | copy-start | bytes 2308
  794.8 16.7 %copy-start.23 = (f32[2,16]{1,0:T(2,128)S(1)}, f32[2,16]{1,0:T(2,128)}, u32[]{:S(2)}) copy-start(f32[2,16]{1,0:T(2,128)} %param.14) | copy-start | bytes 388
  (10 other events, 61.8 us)
Sparse Core Ops, SparseCore 0:
  9.0 52.6 all-gather.2
  63.3 509.1 all-gather.4

commit v2 on v1

--- a/solution.py
+++ b/solution.py
@@ -1,7 +1,7 @@
 import jax
 import jax.numpy as jnp
 from jax import lax
-from jax.sharding import PartitionSpec as P
+from jax.sharding import Mesh, PartitionSpec as P
 
 P_SIZE = 64
 N = 128
@@ -13,6 +13,7 @@
 
 
 epsilon = 1e-05
+SEQ = "seq"
 
 
 def shifted(block, axis, distance):
@@ -42,7 +43,11 @@
     groups = w_in.shape[0]
     row_count = gathered.shape[0]
     rows_first = jnp.transpose(w_in, (1, 0, 2))
-    full_w = lax.all_gather(rows_first, "seq", axis=0, tiled=True)
+    if isinstance(SEQ, tuple):
+        pair_w = lax.all_gather(rows_first, SEQ[2], axis=0, tiled=True)
+        full_w = lax.all_gather(pair_w, SEQ[:2], axis=0, tiled=True)
+    else:
+        full_w = lax.all_gather(rows_first, SEQ, axis=0, tiled=True)
     projected = jnp.einsum(
         "td,dgc->tgc",
         gathered,
@@ -51,7 +56,7 @@
     )
     conv_in = projected[:, :, :CW].astype(jnp.bfloat16)
     raw_dt = projected[:, :, CW:]
-    rim_rows = shifted(conv_in[row_count - (KCONV - 1) :], "seq", 1)
+    rim_rows = shifted(conv_in[row_count - (KCONV - 1) :], SEQ, 1)
     padded = jnp.concatenate([rim_rows, conv_in], axis=0)
     pre_act = jnp.broadcast_to(conv_b[None], (row_count, groups, CW))
     for offset in range(KCONV):
@@ -86,7 +91,7 @@
         keep_before.append(keep_now)
         state_now = keep_all[q][..., None, None] * state_now + fresh_all[q]
         keep_now = keep_now * keep_all[q]
-    incoming = entering(keep_now, state_now, "seq")
+    incoming = entering(keep_now, state_now, SEQ)
     states = jnp.stack(local_states) + jnp.stack(keep_before)[..., None, None] * incoming[None]
 
     scores = jnp.einsum("qign,qjgn->qgij", c_all, b_all, preferred_element_type=jnp.float32)
@@ -118,13 +123,33 @@
     return mix_groups(gathered, w_in, conv_w, conv_b, dt_bias, a_log, d_skip, norm_gain)
 
 
+def split_mesh(mesh):
+    global SEQ
+    devices = mesh.devices
+    try:
+        flat = devices.reshape(-1)
+        across_y = len({d.coords[1] for d in flat})
+        across_x = len({d.coords[0] for d in flat})
+    except (AttributeError, IndexError, TypeError):
+        SEQ = "seq"
+        return mesh
+    seq_size, chan_size = devices.shape
+    if seq_size % (across_y * across_x) or across_y * across_x == seq_size:
+        SEQ = "seq"
+        return mesh
+    pair = seq_size // (across_y * across_x)
+    SEQ = ("y", "x", "zl")
+    return Mesh(devices.reshape(across_y, across_x, pair, chan_size), SEQ + ("chan",))
+
+
 def solution(mesh):
+    mesh = split_mesh(mesh)
     return jax.shard_map(
         per_device,
         mesh=mesh,
         in_specs=(
-            P("seq", "chan"),
-            P("chan", "seq", None),
+            P(SEQ, "chan"),
+            P("chan", SEQ, None),
             P("chan", None, None),
             P("chan", None),
             P("chan", None),
@@ -132,6 +157,6 @@
             P("chan", None),
             P("chan", None),
         ),
-        out_specs=P("seq", "chan"),
+        out_specs=P(SEQ, "chan"),
         check_vma=False,
     )

time: 844 us -> 501 us (0.59); the launches traced: 832 us -> 500 us
  waiting for transfers between devices: 654 us -> 321 us
    all_gather x1 -> x2, waiting for transfers between devices: 511 us -> 173 us  [the longest x1 143 us: mix_groups(): full_w = lax.all_gather(pair_w, SEQ[:2], axis=0, tiled=True)]
  transfers between devices with their start and end apart: 14 -> 15, of which waited for: 11 -> 12; matrix products, arithmetic and copies ran while one was open for 5% -> 8% of each run, Pallas kernels for 0% -> 0%
where the time goes in v2:
time: 501 us; the launch traced here: 500 us
  waiting for transfers between devices  321 us (64%)
  starting transfers between devices  45.6 us (9%)
  local copies, waits for them, and re-layouts  42.9 us (9%)
  other arithmetic  39 us (8%)
  matrix products  38.1 us (8%)
  between operations  13.7 us (3%)
    all_gather x1, waiting for transfers between devices, mix_groups(): full_w = lax.all_gather(pair_w, SEQ[:2], axis=0, tiled=True)  143 us
    ppermute x12, waiting for transfers between devices, shifted(): return lax.ppermute(block, axis, route)  94.7 us
    all_gather x1, waiting for transfers between devices, per_device(): gathered = lax.all_gather(tokens, 'chan', axis=1, tiled=True)  51.5 us
    ppermute x12, starting transfers between devices, shifted(): return lax.ppermute(block, axis, route)  45.5 us
    all_gather x1, waiting for transfers between devices, mix_groups(): pair_w = lax.all_gather(rows_first, SEQ[2], axis=0, tiled=True)  30.1 us
    dot_general x1, matrix products, mix_groups(): jnp.einsum('td,dgc->tgc', gathered, full_w, preferred_element_type=jnp.fl...  22.7 us
    convert_element_type x1, other arithmetic, mix_groups(): inputs = jax.nn.silu(pre_act).astype(jnp.bfloat16)  14.3 us
  transfers between devices with their start and end apart: 15, of which 12 were waited for; matrix products, arithmetic and copies ran while one was open for 8% of the time, Pallas kernels for 0%

profile of v2, /device:TPU:22, one launch (start us, length us, event | category | flops | bytes accessed | tf_op | source)
XLA Modules:
  0.0 500.2 jit_solution(6230936630012961003)
XLA Ops:
  8.1 30.1 %all-gather.6.cloned.1.call-done = bf16[256,2,1296]{0,2,1:T(8,128)(2,1)} async-done(((bf16[128,2,1296]{0,2,1:T(8,128)(2,1)}), bf16[256,2,1296]{0,2,1:T(8,128)(2,1)}) %all-gather.6.cloned.1.call-update) | async-done | bytes 1327120 | tf_op jit(solution)/shard_map/all_gather | solution.py:47
  39.9 51.5 %all-gather.4.cloned.1.call-done = bf16[768,4096]{1,0:T(8,128)(2,1)} async-done(((bf16[768,1024]{1,0:T(8,128)(2,1)}), bf16[768,4096]{1,0:T(8,128)(2,1)}) %all-gather.4.cloned.1.call-update) | async-done | bytes 6291472 | tf_op jit(solution)/shard_map/all_gather | solution.py:122
  91.4 143.1 %all-gather.8.cloned.1.call-done = bf16[4096,2,1296]{0,2,1:T(8,128)(2,1)} async-done(((bf16[256,2,1296]{0,2,1:T(8,128)(2,1)}), bf16[4096,2,1296]{0,2,1:T(8,128)(2,1)}) %all-gather.8.cloned.1.call-update) | async-done | bytes 21233680 | tf_op jit(solution)/shard_map/all_gather | solution.py:48
  234.5 22.7 %fusion.45 = (bf16[768,2,1296]{0,2,1:T(8,128)(2,1)}, f32[768,2,1296]{0,2,1:T(8,128)S(1)}) fusion(bf16[4096,2,1296]{0,2,1:T(8,128)(2,1)} %all-gather.8.cloned.1.call-done, bf16[768,4096]{1,0:T(8,128)(2,1)} %all-gather.4.cloned.1.call-done), kind=kOutput, calls=%fused_computation.110 | convolution fusion | flops 16309444608 | bytes 39469056 | tf_op jit(solution)/shard_map/td,dgc->tgc/dot_general | solution.py:51
  260.7 3.6 collective-permute-start
  266.7 4.3 slice.113
  272.3 14.3 %multiply_convert_fusion.1 = bf16[768,2,1280]{0,2,1:T(8,128)(2,1)} fusion(bf16[768,2,1280]{0,2,1:T(8,128)(2,1)} %slice.113, bf16[3,2,1280]{0,2,1:T(8,128)(2,1)S(1)} %copy.46, f32[2,1280]{1,0:T(2,128)S(1)} %get-tuple-element.31, f32[2,1280]{1,0:T(2,128)S(1)} %get-tuple-element.32, f32[2,1280]{1,0:T(2,128)S(1)} %get-tuple-element.33, ...), kind=kLoop, calls=%fused_computation.3 | loop fusion | flops 51118080 | bytes 7930880 | tf_op jit(solution)/shard_map/convert_element_type | solution.py:64
  286.7 6.3 %copy.47 = bf16[768,2,1280]{2,0,1:T(8,128)(2,1)} copy(bf16[768,2,1280]{0,2,1:T(8,128)(2,1)} %multiply_convert_fusion.1) | data formatting | bytes 7864320 | tf_op jit(solution)/shard_map/convert_element_type | solution.py:64
  293.0 3.9 slice.118
  298.8 3.5 copy.48
  302.3 2.0 fusion.17
  304.3 2.6 copy-done
  307.5 4.4 collective-permute-start.6
  311.9 22.2 %collective-permute-done.6 = f32[2,16,64,128]{3,2,1,0:T(8,128)} collective-permute-done((f32[2,16,64,128]{3,2,1,0:T(8,128)S(1)}, f32[2,16,64,128]{3,2,1,0:T(8,128)}, u32[]{:S(2)}, u32[]{:S(2)}) %collective-permute-start.6) | collective-permute-done | bytes 1048608 | tf_op jit(solution)/shard_map/ppermute | solution.py:22
  334.1 3.6 collective-permute-start.7
  337.7 6.4 %collective-permute-start.1 = (f32[2,16]{1,0:T(2,128)}, f32[2,16]{1,0:T(2,128)S(1)}, u32[]{:S(2)}, u32[]{:S(2)}) collective-permute-start(f32[2,16]{1,0:T(2,128)} %get-tuple-element.25), channel_id=1, source_target_pairs={{0,4},{4,8},{8,12},{12,16},{16,20},{20,24},{24,28},{28,32},{32,36}... | collective-permute-start | bytes 392 | tf_op jit(solution)/shard_map/ppermute | solution.py:22
  344.1 15.8 %collective-permute-done.1 = f32[2,16]{1,0:T(2,128)S(1)} collective-permute-done((f32[2,16]{1,0:T(2,128)}, f32[2,16]{1,0:T(2,128)S(1)}, u32[]{:S(2)}, u32[]{:S(2)}) %collective-permute-start.1) | collective-permute-done | bytes 160 | tf_op jit(solution)/shard_map/ppermute | solution.py:22
  362.0 8.8 %collective-permute-start.8 = (f32[2,16,64,128]{3,2,1,0:T(8,128)S(1)}, f32[2,16,64,128]{3,2,1,0:T(8,128)}, u32[]{:S(2)}, u32[]{:S(2)}) collective-permute-start(f32[2,16,64,128]{3,2,1,0:T(8,128)S(1)} %add_select_fusion.4), channel_id=1, source_target_pairs={{0,8},{4,12},{8,16},{12,20},{16,24},{20,28},{24,32},{28,36},{32,40... | collective-permute-start | bytes 3145736 | tf_op jit(solution)/shard_map/ppermute | solution.py:22
  374.5 13.6 %collective-permute-done.2 = f32[2,16]{1,0:T(2,128)S(1)} collective-permute-done((f32[2,16]{1,0:T(2,128)}, f32[2,16]{1,0:T(2,128)S(1)}, u32[]{:S(2)}, u32[]{:S(2)}) %collective-permute-start.2) | collective-permute-done | bytes 160 | tf_op jit(solution)/shard_map/ppermute | solution.py:22
  391.9 4.2 collective-permute-start.9
  396.7 4.5 collective-permute-start.3
  403.1 15.3 %collective-permute-done.3 = f32[2,16]{1,0:T(2,128)} collective-permute-done((f32[2,16]{1,0:T(2,128)}, f32[2,16]{1,0:T(2,128)}, u32[]{:S(2)}, u32[]{:S(2)}) %collective-permute-start.3) | collective-permute-done | bytes 160 | tf_op jit(solution)/shard_map/ppermute | solution.py:22
  419.1 3.0 collective-permute-start.4
  423.6 2.4 collective-permute-done.4
  433.0 2.6 fusion.28
  439.0 2.7 constant_dynamic-update-slice_fusion.1
  445.5 12.5 %collective-permute-done.10 = f32[2,16,64,128]{3,2,1,0:T(8,128)S(1)} collective-permute-done((f32[2,16,64,128]{3,2,1,0:T(8,128)S(1)}, f32[2,16,64,128]{3,2,1,0:T(8,128)S(1)}, u32[]{:S(2)}, u32[]{:S(2)}) %collective-permute-start.10) | collective-permute-done | bytes 1048608 | tf_op jit(solution)/shard_map/ppermute | solution.py:22
  460.6 8.7 %fusion = f32[6,2,16,64,128]{4,3,2,1,0:T(8,128)} fusion(bf16[6,128,2,16,64]{1,4,3,2,0:T(8,128)(2,1)S(1)} %bitcast.132, f32[6,2,16,128]{3,2,1,0:T(8,128)S(1)} %copy-done.9, f32[6,2,16,128]{3,2,1,0:T(8,128)S(1)} %copy-done.8, f32[6,2,128,128]{3,2,1,0:T(8,128)S(1)} %fusion.32, pred[128,128]{1,0:T(8,128)(4,1)S(1)} %copy-done.10), kind=kOutput, calls=%fused_computation.4 | convolution fusion | flops 421527552 | bytes 10436608 | tf_op jit(solution)/shard_map/qghij,qjghp->qighp/dot_general | solution.py:103
  469.4 10.1 %collective-permute-done.11 = f32[2,16,64,128]{3,2,1,0:T(8,128)S(1)} collective-permute-done((f32[2,16,64,128]{3,2,1,0:T(8,128)S(1)}, f32[2,16,64,128]{3,2,1,0:T(8,128)S(1)}, u32[]{:S(2)}, u32[]{:S(2)}) %collective-permute-start.11) | collective-permute-done | bytes 1048608 | tf_op jit(solution)/shard_map/ppermute | solution.py:22
  479.7 4.4 multiply_reduce_fusion
  484.1 5.6 %copy.58 = f32[6,128,2,16,64]{1,0,4,3,2:T(8,128)S(1)} copy(f32[6,128,2,16,64]{1,4,3,2,0:T(8,128)S(1)} %get-tuple-element.30) | data formatting | bytes 12582912 | tf_op jit(solution)/shard_map/add | solution.py:114
  490.8 2.9 copy.59
  (120 shorter events, 44.9 us)
Async XLA Ops:
  6.5 31.6 %all-gather.6.cloned.1.call-start = ((), (), s32[]{:S(2)}) async-start(), calls=%async_computation.1 | async-start | bytes 1990656 | tf_op jit(solution)/shard_map/all_gather | solution.py:47
  7.3 84.2 %all-gather.4.cloned.1.call-start = ((), (), s32[]{:S(2)}) async-start(), calls=%async_computation | async-start | bytes 7864320 | tf_op jit(solution)/shard_map/all_gather | solution.py:122
  8.0 226.5 %all-gather.8.cloned.1.call-start = ((), (), s32[]{:S(2)}) async-start(), calls=%async_computation.2 | async-start | bytes 22560768 | tf_op jit(solution)/shard_map/all_gather | solution.py:48
  39.9 217.3 %copy-start.22 = (f32[2,16]{1,0:T(2,128)S(1)}, f32[2,16]{1,0:T(2,128)}, u32[]{:S(2)}) copy-start(f32[2,16]{1,0:T(2,128)} %param.12) | copy-start | bytes 388
  260.7 11.2 %collective-permute-start = (bf16[3,2,1280]{2,1,0:T(2,128)(2,1)S(1)}, bf16[3,2,1280]{2,1,0:T(2,128)(2,1)S(1)}, u32[]{:S(2)}, u32[]{:S(2)}) collective-permute-start(bf16[3,2,1280]{2,1,0:T(2,128)(2,1)S(1)} %copy.45), channel_id=1, source_target_pairs={{0,4},{4,8},{8,12},{12,16},{16,20},{20,24},{24,28},{28,32},{32,36}... | collective-permute-start | bytes 46088 | tf_op jit(solution)/shard_map/ppermute | solution.py:22
  266.7 20.0 %copy-start.18 = (f32[6,2,16]{2,1,0:T(2,128)}, f32[6,2,16]{2,1,0:T(2,128)S(1)}, u32[]{:S(2)}) copy-start(f32[6,2,16]{2,1,0:T(2,128)S(1)} %get-tuple-element.19) | copy-start | bytes 2308
  266.7 37.6 %copy-start.13 = (f32[2,16]{1,0:T(2,128)}, f32[2,16]{1,0:T(2,128)S(1)}, u32[]{:S(2)}) copy-start(f32[2,16]{1,0:T(2,128)S(1)} %get-tuple-element.21) | copy-start | bytes 388
  266.7 37.6 %copy-start.15 = (f32[2,16]{1,0:T(2,128)}, f32[2,16]{1,0:T(2,128)S(1)}, u32[]{:S(2)}) copy-start(f32[2,16]{1,0:T(2,128)S(1)} %get-tuple-element.22) | copy-start | bytes 388
  307.5 26.6 %collective-permute-start.6 = (f32[2,16,64,128]{3,2,1,0:T(8,128)S(1)}, f32[2,16,64,128]{3,2,1,0:T(8,128)}, u32[]{:S(2)}, u32[]{:S(2)}) collective-permute-start(f32[2,16,64,128]{3,2,1,0:T(8,128)S(1)} %fusion.22), channel_id=1, source_target_pairs={{0,4},{4,8},{8,12},{12,16},{16,20},{20,24},{24,28},{28,32},{32,36}... | collective-permute-start | bytes 3145736 | tf_op jit(solution)/shard_map/ppermute | solution.py:22
  334.1 26.5 %collective-permute-start.7 = (f32[2,16,64,128]{3,2,1,0:T(8,128)}, f32[2,16,64,128]{3,2,1,0:T(8,128)S(1)}, u32[]{:S(2)}, u32[]{:S(2)}) collective-permute-start(f32[2,16,64,128]{3,2,1,0:T(8,128)} %collective-permute-done.6), channel_id=1, source_target_pairs={{0,4},{4,8},{8,12},{12,16},{16,20},{20,24},{24,28},{28,32},{32,36}... | collective-permute-start | bytes 3145736 | tf_op jit(solution)/shard_map/ppermute | solution.py:22
  337.7 22.3 %collective-permute-start.1 = (f32[2,16]{1,0:T(2,128)}, f32[2,16]{1,0:T(2,128)S(1)}, u32[]{:S(2)}, u32[]{:S(2)}) collective-permute-start(f32[2,16]{1,0:T(2,128)} %get-tuple-element.25), channel_id=1, source_target_pairs={{0,4},{4,8},{8,12},{12,16},{16,20},{20,24},{24,28},{28,32},{32,36}... | collective-permute-start | bytes 392 | tf_op jit(solution)/shard_map/ppermute | solution.py:22
  360.0 13.8 %copy-start.20 = (f32[2,16]{1,0:T(2,128)}, f32[2,16]{1,0:T(2,128)S(1)}, u32[]{:S(2)}) copy-start(f32[2,16]{1,0:T(2,128)S(1)} %collective-permute-done.1) | copy-start | bytes 388
  362.0 27.4 %copy-start.4 = (f32[2,16,64,128]{3,2,1,0:T(8,128)}, f32[2,16,64,128]{3,2,1,0:T(8,128)S(1)}, u32[]{:S(2)}) copy-start(f32[2,16,64,128]{3,2,1,0:T(8,128)S(1)} %add_select_fusion.4) | copy-start | bytes 3145732
  362.0 28.2 %collective-permute-start.8 = (f32[2,16,64,128]{3,2,1,0:T(8,128)S(1)}, f32[2,16,64,128]{3,2,1,0:T(8,128)}, u32[]{:S(2)}, u32[]{:S(2)}) collective-permute-start(f32[2,16,64,128]{3,2,1,0:T(8,128)S(1)} %add_select_fusion.4), channel_id=1, source_target_pairs={{0,8},{4,12},{8,16},{12,20},{16,24},{20,28},{24,32},{28,36},{32,40... | collective-permute-start | bytes 3145736 | tf_op jit(solution)/shard_map/ppermute | solution.py:22
  370.8 70.9 %slice-start = ((s8[6291456]{0:T(1024)(128)(4,1)}), s8[2097152]{0:T(1024)(128)(4,1)S(1)}, s32[]{:S(2)}) async-start(s8[6291456]{0:T(1024)(128)(4,1)} %bitcast.128), calls=%async_computation.3 | async-start | bytes 4194304
  371.9 16.3 %collective-permute-start.2 = (f32[2,16]{1,0:T(2,128)}, f32[2,16]{1,0:T(2,128)S(1)}, u32[]{:S(2)}, u32[]{:S(2)}) collective-permute-start(f32[2,16]{1,0:T(2,128)} %broadcast_select_fusion), channel_id=1, source_target_pairs={{0,4},{4,8},{8,12},{12,16},{16,20},{20,24},{24,28},{28,32},{32,36}... | collective-permute-start | bytes 392 | tf_op jit(solution)/shard_map/ppermute | solution.py:22
  391.9 43.7 %collective-permute-start.9 = (f32[2,16,64,128]{3,2,1,0:T(8,128)S(1)}, f32[2,16,64,128]{3,2,1,0:T(8,128)}, u32[]{:S(2)}, u32[]{:S(2)}) collective-permute-start(f32[2,16,64,128]{3,2,1,0:T(8,128)S(1)} %add_select_fusion.3), channel_id=1, source_target_pairs={{0,16},{4,20},{8,24},{12,28},{16,32},{20,36},{24,40},{28,44},{32,4... | collective-permute-start | bytes 3145736 | tf_op jit(solution)/shard_map/ppermute | solution.py:22
  396.7 21.6 %collective-permute-start.3 = (f32[2,16]{1,0:T(2,128)}, f32[2,16]{1,0:T(2,128)}, u32[]{:S(2)}, u32[]{:S(2)}) collective-permute-start(f32[2,16]{1,0:T(2,128)} %multiply_select_fusion.3), channel_id=1, source_target_pairs={{0,8},{4,12},{8,16},{12,20},{16,24},{20,28},{24,32},{28,36},{32,40... | collective-permute-start | bytes 392 | tf_op jit(solution)/shard_map/ppermute | solution.py:22
  419.1 7.0 %collective-permute-start.4 = (f32[2,16]{1,0:T(2,128)S(1)}, f32[2,16]{1,0:T(2,128)S(1)}, u32[]{:S(2)}, u32[]{:S(2)}) collective-permute-start(f32[2,16]{1,0:T(2,128)S(1)} %multiply_select_fusion.2), channel_id=1, source_target_pairs={{0,16},{4,20},{8,24},{12,28},{16,32},{20,36},{24,40},{28,44},{32,4... | collective-permute-start | bytes 392 | tf_op jit(solution)/shard_map/ppermute | solution.py:22
  426.6 5.8 %collective-permute-start.5 = (f32[2,16]{1,0:T(2,128)}, f32[2,16]{1,0:T(2,128)}, u32[]{:S(2)}, u32[]{:S(2)}) collective-permute-start(f32[2,16]{1,0:T(2,128)} %multiply_select_fusion.1), channel_id=1, source_target_pairs={{0,32},{4,36},{8,40},{12,44},{16,48},{20,52},{24,56},{28,60},{32,6... | collective-permute-start | bytes 392 | tf_op jit(solution)/shard_map/ppermute | solution.py:22
  437.0 21.0 %collective-permute-start.10 = (f32[2,16,64,128]{3,2,1,0:T(8,128)S(1)}, f32[2,16,64,128]{3,2,1,0:T(8,128)S(1)}, u32[]{:S(2)}, u32[]{:S(2)}) collective-permute-start(f32[2,16,64,128]{3,2,1,0:T(8,128)S(1)} %add_select_fusion.2), channel_id=1, source_target_pairs={{0,32},{4,36},{8,40},{12,44},{16,48},{20,52},{24,56},{28,60},{32,6... | collective-permute-start | bytes 3145736 | tf_op jit(solution)/shard_map/ppermute | solution.py:22
  442.9 17.2 %copy-start.5 = (bf16[6,128,2,128]{3,1,0,2:T(8,128)(2,1)S(1)}, bf16[6,128,2,128]{3,1,0,2:T(8,128)(2,1)}, u32[]{:S(2)}) copy-start(bf16[6,128,2,128]{3,1,0,2:T(8,128)(2,1)} %get-tuple-element.11) | copy-start | bytes 1179652
  442.9 17.7 %copy-start.2 = (bf16[6,128,2,1024]{1,3,2,0:T(8,128)(2,1)S(1)}, bf16[6,128,2,1024]{1,3,2,0:T(8,128)(2,1)}, u32[]{:S(2)}) copy-start(bf16[6,128,2,1024]{1,3,2,0:T(8,128)(2,1)} %copy-done.1) | copy-start | bytes 9437188
  442.9 17.7 %copy-start.8 = (f32[6,2,16,128]{3,2,1,0:T(8,128)S(1)}, f32[6,2,16,128]{3,2,1,0:T(8,128)}, u32[]{:S(2)}) copy-start(f32[6,2,16,128]{3,2,1,0:T(8,128)} %copy.52) | copy-start | bytes 294916
  442.9 17.7 %copy-start.9 = (f32[6,2,16,128]{3,2,1,0:T(8,128)S(1)}, f32[6,2,16,128]{3,2,1,0:T(8,128)}, u32[]{:S(2)}) copy-start(f32[6,2,16,128]{3,2,1,0:T(8,128)} %copy.54) | copy-start | bytes 294916
  442.9 17.7 %copy-start.10 = (pred[128,128]{1,0:T(8,128)(4,1)S(1)}, pred[128,128]{1,0:T(8,128)(4,1)}, u32[]{:S(2)}) copy-start(pred[128,128]{1,0:T(8,128)(4,1)} %iota_compare_fusion) | copy-start | bytes 49156
  458.9 20.6 %collective-permute-start.11 = (f32[2,16,64,128]{3,2,1,0:T(8,128)S(1)}, f32[2,16,64,128]{3,2,1,0:T(8,128)S(1)}, u32[]{:S(2)}, u32[]{:S(2)}) collective-permute-start(f32[2,16,64,128]{3,2,1,0:T(8,128)S(1)} %add_select_fusion.1), channel_id=1, source_target_pairs={{0,64},{4,68},{8,72},{12,76},{16,80},{20,84},{24,88},{28,92},{32,9... | collective-permute-start | bytes 3145736 | tf_op jit(solution)/shard_map/ppermute | solution.py:22
  460.2 19.5 %slice-start.2 = ((s8[6291456]{0:T(1024)(128)(4,1)}), s8[4194304]{0:T(1024)(128)(4,1)S(1)}, s32[]{:S(2)}) async-start(s8[6291456]{0:T(1024)(128)(4,1)} %bitcast.136), calls=%async_computation.5 | async-start | bytes 8388608
  460.6 19.1 %slice-start.3 = ((s8[6291456]{0:T(1024)(128)(4,1)}), s8[2097152]{0:T(1024)(128)(4,1)S(1)}, s32[]{:S(2)}) async-start(s8[6291456]{0:T(1024)(128)(4,1)} %bitcast.136), calls=%async_computation.6 | async-start | bytes 4194304
  460.6 19.1 %copy-start.7 = (f32[6,128,2,16]{1,3,2,0:T(8,128)S(1)}, f32[6,128,2,16]{1,3,2,0:T(8,128)}, u32[]{:S(2)}) copy-start(f32[6,128,2,16]{1,3,2,0:T(8,128)} %copy.55) | copy-start | bytes 294916
  460.6 19.1 %copy-start.19 = (f32[6,2,16]{2,1,0:T(2,128)S(1)}, f32[6,2,16]{2,1,0:T(2,128)}, u32[]{:S(2)}) copy-start(f32[6,2,16]{2,1,0:T(2,128)} %copy-done.18) | copy-start | bytes 2308
  460.6 19.1 %copy-start.23 = (f32[2,16]{1,0:T(2,128)S(1)}, f32[2,16]{1,0:T(2,128)}, u32[]{:S(2)}) copy-start(f32[2,16]{1,0:T(2,128)} %param.14) | copy-start | bytes 388
  (11 other events, 76.1 us)
Sparse Core Ops, SparseCore 0:
  9.0 29.1 all-gather.5
  39.8 51.5 all-gather.3
  93.5 140.9 all-gather.7

commit v3 on v2

--- a/solution.py
+++ b/solution.py
@@ -22,21 +22,51 @@
     return lax.ppermute(block, axis, route)
 
 
-def entering(keep, end, axis):
+def combine(earlier, later):
+    return (earlier[0] * later[0], later[0][..., None, None] * earlier[1] + later[1])
+
+
+def gather_level(own, axis, need_total):
+    size = lax.axis_size(axis)
     place = lax.axis_index(axis)
-    size = lax.axis_size(axis)
-    keep = jnp.where(place == 0, 1.0, shifted(keep, axis, 1))
-    end = shifted(end, axis, 1)
-    distance = 1
-    while distance < size:
-        earlier_end = shifted(end, axis, distance)
-        reach = place >= distance
-        end = jnp.where(reach, keep[..., None, None] * earlier_end + end, end)
-        if distance * 2 < size:
-            earlier_keep = shifted(keep, axis, distance)
-            keep = jnp.where(reach, keep * earlier_keep, keep)
-        distance *= 2
-    return end
+    groups, heads = own[0].shape
+    tail = own[1].shape[-1]
+    packed = jnp.concatenate(
+        [own[1], jnp.broadcast_to(own[0][..., None, None], (groups, heads, 8, tail))], axis=2
+    )
+    received = [None]
+    for distance in range(1, size):
+        if need_total:
+            route = [(i, (i + distance) % size) for i in range(size)]
+        else:
+            route = [(i, i + distance) for i in range(size - distance)]
+        got = lax.ppermute(packed, axis, route)
+        received.append((got[:, :, -8, 0], got[:, :, :-8]))
+    prefix = (jnp.ones_like(own[0]), jnp.zeros_like(own[1]))
+    for distance in range(size - 1, 0, -1):
+        joined = combine(prefix, received[distance])
+        reach = distance <= place
+        prefix = (jnp.where(reach, joined[0], prefix[0]), jnp.where(reach, joined[1], prefix[1]))
+    if not need_total:
+        return prefix, None
+    total = combine(prefix, own)
+    for distance in range(size - 1, 0, -1):
+        joined = combine(total, received[distance])
+        beyond = distance > place
+        total = (jnp.where(beyond, joined[0], total[0]), jnp.where(beyond, joined[1], total[1]))
+    return prefix, total
+
+
+def entering(keep, end, axes):
+    carried = (keep, end)
+    prefixes = []
+    for level, axis in enumerate(reversed(axes)):
+        prefix, carried = gather_level(carried, axis, level < len(axes) - 1)
+        prefixes.append(prefix)
+    result = prefixes[-1]
+    for prefix in reversed(prefixes[:-1]):
+        result = combine(result, prefix)
+    return result[1]
 
 
 def mix_groups(gathered, w_in, conv_w, conv_b, dt_bias, a_log, d_skip, norm_gain):
@@ -91,7 +121,7 @@
         keep_before.append(keep_now)
         state_now = keep_all[q][..., None, None] * state_now + fresh_all[q]
         keep_now = keep_now * keep_all[q]
-    incoming = entering(keep_now, state_now, SEQ)
+    incoming = entering(keep_now, state_now, SEQ if isinstance(SEQ, tuple) else (SEQ,))
     states = jnp.stack(local_states) + jnp.stack(keep_before)[..., None, None] * incoming[None]
 
     scores = jnp.einsum("qign,qjgn->qgij", c_all, b_all, preferred_element_type=jnp.float32)

time: 501 us -> 477 us (0.952)
  starting transfers between devices: 45.6 us -> 13.8 us
  waiting for transfers between devices: 321 us -> 336 us
  other arithmetic: 39 us -> 30.4 us
    ppermute x0 -> x7, waiting for transfers between devices: none -> 109 us  [gather_level(): got = lax.ppermute(packed, axis, route)]
    ppermute x12 -> x1, waiting for transfers between devices: 94.7 us -> 0.01 us  [shifted(): return lax.ppermute(block, axis, route)]
    ppermute x12 -> x1, starting transfers between devices: 45.5 us -> 3.6 us  [shifted(): return lax.ppermute(block, axis, route)]
    ppermute x0 -> x7, starting transfers between devices: none -> 10.1 us  [gather_level(): got = lax.ppermute(packed, axis, route)]
    unnamed x9 -> x8, other arithmetic: 7.8 us -> 0.89 us
  transfers between devices with their start and end apart: 15 -> 11, of which waited for: 12 -> 8; matrix products, arithmetic and copies ran while one was open for 8% -> 5% of each run, Pallas kernels for 0% -> 0%
where the time goes in v3:
time: 477 us; the launch traced here: 473 us
  waiting for transfers between devices  336 us (70%)
  local copies, waits for them, and re-layouts  41.3 us (9%)
  matrix products  38.2 us (8%)
  other arithmetic  30.4 us (6%)
  starting transfers between devices  13.8 us (3%)
  between operations  13.7 us (3%)
    all_gather x1, waiting for transfers between devices, mix_groups(): full_w = lax.all_gather(pair_w, SEQ[:2], axis=0, tiled=True)  143 us
    ppermute x7, waiting for transfers between devices, gather_level(): got = lax.ppermute(packed, axis, route)  109 us
    all_gather x1, waiting for transfers between devices, per_device(): gathered = lax.all_gather(tokens, 'chan', axis=1, tiled=True)  51.5 us
    all_gather x1, waiting for transfers between devices, mix_groups(): pair_w = lax.all_gather(rows_first, SEQ[2], axis=0, tiled=True)  30.1 us
    dot_general x1, matrix products, mix_groups(): jnp.einsum('td,dgc->tgc', gathered, full_w, preferred_element_type=jnp.fl...  22.7 us
    convert_element_type x1, other arithmetic, mix_groups(): inputs = jax.nn.silu(pre_act).astype(jnp.bfloat16)  14.3 us
    ppermute x7, starting transfers between devices, gather_level(): got = lax.ppermute(packed, axis, route)  10.1 us
  transfers between devices with their start and end apart: 11, of which 8 were waited for; matrix products, arithmetic and copies ran while one was open for 5% of the time, Pallas kernels for 0%

profile of v3, /device:TPU:22, one launch (start us, length us, event | category | flops | bytes accessed | tf_op | source)
XLA Modules:
  0.0 472.9 jit_solution(5744511126239999406)
XLA Ops:
  8.1 30.1 %all-gather.6.cloned.1.call-done = bf16[256,2,1296]{0,2,1:T(8,128)(2,1)} async-done(((bf16[128,2,1296]{0,2,1:T(8,128)(2,1)}), bf16[256,2,1296]{0,2,1:T(8,128)(2,1)}) %all-gather.6.cloned.1.call-update) | async-done | bytes 1327120 | tf_op jit(solution)/shard_map/all_gather | solution.py:77
  39.9 51.5 %all-gather.4.cloned.1.call-done = bf16[768,4096]{1,0:T(8,128)(2,1)} async-done(((bf16[768,1024]{1,0:T(8,128)(2,1)}), bf16[768,4096]{1,0:T(8,128)(2,1)}) %all-gather.4.cloned.1.call-update) | async-done | bytes 6291472 | tf_op jit(solution)/shard_map/all_gather | solution.py:152
  91.4 143.1 %all-gather.8.cloned.1.call-done = bf16[4096,2,1296]{0,2,1:T(8,128)(2,1)} async-done(((bf16[256,2,1296]{0,2,1:T(8,128)(2,1)}), bf16[4096,2,1296]{0,2,1:T(8,128)(2,1)}) %all-gather.8.cloned.1.call-update) | async-done | bytes 21233680 | tf_op jit(solution)/shard_map/all_gather | solution.py:78
  234.5 22.7 %fusion.56 = (bf16[768,2,1296]{0,2,1:T(8,128)(2,1)}, f32[768,2,1296]{0,2,1:T(8,128)S(1)}) fusion(bf16[4096,2,1296]{0,2,1:T(8,128)(2,1)} %all-gather.8.cloned.1.call-done, bf16[768,4096]{1,0:T(8,128)(2,1)} %all-gather.4.cloned.1.call-done), kind=kOutput, calls=%fused_computation.140 | convolution fusion | flops 16309444608 | bytes 39469056 | tf_op jit(solution)/shard_map/td,dgc->tgc/dot_general | solution.py:81
  259.2 1.4 slice.168
  260.8 3.6 collective-permute-start
  264.4 1.7 exponential_multiply_fusion
  266.7 4.2 slice.169
  272.4 14.3 %multiply_convert_fusion.1 = bf16[768,2,1280]{0,2,1:T(8,128)(2,1)} fusion(bf16[768,2,1280]{0,2,1:T(8,128)(2,1)} %slice.169, bf16[3,2,1280]{0,2,1:T(8,128)(2,1)S(1)} %copy.49, f32[2,1280]{1,0:T(2,128)S(1)} %get-tuple-element.43, f32[2,1280]{1,0:T(2,128)S(1)} %get-tuple-element.44, f32[2,1280]{1,0:T(2,128)S(1)} %get-tuple-element.45, ...), kind=kLoop, calls=%fused_computation.3 | loop fusion | flops 51118080 | bytes 7930880 | tf_op jit(solution)/shard_map/convert_element_type | solution.py:94
  286.7 6.4 %copy.50 = bf16[768,2,1280]{2,0,1:T(8,128)(2,1)} copy(bf16[768,2,1280]{0,2,1:T(8,128)(2,1)} %multiply_convert_fusion.1) | data formatting | bytes 7864320 | tf_op jit(solution)/shard_map/convert_element_type | solution.py:94
  293.1 3.9 slice.174
  296.9 2.0 fusion.54
  298.9 3.6 copy.51
  302.6 2.0 fusion.17
  304.6 2.6 copy-done
  309.0 2.5 collective-permute-start.1
  313.4 1.4 copy.55
  315.4 1.2 copy.58
  316.7 19.9 %collective-permute-done.1 = f32[2,16,72,128]{3,2,1,0:T(8,128)S(1)} collective-permute-done((f32[2,16,72,128]{3,2,1,0:T(8,128)}, f32[2,16,72,128]{3,2,1,0:T(8,128)S(1)}, u32[]{:S(2)}, u32[]{:S(2)}) %collective-permute-start.1) | collective-permute-done | bytes 1179680 | tf_op jit(solution)/shard_map/ppermute | solution.py:43
  336.9 3.4 add_select_fusion.2
  340.6 1.5 collective-permute-start.3
  342.1 1.7 collective-permute-start.4
  344.8 48.2 %collective-permute-done.2 = f32[2,16,72,128]{3,2,1,0:T(8,128)S(1)} collective-permute-done((f32[2,16,72,128]{3,2,1,0:T(8,128)S(1)}, f32[2,16,72,128]{3,2,1,0:T(8,128)S(1)}, u32[]{:S(2)}, u32[]{:S(2)}) %collective-permute-start.2) | collective-permute-done | bytes 1179680 | tf_op jit(solution)/shard_map/ppermute | solution.py:43
  395.0 1.3 collective-permute-start.6
  397.3 2.2 collective-permute-start.5
  399.9 8.8 %fusion = f32[6,2,16,64,128]{4,3,2,1,0:T(8,128)} fusion(bf16[6,128,2,16,64]{1,4,3,2,0:T(8,128)(2,1)S(1)} %bitcast.146, f32[6,2,16,128]{3,2,1,0:T(8,128)S(1)} %copy-done.13, f32[6,2,16,128]{3,2,1,0:T(8,128)S(1)} %copy.55, f32[6,2,128,128]{3,2,1,0:T(8,128)S(1)} %fusion.39, pred[128,128]{1,0:T(8,128)(4,1)S(1)} %copy-done.14), kind=kOutput, calls=%fused_computation.4 | convolution fusion | flops 421527552 | bytes 10436608 | tf_op jit(solution)/shard_map/qghij,qjghp->qighp/dot_general | solution.py:133
  408.8 18.6 %collective-permute-done.6 = f32[2,16,72,128]{3,2,1,0:T(8,128)S(1)} collective-permute-done((f32[2,16,72,128]{3,2,1,0:T(8,128)S(1)}, f32[2,16,72,128]{3,2,1,0:T(8,128)S(1)}, u32[]{:S(2)}, u32[]{:S(2)}) %collective-permute-start.6) | collective-permute-done | bytes 1179680 | tf_op jit(solution)/shard_map/ppermute | solution.py:43
  427.8 22.1 %collective-permute-done.5 = f32[2,16,72,128]{3,2,1,0:T(8,128)S(1)} collective-permute-done((f32[2,16,72,128]{3,2,1,0:T(8,128)S(1)}, f32[2,16,72,128]{3,2,1,0:T(8,128)S(1)}, u32[]{:S(2)}, u32[]{:S(2)}) %collective-permute-start.5) | collective-permute-done | bytes 1179680 | tf_op jit(solution)/shard_map/ppermute | solution.py:43
  450.1 2.3 fusion.26
  452.4 4.3 multiply_reduce_fusion
  456.7 5.6 %copy.62 = f32[6,128,2,16,64]{1,0,4,3,2:T(8,128)S(1)} copy(f32[6,128,2,16,64]{1,4,3,2,0:T(8,128)S(1)} %get-tuple-element.42) | data formatting | bytes 12582912 | tf_op jit(solution)/shard_map/add | solution.py:144
  463.5 2.9 copy.63
  (118 shorter events, 18.1 us)
Async XLA Ops:
  6.5 31.6 %all-gather.6.cloned.1.call-start = ((), (), s32[]{:S(2)}) async-start(), calls=%async_computation.1 | async-start | bytes 1990656 | tf_op jit(solution)/shard_map/all_gather | solution.py:77
  7.3 84.2 %all-gather.4.cloned.1.call-start = ((), (), s32[]{:S(2)}) async-start(), calls=%async_computation | async-start | bytes 7864320 | tf_op jit(solution)/shard_map/all_gather | solution.py:152
  8.0 226.5 %all-gather.8.cloned.1.call-start = ((), (), s32[]{:S(2)}) async-start(), calls=%async_computation.2 | async-start | bytes 22560768 | tf_op jit(solution)/shard_map/all_gather | solution.py:78
  39.9 217.3 %copy-start.24 = (f32[2,16]{1,0:T(2,128)S(1)}, f32[2,16]{1,0:T(2,128)}, u32[]{:S(2)}) copy-start(f32[2,16]{1,0:T(2,128)} %param.12) | copy-start | bytes 388
  258.1 12.8 %copy-start.6 = (f32[6,128,2,16]{3,2,1,0:T(2,128)}, f32[6,128,2,16]{3,2,1,0:T(2,128)S(1)}, u32[]{:S(2)}) copy-start(f32[6,128,2,16]{3,2,1,0:T(2,128)S(1)} %fusion.57) | copy-start | bytes 294916
  260.8 11.6 %copy-start.17 = (f32[2,1280]{1,0:T(2,128)S(1)}, f32[2,1280]{1,0:T(2,128)}, u32[]{:S(2)}) copy-start(f32[2,1280]{1,0:T(2,128)} %param.11) | copy-start | bytes 30724
  260.8 11.1 %collective-permute-start = (bf16[3,2,1280]{2,1,0:T(2,128)(2,1)S(1)}, bf16[3,2,1280]{2,1,0:T(2,128)(2,1)S(1)}, u32[]{:S(2)}, u32[]{:S(2)}) collective-permute-start(bf16[3,2,1280]{2,1,0:T(2,128)(2,1)S(1)} %copy.48), channel_id=1, source_target_pairs={{0,4},{4,8},{8,12},{12,16},{16,20},{20,24},{24,28},{28,32},{32,36}... | collective-permute-start | bytes 46088 | tf_op jit(solution)/shard_map/ppermute | solution.py:22
  266.7 19.9 %copy-start.21 = (f32[6,2,16]{2,1,0:T(2,128)}, f32[6,2,16]{2,1,0:T(2,128)S(1)}, u32[]{:S(2)}) copy-start(f32[6,2,16]{2,1,0:T(2,128)S(1)} %get-tuple-element.30) | copy-start | bytes 2308
  304.6 7.0 %copy-start.20 = (f32[2,1024]{1,0:T(2,128)S(1)}, f32[2,1024]{1,0:T(2,128)}, u32[]{:S(2)}) copy-start(f32[2,1024]{1,0:T(2,128)} %param.15) | copy-start | bytes 24580
  304.6 8.7 %copy-start.23 = (f32[2,16,1,1]{1,0,3,2:T(2,128)S(1)}, f32[2,16,1,1]{1,0,3,2:T(2,128)}, u32[]{:S(2)}) copy-start(f32[2,16,1,1]{1,0,3,2:T(2,128)} %get-tuple-element.31) | copy-start | bytes 388
  304.6 10.1 %copy-start.12 = (f32[6,128,2,16]{1,0,3,2:T(8,128)S(1)}, f32[6,128,2,16]{1,0,3,2:T(8,128)}, u32[]{:S(2)}) copy-start(f32[6,128,2,16]{1,0,3,2:T(8,128)} %copy-done.11) | copy-start | bytes 294916
  307.3 29.6 %copy-start.16 = (f32[2,16]{1,0:T(2,128)S(1)}, f32[2,16]{1,0:T(2,128)}, u32[]{:S(2)}) copy-start(f32[2,16]{1,0:T(2,128)} %get-tuple-element.36) | copy-start | bytes 388
  309.0 27.6 %collective-permute-start.1 = (f32[2,16,72,128]{3,2,1,0:T(8,128)}, f32[2,16,72,128]{3,2,1,0:T(8,128)S(1)}, u32[]{:S(2)}, u32[]{:S(2)}) collective-permute-start(f32[2,16,72,128]{3,2,1,0:T(8,128)} %pad_maximum_fusion.1), channel_id=1, source_target_pairs={{0,4},{4,0},{1,5},{5,1},{2,6},{6,2},{3,7},{7,3},{8,12},{12,8},{9,1... | collective-permute-start | bytes 3538952 | tf_op jit(solution)/shard_map/ppermute | solution.py:43
  313.4 30.4 %slice-start = ((s8[6291456]{0:T(1024)(128)(4,1)}), s8[2097152]{0:T(1024)(128)(4,1)S(1)}, s32[]{:S(2)}) async-start(s8[6291456]{0:T(1024)(128)(4,1)} %bitcast.142), calls=%async_computation.3 | async-start | bytes 4194304
  316.7 27.1 %copy-start.3 = (f32[6,2,16,64,128]{4,3,2,1,0:T(8,128)S(1)}, f32[6,2,16,64,128]{4,3,2,1,0:T(8,128)}, u32[]{:S(2)}) copy-start(f32[6,2,16,64,128]{4,3,2,1,0:T(8,128)} %broadcast_dynamic-update-slice_fusion) | copy-start | bytes 18874372
  336.9 6.9 %slice-start.1 = ((s8[6291456]{0:T(1024)(128)(4,1)}), s8[4194304]{0:T(1024)(128)(4,1)S(1)}, s32[]{:S(2)}) async-start(s8[6291456]{0:T(1024)(128)(4,1)} %bitcast.142), calls=%async_computation.4 | async-start | bytes 8388608
  340.5 52.5 %collective-permute-start.2 = (f32[2,16,72,128]{3,2,1,0:T(8,128)S(1)}, f32[2,16,72,128]{3,2,1,0:T(8,128)S(1)}, u32[]{:S(2)}, u32[]{:S(2)}) collective-permute-start(f32[2,16,72,128]{3,2,1,0:T(8,128)S(1)} %pad_maximum_fusion.2), channel_id=1, source_target_pairs={{0,24},{8,0},{16,8},{24,16},{1,25},{9,1},{17,9},{25,17},{2,26},{10... | collective-permute-start | bytes 3538952 | tf_op jit(solution)/shard_map/ppermute | solution.py:43
  340.6 52.4 %collective-permute-start.3 = (f32[2,16,72,128]{3,2,1,0:T(8,128)S(1)}, f32[2,16,72,128]{3,2,1,0:T(8,128)S(1)}, u32[]{:S(2)}, u32[]{:S(2)}) collective-permute-start(f32[2,16,72,128]{3,2,1,0:T(8,128)S(1)} %pad_maximum_fusion.2), channel_id=1, source_target_pairs={{0,16},{8,24},{16,0},{24,8},{1,17},{9,25},{17,1},{25,9},{2,18},{10... | collective-permute-start | bytes 3538952 | tf_op jit(solution)/shard_map/ppermute | solution.py:43
  342.1 51.5 %collective-permute-start.4 = (f32[2,16,72,128]{3,2,1,0:T(8,128)S(1)}, f32[2,16,72,128]{3,2,1,0:T(8,128)S(1)}, u32[]{:S(2)}, u32[]{:S(2)}) collective-permute-start(f32[2,16,72,128]{3,2,1,0:T(8,128)S(1)} %pad_maximum_fusion.2), channel_id=1, source_target_pairs={{0,8},{8,16},{16,24},{24,0},{1,9},{9,17},{17,25},{25,1},{2,10},{10... | collective-permute-start | bytes 3538952 | tf_op jit(solution)/shard_map/ppermute | solution.py:43
  344.7 54.8 %copy-start.8 = (bf16[6,128,2,128]{3,1,0,2:T(8,128)(2,1)S(1)}, bf16[6,128,2,128]{3,1,0,2:T(8,128)(2,1)}, u32[]{:S(2)}) copy-start(bf16[6,128,2,128]{3,1,0,2:T(8,128)(2,1)} %copy-done.7) | copy-start | bytes 1179652
  344.7 54.8 %copy-start.9 = (bf16[6,128,2,128]{3,1,0,2:T(8,128)(2,1)S(1)}, bf16[6,128,2,128]{3,1,0,2:T(8,128)(2,1)}, u32[]{:S(2)}) copy-start(bf16[6,128,2,128]{3,1,0,2:T(8,128)(2,1)} %get-tuple-element.20) | copy-start | bytes 1179652
  344.7 55.2 %copy-start.2 = (bf16[6,128,2,1024]{1,3,2,0:T(8,128)(2,1)S(1)}, bf16[6,128,2,1024]{1,3,2,0:T(8,128)(2,1)}, u32[]{:S(2)}) copy-start(bf16[6,128,2,1024]{1,3,2,0:T(8,128)(2,1)} %copy-done.1) | copy-start | bytes 9437188
  344.7 55.2 %copy-start.13 = (f32[6,2,16,128]{3,2,1,0:T(8,128)S(1)}, f32[6,2,16,128]{3,2,1,0:T(8,128)}, u32[]{:S(2)}) copy-start(f32[6,2,16,128]{3,2,1,0:T(8,128)} %copy.57) | copy-start | bytes 294916
  344.7 55.2 %copy-start.14 = (pred[128,128]{1,0:T(8,128)(4,1)S(1)}, pred[128,128]{1,0:T(8,128)(4,1)}, u32[]{:S(2)}) copy-start(pred[128,128]{1,0:T(8,128)(4,1)} %iota_compare_fusion) | copy-start | bytes 49156
  395.0 32.4 %collective-permute-start.6 = (f32[2,16,72,128]{3,2,1,0:T(8,128)S(1)}, f32[2,16,72,128]{3,2,1,0:T(8,128)S(1)}, u32[]{:S(2)}, u32[]{:S(2)}) collective-permute-start(f32[2,16,72,128]{3,2,1,0:T(8,128)S(1)} %pad_maximum_fusion.3), channel_id=1, source_target_pairs={{0,64},{32,96},{1,65},{33,97},{2,66},{34,98},{3,67},{35,99},{4,68}... | collective-permute-start | bytes 3538952 | tf_op jit(solution)/shard_map/ppermute | solution.py:43
  396.5 12.2 %copy-start.4 = (f32[6,2,16,64,128]{4,3,2,1,0:T(8,128)}, f32[6,2,16,64,128]{4,3,2,1,0:T(8,128)S(1)}, u32[]{:S(2)}) copy-start(f32[6,2,16,64,128]{4,3,2,1,0:T(8,128)S(1)} %add_dynamic-update-slice_fusion) | copy-start | bytes 18874372
  396.5 31.0 %collective-permute-start.7 = (f32[2,16,72,128]{3,2,1,0:T(8,128)S(1)}, f32[2,16,72,128]{3,2,1,0:T(8,128)S(1)}, u32[]{:S(2)}, u32[]{:S(2)}) collective-permute-start(f32[2,16,72,128]{3,2,1,0:T(8,128)S(1)} %pad_maximum_fusion.3), channel_id=1, source_target_pairs={{0,96},{1,97},{2,98},{3,99},{4,100},{5,101},{6,102},{7,103},{8,104... | collective-permute-start | bytes 3538952 | tf_op jit(solution)/shard_map/ppermute | solution.py:43
  397.3 52.6 %collective-permute-start.5 = (f32[2,16,72,128]{3,2,1,0:T(8,128)S(1)}, f32[2,16,72,128]{3,2,1,0:T(8,128)S(1)}, u32[]{:S(2)}, u32[]{:S(2)}) collective-permute-start(f32[2,16,72,128]{3,2,1,0:T(8,128)S(1)} %pad_maximum_fusion.3), channel_id=1, source_target_pairs={{0,32},{32,64},{64,96},{1,33},{33,65},{65,97},{2,34},{34,66},{66,9... | collective-permute-start | bytes 3538952 | tf_op jit(solution)/shard_map/ppermute | solution.py:43
  408.7 43.6 %copy-start.10 = (bf16[6,128,2,128]{3,1,0,2:T(8,128)(2,1)S(1)}, bf16[6,128,2,128]{3,1,0,2:T(8,128)(2,1)}, u32[]{:S(2)}) copy-start(bf16[6,128,2,128]{3,1,0,2:T(8,128)(2,1)} %get-tuple-element.20) | copy-start | bytes 1179652
  408.7 43.6 %copy-start.22 = (f32[6,2,16]{2,1,0:T(2,128)S(1)}, f32[6,2,16]{2,1,0:T(2,128)}, u32[]{:S(2)}) copy-start(f32[6,2,16]{2,1,0:T(2,128)} %copy-done.21) | copy-start | bytes 2308
  408.7 43.6 %copy-start.25 = (f32[2,16]{1,0:T(2,128)S(1)}, f32[2,16]{1,0:T(2,128)}, u32[]{:S(2)}) copy-start(f32[2,16]{1,0:T(2,128)} %param.14) | copy-start | bytes 388
  427.4 25.0 %copy-start.5 = (f32[6,2,16,64,128]{4,3,2,1,0:T(8,128)S(1)}, f32[6,2,16,64,128]{4,3,2,1,0:T(8,128)}, u32[]{:S(2)}) copy-start(f32[6,2,16,64,128]{4,3,2,1,0:T(8,128)} %copy-done.4) | copy-start | bytes 18874372
  (7 other events, 29.9 us)
Sparse Core Ops, SparseCore 0:
  9.0 29.1 all-gather.5
  39.8 51.5 all-gather.3
  93.5 140.9 all-gather.7

commit v4 on v3

--- a/solution.py
+++ b/solution.py
@@ -149,7 +149,19 @@
 
 
 def per_device(tokens, w_in, conv_w, conv_b, dt_bias, a_log, d_skip, norm_gain):
-    gathered = lax.all_gather(tokens, "chan", axis=1, tiled=True)
+    size = lax.axis_size("chan")
+    place = lax.axis_index("chan")
+    width = tokens.shape[1]
+    gathered = jnp.zeros((tokens.shape[0], width * size), tokens.dtype)
+    for distance in range(size):
+        if distance:
+            piece = lax.ppermute(
+                tokens, "chan", [(i, (i + distance) % size) for i in range(size)]
+            )
+        else:
+            piece = tokens
+        source = (place - distance) % size
+        gathered = lax.dynamic_update_slice(gathered, piece, (0, source * width))
     return mix_groups(gathered, w_in, conv_w, conv_b, dt_bias, a_log, d_skip, norm_gain)
 
 

time: 477 us -> 425 us (0.89)
  waiting for transfers between devices: 336 us -> 268 us
  local copies, waits for them, and re-layouts: 41.3 us -> 51.6 us
  starting transfers between devices: 13.8 us -> 19.9 us
    all_gather x1, waiting for transfers between devices: 143 us -> 72.4 us  [mix_groups(): full_w = lax.all_gather(pair_w, SEQ[:2], axis=0, tiled=True)]
    ppermute x0 -> x3, waiting for transfers between devices: none -> 54.1 us  [per_device(): lax.ppermute(tokens, 'chan', [(i, (i + distance) % size) for i in range(s...]
    all_gather x1 -> x0, waiting for transfers between devices: 51.5 us -> none  [per_device(): gathered = lax.all_gather(tokens, 'chan', axis=1, tiled=True)]
    dynamic_update_slice x0 -> x4, local copies, waits for them, and re-layouts: none -> 8.18 us  [per_device(): gathered = lax.dynamic_update_slice(gathered, piece, (0, source * width))]
    ppermute x0 -> x3, starting transfers between devices: none -> 5.89 us  [per_device(): lax.ppermute(tokens, 'chan', [(i, (i + distance) % size) for i in range(s...]
  transfers between devices with their start and end apart: 11 -> 13, of which waited for: 8 -> 9; matrix products, arithmetic and copies ran while one was open for 5% -> 8% of each run, Pallas kernels for 0% -> 0%
where the time goes in v4:
time: 425 us; the launch traced here: 421 us
  waiting for transfers between devices  268 us (63%)
  local copies, waits for them, and re-layouts  51.6 us (12%)
  matrix products  38.1 us (9%)
  other arithmetic  29.8 us (7%)
  starting transfers between devices  19.9 us (5%)
  between operations  14 us (3%)
    ppermute x7, waiting for transfers between devices, gather_level(): got = lax.ppermute(packed, axis, route)  110 us
    all_gather x1, waiting for transfers between devices, mix_groups(): full_w = lax.all_gather(pair_w, SEQ[:2], axis=0, tiled=True)  72.4 us
    ppermute x3, waiting for transfers between devices, per_device(): lax.ppermute(tokens, 'chan', [(i, (i + distance) % size) for i in range(s...  54.1 us
    all_gather x1, waiting for transfers between devices, mix_groups(): pair_w = lax.all_gather(rows_first, SEQ[2], axis=0, tiled=True)  30.9 us
    dot_general x1, matrix products, mix_groups(): jnp.einsum('td,dgc->tgc', gathered, full_w, preferred_element_type=jnp.fl...  22.6 us
    convert_element_type x1, other arithmetic, mix_groups(): inputs = jax.nn.silu(pre_act).astype(jnp.bfloat16)  14.3 us
    ppermute x7, starting transfers between devices, gather_level(): got = lax.ppermute(packed, axis, route)  10.3 us
    dot_general x1, matrix products, mix_groups(): jnp.einsum('qghij,qjghp->qighp', weights, x_all, preferred_element_type=j...  8.78 us
  transfers between devices with their start and end apart: 13, of which 9 were waited for; matrix products, arithmetic and copies ran while one was open for 8% of the time, Pallas kernels for 0%

profile of v4, /device:TPU:22, one launch (start us, length us, event | category | flops | bytes accessed | tf_op | source)
XLA Modules:
  0.0 421.4 jit_solution(18259313116447766664)
XLA Ops:
  7.3 30.9 %all-gather.3.cloned.1.call-done = bf16[256,2,1296]{0,2,1:T(8,128)(2,1)} async-done(((bf16[128,2,1296]{0,2,1:T(8,128)(2,1)}), bf16[256,2,1296]{0,2,1:T(8,128)(2,1)}) %all-gather.3.cloned.1.call-update) | async-done | bytes 1327120 | tf_op jit(solution)/shard_map/all_gather | solution.py:77
  38.3 2.9 collective-permute-start.1
  41.2 2.9 collective-permute-start.2
  44.8 3.5 broadcast_in_dim.19
  49.7 26.5 %collective-permute-done = bf16[768,1024]{1,0:T(8,128)(2,1)} collective-permute-done((bf16[768,1024]{1,0:T(8,128)(2,1)}, bf16[768,1024]{1,0:T(8,128)(2,1)}, u32[]{:S(2)}, u32[]{:S(2)}) %collective-permute-start) | collective-permute-done | bytes 1572896 | tf_op jit(solution)/shard_map/ppermute | solution.py:158
  76.2 2.8 constant_dynamic-update-slice_fusion.10
  78.9 2.8 constant_dynamic-update-slice_fusion.9
  81.7 27.7 %collective-permute-done.2 = bf16[768,1024]{1,0:T(8,128)(2,1)S(1)} collective-permute-done((bf16[768,1024]{1,0:T(8,128)(2,1)}, bf16[768,1024]{1,0:T(8,128)(2,1)S(1)}, u32[]{:S(2)}, u32[]{:S(2)}) %collective-permute-start.2) | collective-permute-done | bytes 1572896 | tf_op jit(solution)/shard_map/ppermute | solution.py:158
  110.7 72.4 %all-gather.5.cloned.1.call-done = bf16[4096,2,1296]{0,2,1:T(8,128)(2,1)} async-done(((bf16[256,2,1296]{0,2,1:T(8,128)(2,1)}), bf16[4096,2,1296]{0,2,1:T(8,128)(2,1)}) %all-gather.5.cloned.1.call-update) | async-done | bytes 21233680 | tf_op jit(solution)/shard_map/all_gather | solution.py:78
  183.1 22.6 %fusion.56 = (bf16[768,2,1296]{0,2,1:T(8,128)(2,1)}, f32[768,2,1296]{0,2,1:T(8,128)S(1)}) fusion(bf16[4096,2,1296]{0,2,1:T(8,128)(2,1)} %all-gather.5.cloned.1.call-done, bf16[768,4096]{1,0:T(8,128)(2,1)} %constant_dynamic-update-slice_fusion.8), kind=kOutput, calls=%fused_computation.144 | convolution fusion | flops 16309444608 | bytes 39469056 | tf_op jit(solution)/shard_map/td,dgc->tgc/dot_general | solution.py:81
  208.7 3.7 collective-permute-start.3
  215.3 4.2 %slice.169 = bf16[768,2,1280]{0,2,1:T(8,128)(2,1)} slice(bf16[768,2,1296]{0,2,1:T(8,128)(2,1)} %get-tuple-element.39), slice={[0:768], [0:2], [0:1280]} | slice | bytes 7864320 | tf_op jit(solution)/shard_map/slice | solution.py:87
  220.9 14.3 %multiply_convert_fusion.1 = bf16[768,2,1280]{0,2,1:T(8,128)(2,1)} fusion(bf16[768,2,1280]{0,2,1:T(8,128)(2,1)} %slice.169, bf16[3,2,1280]{0,2,1:T(8,128)(2,1)S(1)} %copy.49, f32[2,1280]{1,0:T(2,128)S(1)} %get-tuple-element.43, f32[2,1280]{1,0:T(2,128)S(1)} %get-tuple-element.44, f32[2,1280]{1,0:T(2,128)S(1)} %get-tuple-element.45, ...), kind=kLoop, calls=%fused_computation.3 | loop fusion | flops 51118080 | bytes 7930880 | tf_op jit(solution)/shard_map/convert_element_type | solution.py:94
  235.2 6.1 %copy.50 = bf16[768,2,1280]{2,0,1:T(8,128)(2,1)} copy(bf16[768,2,1280]{0,2,1:T(8,128)(2,1)} %multiply_convert_fusion.1) | data formatting | bytes 7864320 | tf_op jit(solution)/shard_map/convert_element_type | solution.py:94
  241.4 2.0 fusion.54
  243.3 4.0 slice.174
  247.3 3.5 copy.51
  250.9 2.0 fusion.17
  252.9 2.6 copy-done
  257.3 2.5 collective-permute-start.4
  264.3 20.5 %collective-permute-done.4 = f32[2,16,72,128]{3,2,1,0:T(8,128)S(1)} collective-permute-done((f32[2,16,72,128]{3,2,1,0:T(8,128)}, f32[2,16,72,128]{3,2,1,0:T(8,128)S(1)}, u32[]{:S(2)}, u32[]{:S(2)}) %collective-permute-start.4) | collective-permute-done | bytes 1179680 | tf_op jit(solution)/shard_map/ppermute | solution.py:43
  285.1 3.4 add_select_fusion.2
  290.3 1.8 collective-permute-start.7
  293.0 48.2 %collective-permute-done.5 = f32[2,16,72,128]{3,2,1,0:T(8,128)S(1)} collective-permute-done((f32[2,16,72,128]{3,2,1,0:T(8,128)S(1)}, f32[2,16,72,128]{3,2,1,0:T(8,128)S(1)}, u32[]{:S(2)}, u32[]{:S(2)}) %collective-permute-start.5) | collective-permute-done | bytes 1179680 | tf_op jit(solution)/shard_map/ppermute | solution.py:43
  345.5 2.4 collective-permute-start.8
  348.4 8.8 %fusion = f32[6,2,16,64,128]{4,3,2,1,0:T(8,128)} fusion(bf16[6,128,2,16,64]{1,4,3,2,0:T(8,128)(2,1)S(1)} %bitcast.146, f32[6,2,16,128]{3,2,1,0:T(8,128)S(1)} %copy-done.14, f32[6,2,16,128]{3,2,1,0:T(8,128)S(1)} %copy.55, f32[6,2,128,128]{3,2,1,0:T(8,128)S(1)} %fusion.39, pred[128,128]{1,0:T(8,128)(4,1)S(1)} %iota_compare_fusion), kind=kOutput, calls=%fused_computation.4 | convolution fusion | flops 421527552 | bytes 10436608 | tf_op jit(solution)/shard_map/qghij,qjghp->qighp/dot_general | solution.py:133
  357.2 18.4 %collective-permute-done.9 = f32[2,16,72,128]{3,2,1,0:T(8,128)S(1)} collective-permute-done((f32[2,16,72,128]{3,2,1,0:T(8,128)S(1)}, f32[2,16,72,128]{3,2,1,0:T(8,128)S(1)}, u32[]{:S(2)}, u32[]{:S(2)}) %collective-permute-start.9) | collective-permute-done | bytes 1179680 | tf_op jit(solution)/shard_map/ppermute | solution.py:43
  376.0 22.1 %collective-permute-done.8 = f32[2,16,72,128]{3,2,1,0:T(8,128)S(1)} collective-permute-done((f32[2,16,72,128]{3,2,1,0:T(8,128)S(1)}, f32[2,16,72,128]{3,2,1,0:T(8,128)S(1)}, u32[]{:S(2)}, u32[]{:S(2)}) %collective-permute-start.8) | collective-permute-done | bytes 1179680 | tf_op jit(solution)/shard_map/ppermute | solution.py:43
  398.3 2.3 fusion.26
  400.6 4.4 %multiply_reduce_fusion = (f32[6,128,2]{1,2,0:T(2,128)S(1)}, f32[6,128,2,16,64]{1,4,3,2,0:T(8,128)S(1)}) fusion(bf16[6,128,2,128]{3,1,0,2:T(8,128)(2,1)S(1)} %copy-done.10, f32[6,2,16,64,128]{4,3,2,1,0:T(8,128)S(1)} %copy-done.5, f32[2,16,64,128]{3,2,1,0:T(8,128)S(1)} %fusion.26, f32[6,2,16]{2,1,0:T(2,128)S(1)} %copy-done.23, ...), kind=kOutput, calls=%fused_computation.14 | convolution fusion | flops 418380288 | bytes 23567232 | tf_op jit(solution)/shard_map/qign,qghpn->qighp/dot_general | solution.py:138
  405.0 5.6 %copy.62 = f32[6,128,2,16,64]{1,0,4,3,2:T(8,128)S(1)} copy(f32[6,128,2,16,64]{1,4,3,2,0:T(8,128)S(1)} %get-tuple-element.42) | data formatting | bytes 12582912 | tf_op jit(solution)/shard_map/add | solution.py:144
  411.7 2.9 copy.63
  (128 shorter events, 26.9 us)
Async XLA Ops:
  6.5 41.7 %copy-start.13 = (bf16[768,1024]{1,0:T(8,128)(2,1)S(1)}, bf16[768,1024]{1,0:T(8,128)(2,1)}, u32[]{:S(2)}) copy-start(bf16[768,1024]{1,0:T(8,128)(2,1)} %param.8) | copy-start | bytes 4718596
  6.5 43.1 %copy-start.15 = (f32[2,4,1280]{2,1,0:T(4,128)S(1)}, f32[2,4,1280]{2,1,0:T(4,128)}, u32[]{:S(2)}) copy-start(f32[2,4,1280]{2,1,0:T(4,128)} %param.10) | copy-start | bytes 122884
  6.5 31.6 %all-gather.3.cloned.1.call-start = ((), (), s32[]{:S(2)}) async-start(), calls=%async_computation | async-start | bytes 1990656 | tf_op jit(solution)/shard_map/all_gather | solution.py:77
  7.3 175.8 %all-gather.5.cloned.1.call-start = ((), (), s32[]{:S(2)}) async-start(), calls=%async_computation.1 | async-start | bytes 22560768 | tf_op jit(solution)/shard_map/all_gather | solution.py:78
  38.2 38.0 %collective-permute-start = (bf16[768,1024]{1,0:T(8,128)(2,1)}, bf16[768,1024]{1,0:T(8,128)(2,1)}, u32[]{:S(2)}, u32[]{:S(2)}) collective-permute-start(bf16[768,1024]{1,0:T(8,128)(2,1)} %param.8), channel_id=1, source_target_pairs={{0,1},{1,2},{2,3},{3,0},{4,5},{5,6},{6,7},{7,4},{8,9},{9,10},{10,1... | collective-permute-start | bytes 4718600 | tf_op jit(solution)/shard_map/ppermute | solution.py:158
  38.3 40.7 %collective-permute-start.1 = (bf16[768,1024]{1,0:T(8,128)(2,1)}, bf16[768,1024]{1,0:T(8,128)(2,1)}, u32[]{:S(2)}, u32[]{:S(2)}) collective-permute-start(bf16[768,1024]{1,0:T(8,128)(2,1)} %param.8), channel_id=1, source_target_pairs={{0,2},{1,3},{2,0},{3,1},{4,6},{5,7},{6,4},{7,5},{8,10},{9,11},{10,... | collective-permute-start | bytes 4718600 | tf_op jit(solution)/shard_map/ppermute | solution.py:158
  41.2 68.1 %collective-permute-start.2 = (bf16[768,1024]{1,0:T(8,128)(2,1)}, bf16[768,1024]{1,0:T(8,128)(2,1)S(1)}, u32[]{:S(2)}, u32[]{:S(2)}) collective-permute-start(bf16[768,1024]{1,0:T(8,128)(2,1)} %param.8), channel_id=1, source_target_pairs={{0,3},{1,0},{2,1},{3,2},{4,7},{5,4},{6,5},{7,6},{8,11},{9,8},{10,9... | collective-permute-start | bytes 4718600 | tf_op jit(solution)/shard_map/ppermute | solution.py:158
  110.7 95.1 %copy-start.25 = (f32[2,16]{1,0:T(2,128)S(1)}, f32[2,16]{1,0:T(2,128)}, u32[]{:S(2)}) copy-start(f32[2,16]{1,0:T(2,128)} %param.12) | copy-start | bytes 388
  206.6 12.9 %copy-start.6 = (f32[6,128,2,16]{3,2,1,0:T(2,128)}, f32[6,128,2,16]{3,2,1,0:T(2,128)S(1)}, u32[]{:S(2)}) copy-start(f32[6,128,2,16]{3,2,1,0:T(2,128)S(1)} %fusion.57) | copy-start | bytes 294916
  208.7 11.8 %collective-permute-start.3 = (bf16[3,2,1280]{2,1,0:T(2,128)(2,1)S(1)}, bf16[3,2,1280]{2,1,0:T(2,128)(2,1)S(1)}, u32[]{:S(2)}, u32[]{:S(2)}) collective-permute-start(bf16[3,2,1280]{2,1,0:T(2,128)(2,1)S(1)} %copy.48), channel_id=1, source_target_pairs={{0,4},{4,8},{8,12},{12,16},{16,20},{20,24},{24,28},{28,32},{32,36}... | collective-permute-start | bytes 46088 | tf_op jit(solution)/shard_map/ppermute | solution.py:22
  215.3 19.9 %copy-start.22 = (f32[6,2,16]{2,1,0:T(2,128)}, f32[6,2,16]{2,1,0:T(2,128)S(1)}, u32[]{:S(2)}) copy-start(f32[6,2,16]{2,1,0:T(2,128)S(1)} %get-tuple-element.30) | copy-start | bytes 2308
  252.9 9.4 %copy-start.12 = (f32[6,128,2,16]{1,0,3,2:T(8,128)S(1)}, f32[6,128,2,16]{1,0,3,2:T(8,128)}, u32[]{:S(2)}) copy-start(f32[6,128,2,16]{1,0,3,2:T(8,128)} %copy-done.11) | copy-start | bytes 294916
  252.9 10.1 %copy-start.24 = (f32[2,16,1,1]{1,0,3,2:T(2,128)S(1)}, f32[2,16,1,1]{1,0,3,2:T(2,128)}, u32[]{:S(2)}) copy-start(f32[2,16,1,1]{1,0,3,2:T(2,128)} %get-tuple-element.31) | copy-start | bytes 388
  255.5 29.6 %copy-start.17 = (f32[2,16]{1,0:T(2,128)S(1)}, f32[2,16]{1,0:T(2,128)}, u32[]{:S(2)}) copy-start(f32[2,16]{1,0:T(2,128)} %get-tuple-element.36) | copy-start | bytes 388
  257.3 27.6 %collective-permute-start.4 = (f32[2,16,72,128]{3,2,1,0:T(8,128)}, f32[2,16,72,128]{3,2,1,0:T(8,128)S(1)}, u32[]{:S(2)}, u32[]{:S(2)}) collective-permute-start(f32[2,16,72,128]{3,2,1,0:T(8,128)} %pad_maximum_fusion.1), channel_id=1, source_target_pairs={{0,4},{4,0},{1,5},{5,1},{2,6},{6,2},{3,7},{7,3},{8,12},{12,8},{9,1... | collective-permute-start | bytes 3538952 | tf_op jit(solution)/shard_map/ppermute | solution.py:43
  260.9 31.1 %slice-start = ((s8[6291456]{0:T(1024)(128)(4,1)}), s8[2097152]{0:T(1024)(128)(4,1)S(1)}, s32[]{:S(2)}) async-start(s8[6291456]{0:T(1024)(128)(4,1)} %bitcast.142), calls=%async_computation.2 | async-start | bytes 4194304
  264.3 27.7 %copy-start.3 = (f32[6,2,16,64,128]{4,3,2,1,0:T(8,128)S(1)}, f32[6,2,16,64,128]{4,3,2,1,0:T(8,128)}, u32[]{:S(2)}) copy-start(f32[6,2,16,64,128]{4,3,2,1,0:T(8,128)} %broadcast_dynamic-update-slice_fusion) | copy-start | bytes 18874372
  288.7 52.5 %collective-permute-start.5 = (f32[2,16,72,128]{3,2,1,0:T(8,128)S(1)}, f32[2,16,72,128]{3,2,1,0:T(8,128)S(1)}, u32[]{:S(2)}, u32[]{:S(2)}) collective-permute-start(f32[2,16,72,128]{3,2,1,0:T(8,128)S(1)} %pad_maximum_fusion.2), channel_id=1, source_target_pairs={{0,24},{8,0},{16,8},{24,16},{1,25},{9,1},{17,9},{25,17},{2,26},{10... | collective-permute-start | bytes 3538952 | tf_op jit(solution)/shard_map/ppermute | solution.py:43
  288.8 52.4 %collective-permute-start.6 = (f32[2,16,72,128]{3,2,1,0:T(8,128)S(1)}, f32[2,16,72,128]{3,2,1,0:T(8,128)S(1)}, u32[]{:S(2)}, u32[]{:S(2)}) collective-permute-start(f32[2,16,72,128]{3,2,1,0:T(8,128)S(1)} %pad_maximum_fusion.2), channel_id=1, source_target_pairs={{0,16},{8,24},{16,0},{24,8},{1,17},{9,25},{17,1},{25,9},{2,18},{10... | collective-permute-start | bytes 3538952 | tf_op jit(solution)/shard_map/ppermute | solution.py:43
  290.3 51.6 %collective-permute-start.7 = (f32[2,16,72,128]{3,2,1,0:T(8,128)S(1)}, f32[2,16,72,128]{3,2,1,0:T(8,128)S(1)}, u32[]{:S(2)}, u32[]{:S(2)}) collective-permute-start(f32[2,16,72,128]{3,2,1,0:T(8,128)S(1)} %pad_maximum_fusion.2), channel_id=1, source_target_pairs={{0,8},{8,16},{16,24},{24,0},{1,9},{9,17},{17,25},{25,1},{2,10},{10... | collective-permute-start | bytes 3538952 | tf_op jit(solution)/shard_map/ppermute | solution.py:43
  293.0 55.0 %copy-start.8 = (bf16[6,128,2,128]{3,1,0,2:T(8,128)(2,1)S(1)}, bf16[6,128,2,128]{3,1,0,2:T(8,128)(2,1)}, u32[]{:S(2)}) copy-start(bf16[6,128,2,128]{3,1,0,2:T(8,128)(2,1)} %copy-done.7) | copy-start | bytes 1179652
  293.0 55.0 %copy-start.9 = (bf16[6,128,2,128]{3,1,0,2:T(8,128)(2,1)S(1)}, bf16[6,128,2,128]{3,1,0,2:T(8,128)(2,1)}, u32[]{:S(2)}) copy-start(bf16[6,128,2,128]{3,1,0,2:T(8,128)(2,1)} %get-tuple-element.20) | copy-start | bytes 1179652
  293.0 55.4 %copy-start.2 = (bf16[6,128,2,1024]{1,3,2,0:T(8,128)(2,1)S(1)}, bf16[6,128,2,1024]{1,3,2,0:T(8,128)(2,1)}, u32[]{:S(2)}) copy-start(bf16[6,128,2,1024]{1,3,2,0:T(8,128)(2,1)} %copy-done.1) | copy-start | bytes 9437188
  293.0 55.4 %copy-start.14 = (f32[6,2,16,128]{3,2,1,0:T(8,128)S(1)}, f32[6,2,16,128]{3,2,1,0:T(8,128)}, u32[]{:S(2)}) copy-start(f32[6,2,16,128]{3,2,1,0:T(8,128)} %copy.57) | copy-start | bytes 294916
  343.2 32.4 %collective-permute-start.9 = (f32[2,16,72,128]{3,2,1,0:T(8,128)S(1)}, f32[2,16,72,128]{3,2,1,0:T(8,128)S(1)}, u32[]{:S(2)}, u32[]{:S(2)}) collective-permute-start(f32[2,16,72,128]{3,2,1,0:T(8,128)S(1)} %pad_maximum_fusion.3), channel_id=1, source_target_pairs={{0,64},{32,96},{1,65},{33,97},{2,66},{34,98},{3,67},{35,99},{4,68}... | collective-permute-start | bytes 3538952 | tf_op jit(solution)/shard_map/ppermute | solution.py:43
  344.8 12.4 %copy-start.4 = (f32[6,2,16,64,128]{4,3,2,1,0:T(8,128)}, f32[6,2,16,64,128]{4,3,2,1,0:T(8,128)S(1)}, u32[]{:S(2)}) copy-start(f32[6,2,16,64,128]{4,3,2,1,0:T(8,128)S(1)} %add_dynamic-update-slice_fusion) | copy-start | bytes 18874372
  344.8 31.0 %collective-permute-start.10 = (f32[2,16,72,128]{3,2,1,0:T(8,128)S(1)}, f32[2,16,72,128]{3,2,1,0:T(8,128)S(1)}, u32[]{:S(2)}, u32[]{:S(2)}) collective-permute-start(f32[2,16,72,128]{3,2,1,0:T(8,128)S(1)} %pad_maximum_fusion.3), channel_id=1, source_target_pairs={{0,96},{1,97},{2,98},{3,99},{4,100},{5,101},{6,102},{7,103},{8,104... | collective-permute-start | bytes 3538952 | tf_op jit(solution)/shard_map/ppermute | solution.py:43
  345.5 52.6 %collective-permute-start.8 = (f32[2,16,72,128]{3,2,1,0:T(8,128)S(1)}, f32[2,16,72,128]{3,2,1,0:T(8,128)S(1)}, u32[]{:S(2)}, u32[]{:S(2)}) collective-permute-start(f32[2,16,72,128]{3,2,1,0:T(8,128)S(1)} %pad_maximum_fusion.3), channel_id=1, source_target_pairs={{0,32},{32,64},{64,96},{1,33},{33,65},{65,97},{2,34},{34,66},{66,9... | collective-permute-start | bytes 3538952 | tf_op jit(solution)/shard_map/ppermute | solution.py:43
  357.2 43.4 %copy-start.10 = (bf16[6,128,2,128]{3,1,0,2:T(8,128)(2,1)S(1)}, bf16[6,128,2,128]{3,1,0,2:T(8,128)(2,1)}, u32[]{:S(2)}) copy-start(bf16[6,128,2,128]{3,1,0,2:T(8,128)(2,1)} %get-tuple-element.20) | copy-start | bytes 1179652
  357.2 43.4 %copy-start.23 = (f32[6,2,16]{2,1,0:T(2,128)S(1)}, f32[6,2,16]{2,1,0:T(2,128)}, u32[]{:S(2)}) copy-start(f32[6,2,16]{2,1,0:T(2,128)} %copy-done.22) | copy-start | bytes 2308
  357.2 43.4 %copy-start.26 = (f32[2,16]{1,0:T(2,128)S(1)}, f32[2,16]{1,0:T(2,128)}, u32[]{:S(2)}) copy-start(f32[2,16]{1,0:T(2,128)} %param.14) | copy-start | bytes 388
  375.6 25.0 %copy-start.5 = (f32[6,2,16,64,128]{4,3,2,1,0:T(8,128)S(1)}, f32[6,2,16,64,128]{4,3,2,1,0:T(8,128)}, u32[]{:S(2)}) copy-start(f32[6,2,16,64,128]{4,3,2,1,0:T(8,128)} %copy-done.4) | copy-start | bytes 18874372
  (10 other events, 52.9 us)
Sparse Core Ops, SparseCore 0:
  9.0 29.1 all-gather.2
  40.3 142.7 all-gather.4

commit v5 on v4

--- a/solution.py
+++ b/solution.py
@@ -74,7 +74,19 @@
     row_count = gathered.shape[0]
     rows_first = jnp.transpose(w_in, (1, 0, 2))
     if isinstance(SEQ, tuple):
-        pair_w = lax.all_gather(rows_first, SEQ[2], axis=0, tiled=True)
+        pair = lax.axis_size(SEQ[2])
+        slot = lax.axis_index(SEQ[2])
+        piece = rows_first.shape[0]
+        pair_w = jnp.zeros((piece * pair,) + rows_first.shape[1:], rows_first.dtype)
+        for distance in range(pair):
+            if distance:
+                rows = lax.ppermute(
+                    rows_first, SEQ[2], [(i, (i + distance) % pair) for i in range(pair)]
+                )
+            else:
+                rows = rows_first
+            source = (slot - distance) % pair
+            pair_w = lax.dynamic_update_slice(pair_w, rows, (source * piece, 0, 0))
         full_w = lax.all_gather(pair_w, SEQ[:2], axis=0, tiled=True)
     else:
         full_w = lax.all_gather(rows_first, SEQ, axis=0, tiled=True)

time: 425 us -> 413 us (0.972)
  waiting for transfers between devices: 268 us -> 247 us
  local copies, waits for them, and re-layouts: 51.6 us -> 57 us
    all_gather x1 -> x0, waiting for transfers between devices: 30.9 us -> none  [mix_groups(): pair_w = lax.all_gather(rows_first, SEQ[2], axis=0, tiled=True)]
    ppermute x0 -> x1, waiting for transfers between devices: none -> 13.9 us  [mix_groups(): lax.ppermute(rows_first, SEQ[2], [(i, (i + distance) % pair) for i in ran...]
  transfers between devices with their start and end apart: 13 -> 13, of which waited for: 9 -> 9; matrix products, arithmetic and copies ran while one was open for 8% -> 9% of each run, Pallas kernels for 0% -> 0%
where the time goes in v5:
time: 413 us; the launch traced here: 409 us
  waiting for transfers between devices  247 us (60%)
  local copies, waits for them, and re-layouts  57 us (14%)
  matrix products  38.2 us (9%)
  other arithmetic  29.7 us (7%)
  starting transfers between devices  22.6 us (5%)
  between operations  14 us (3%)
    ppermute x7, waiting for transfers between devices, gather_level(): got = lax.ppermute(packed, axis, route)  110 us
    all_gather x1, waiting for transfers between devices, mix_groups(): full_w = lax.all_gather(pair_w, SEQ[:2], axis=0, tiled=True)  69.1 us
    ppermute x3, waiting for transfers between devices, per_device(): lax.ppermute(tokens, 'chan', [(i, (i + distance) % size) for i in range(s...  54.2 us
    dot_general x1, matrix products, mix_groups(): jnp.einsum('td,dgc->tgc', gathered, full_w, preferred_element_type=jnp.fl...  22.7 us
    convert_element_type x1, other arithmetic, mix_groups(): inputs = jax.nn.silu(pre_act).astype(jnp.bfloat16)  14.3 us
    ppermute x1, waiting for transfers between devices, mix_groups(): lax.ppermute(rows_first, SEQ[2], [(i, (i + distance) % pair) for i in ran...  13.9 us
    ppermute x7, starting transfers between devices, gather_level(): got = lax.ppermute(packed, axis, route)  10.3 us
    dynamic_update_slice x4, local copies, waits for them, and re-layouts, per_device(): gathered = lax.dynamic_update_slice(gathered, piece, (0, source * width))  9.59 us
  transfers between devices with their start and end apart: 13, of which 9 were waited for; matrix products, arithmetic and copies ran while one was open for 9% of the time, Pallas kernels for 0%

profile of v5, /device:TPU:22, one launch (start us, length us, event | category | flops | bytes accessed | tf_op | source)
XLA Modules:
  0.0 408.5 jit_solution(1248516923281096063)
XLA Ops:
  9.8 13.9 %collective-permute-done.3 = bf16[128,2,1296]{0,2,1:T(8,128)(2,1)} collective-permute-done((bf16[128,2,1296]{0,2,1:T(8,128)(2,1)}, bf16[128,2,1296]{0,2,1:T(8,128)(2,1)}, u32[]{:S(2)}, u32[]{:S(2)}) %collective-permute-start.3) | collective-permute-done | bytes 663584 | tf_op jit(solution)/shard_map/ppermute | solution.py:83
  26.1 3.8 collective-permute-start.1
  29.9 2.9 collective-permute-start.2
  33.4 3.5 broadcast_in_dim.21
  38.4 25.4 %collective-permute-done = bf16[768,1024]{1,0:T(8,128)(2,1)} collective-permute-done((bf16[768,1024]{1,0:T(8,128)(2,1)}, bf16[768,1024]{1,0:T(8,128)(2,1)}, u32[]{:S(2)}, u32[]{:S(2)}) %collective-permute-start) | collective-permute-done | bytes 1572896 | tf_op jit(solution)/shard_map/ppermute | solution.py:170
  63.8 2.8 constant_dynamic-update-slice_fusion.12
  66.5 2.7 constant_dynamic-update-slice_fusion.11
  69.2 28.8 %collective-permute-done.2 = bf16[768,1024]{1,0:T(8,128)(2,1)} collective-permute-done((bf16[768,1024]{1,0:T(8,128)(2,1)}, bf16[768,1024]{1,0:T(8,128)(2,1)}, u32[]{:S(2)}, u32[]{:S(2)}) %collective-permute-start.2) | collective-permute-done | bytes 1572896 | tf_op jit(solution)/shard_map/ppermute | solution.py:170
  98.0 2.8 constant_dynamic-update-slice_fusion.10
  100.8 69.1 %all-gather.2.cloned.1.call-done = bf16[4096,2,1296]{0,2,1:T(8,128)(2,1)} async-done(((bf16[256,2,1296]{0,2,1:T(8,128)(2,1)}), bf16[4096,2,1296]{0,2,1:T(8,128)(2,1)}) %all-gather.2.cloned.1.call-update) | async-done | bytes 21233680 | tf_op jit(solution)/shard_map/all_gather | solution.py:90
  169.9 22.7 %fusion.56 = (bf16[768,2,1296]{0,2,1:T(8,128)(2,1)}, f32[768,2,1296]{0,2,1:T(8,128)S(1)}) fusion(bf16[4096,2,1296]{0,2,1:T(8,128)(2,1)} %all-gather.2.cloned.1.call-done, bf16[768,4096]{1,0:T(8,128)(2,1)} %constant_dynamic-update-slice_fusion.10), kind=kOutput, calls=%fused_computation.146 | convolution fusion | flops 16309444608 | bytes 39469056 | tf_op jit(solution)/shard_map/td,dgc->tgc/dot_general | solution.py:93
  195.5 3.6 collective-permute-start.4
  202.1 4.2 %slice.169 = bf16[768,2,1280]{0,2,1:T(8,128)(2,1)} slice(bf16[768,2,1296]{0,2,1:T(8,128)(2,1)} %get-tuple-element.39), slice={[0:768], [0:2], [0:1280]} | slice | bytes 7864320 | tf_op jit(solution)/shard_map/slice | solution.py:99
  207.8 14.3 %multiply_convert_fusion.1 = bf16[768,2,1280]{0,2,1:T(8,128)(2,1)} fusion(bf16[768,2,1280]{0,2,1:T(8,128)(2,1)} %slice.169, bf16[3,2,1280]{0,2,1:T(8,128)(2,1)S(1)} %copy.49, f32[2,1280]{1,0:T(2,128)S(1)} %get-tuple-element.43, f32[2,1280]{1,0:T(2,128)S(1)} %get-tuple-element.44, f32[2,1280]{1,0:T(2,128)S(1)} %get-tuple-element.45, ...), kind=kLoop, calls=%fused_computation.3 | loop fusion | flops 51118080 | bytes 7930880 | tf_op jit(solution)/shard_map/convert_element_type | solution.py:106
  222.1 6.4 %copy.50 = bf16[768,2,1280]{2,0,1:T(8,128)(2,1)} copy(bf16[768,2,1280]{0,2,1:T(8,128)(2,1)} %multiply_convert_fusion.1) | data formatting | bytes 7864320 | tf_op jit(solution)/shard_map/convert_element_type | solution.py:106
  228.5 2.0 fusion.54
  230.5 4.0 slice.174
  234.5 3.5 copy.51
  238.0 2.0 fusion.17
  240.0 2.6 copy-done
  244.4 2.5 collective-permute-start.5
  251.5 20.5 %collective-permute-done.5 = f32[2,16,72,128]{3,2,1,0:T(8,128)S(1)} collective-permute-done((f32[2,16,72,128]{3,2,1,0:T(8,128)}, f32[2,16,72,128]{3,2,1,0:T(8,128)S(1)}, u32[]{:S(2)}, u32[]{:S(2)}) %collective-permute-start.5) | collective-permute-done | bytes 1179680 | tf_op jit(solution)/shard_map/ppermute | solution.py:43
  272.2 3.4 add_select_fusion.2
  280.1 48.2 %collective-permute-done.6 = f32[2,16,72,128]{3,2,1,0:T(8,128)S(1)} collective-permute-done((f32[2,16,72,128]{3,2,1,0:T(8,128)S(1)}, f32[2,16,72,128]{3,2,1,0:T(8,128)S(1)}, u32[]{:S(2)}, u32[]{:S(2)}) %collective-permute-start.6) | collective-permute-done | bytes 1179680 | tf_op jit(solution)/shard_map/ppermute | solution.py:43
  332.6 2.4 collective-permute-start.9
  335.5 8.8 %fusion = f32[6,2,16,64,128]{4,3,2,1,0:T(8,128)} fusion(bf16[6,128,2,16,64]{1,4,3,2,0:T(8,128)(2,1)S(1)} %bitcast.147, f32[6,2,16,128]{3,2,1,0:T(8,128)S(1)} %copy-done.15, f32[6,2,16,128]{3,2,1,0:T(8,128)S(1)} %copy.55, f32[6,2,128,128]{3,2,1,0:T(8,128)S(1)} %fusion.39, pred[128,128]{1,0:T(8,128)(4,1)S(1)} %iota_compare_fusion), kind=kOutput, calls=%fused_computation.4 | convolution fusion | flops 421527552 | bytes 10436608 | tf_op jit(solution)/shard_map/qghij,qjghp->qighp/dot_general | solution.py:145
  344.3 18.4 %collective-permute-done.10 = f32[2,16,72,128]{3,2,1,0:T(8,128)S(1)} collective-permute-done((f32[2,16,72,128]{3,2,1,0:T(8,128)S(1)}, f32[2,16,72,128]{3,2,1,0:T(8,128)S(1)}, u32[]{:S(2)}, u32[]{:S(2)}) %collective-permute-start.10) | collective-permute-done | bytes 1179680 | tf_op jit(solution)/shard_map/ppermute | solution.py:43
  363.1 22.1 %collective-permute-done.9 = f32[2,16,72,128]{3,2,1,0:T(8,128)S(1)} collective-permute-done((f32[2,16,72,128]{3,2,1,0:T(8,128)S(1)}, f32[2,16,72,128]{3,2,1,0:T(8,128)S(1)}, u32[]{:S(2)}, u32[]{:S(2)}) %collective-permute-start.9) | collective-permute-done | bytes 1179680 | tf_op jit(solution)/shard_map/ppermute | solution.py:43
  385.4 2.3 fusion.26
  387.8 4.4 %multiply_reduce_fusion = (f32[6,128,2]{1,2,0:T(2,128)S(1)}, f32[6,128,2,16,64]{1,4,3,2,0:T(8,128)S(1)}) fusion(bf16[6,128,2,128]{3,1,0,2:T(8,128)(2,1)S(1)} %copy-done.11, f32[6,2,16,64,128]{4,3,2,1,0:T(8,128)S(1)} %copy-done.5, f32[2,16,64,128]{3,2,1,0:T(8,128)S(1)} %fusion.26, f32[6,2,16]{2,1,0:T(2,128)S(1)} %copy-done.24, ...), kind=kOutput, calls=%fused_computation.14 | convolution fusion | flops 418380288 | bytes 23567232 | tf_op jit(solution)/shard_map/qign,qghpn->qighp/dot_general | solution.py:150
  392.1 5.6 %copy.62 = f32[6,128,2,16,64]{1,0,4,3,2:T(8,128)S(1)} copy(f32[6,128,2,16,64]{1,4,3,2,0:T(8,128)S(1)} %get-tuple-element.42) | data formatting | bytes 12582912 | tf_op jit(solution)/shard_map/add | solution.py:156
  398.8 2.9 copy.63
  (132 shorter events, 32.3 us)
Async XLA Ops:
  6.5 30.4 %copy-start.14 = (bf16[768,1024]{1,0:T(8,128)(2,1)S(1)}, bf16[768,1024]{1,0:T(8,128)(2,1)}, u32[]{:S(2)}) copy-start(bf16[768,1024]{1,0:T(8,128)(2,1)} %param.8) | copy-start | bytes 4718596
  6.5 163.4 %all-gather.2.cloned.1.call-start = ((), (), s32[]{:S(2)}) async-start(), calls=%async_computation | async-start | bytes 22560768 | tf_op jit(solution)/shard_map/all_gather | solution.py:90
  6.5 17.1 %collective-permute-start.3 = (bf16[128,2,1296]{0,2,1:T(8,128)(2,1)}, bf16[128,2,1296]{0,2,1:T(8,128)(2,1)}, u32[]{:S(2)}, u32[]{:S(2)}) collective-permute-start(bf16[128,2,1296]{0,2,1:T(8,128)(2,1)} %bitcast.153), channel_id=1, source_target_pairs={{0,4},{4,0},{1,5},{5,1},{2,6},{6,2},{3,7},{7,3},{8,12},{12,8},{9,1... | collective-permute-start | bytes 1990664 | tf_op jit(solution)/shard_map/ppermute | solution.py:83
  9.8 28.5 %copy-start.16 = (f32[2,4,1280]{2,1,0:T(4,128)S(1)}, f32[2,4,1280]{2,1,0:T(4,128)}, u32[]{:S(2)}) copy-start(f32[2,4,1280]{2,1,0:T(4,128)} %param.10) | copy-start | bytes 122884
  26.0 37.8 %collective-permute-start = (bf16[768,1024]{1,0:T(8,128)(2,1)}, bf16[768,1024]{1,0:T(8,128)(2,1)}, u32[]{:S(2)}, u32[]{:S(2)}) collective-permute-start(bf16[768,1024]{1,0:T(8,128)(2,1)} %param.8), channel_id=1, source_target_pairs={{0,1},{1,2},{2,3},{3,0},{4,5},{5,6},{6,7},{7,4},{8,9},{9,10},{10,1... | collective-permute-start | bytes 4718600 | tf_op jit(solution)/shard_map/ppermute | solution.py:170
  26.1 40.4 %collective-permute-start.1 = (bf16[768,1024]{1,0:T(8,128)(2,1)}, bf16[768,1024]{1,0:T(8,128)(2,1)}, u32[]{:S(2)}, u32[]{:S(2)}) collective-permute-start(bf16[768,1024]{1,0:T(8,128)(2,1)} %param.8), channel_id=1, source_target_pairs={{0,2},{1,3},{2,0},{3,1},{4,6},{5,7},{6,4},{7,5},{8,10},{9,11},{10,... | collective-permute-start | bytes 4718600 | tf_op jit(solution)/shard_map/ppermute | solution.py:170
  29.9 68.1 %collective-permute-start.2 = (bf16[768,1024]{1,0:T(8,128)(2,1)}, bf16[768,1024]{1,0:T(8,128)(2,1)}, u32[]{:S(2)}, u32[]{:S(2)}) collective-permute-start(bf16[768,1024]{1,0:T(8,128)(2,1)} %param.8), channel_id=1, source_target_pairs={{0,3},{1,0},{2,1},{3,2},{4,7},{5,4},{6,5},{7,6},{8,11},{9,8},{10,9... | collective-permute-start | bytes 4718600 | tf_op jit(solution)/shard_map/ppermute | solution.py:170
  100.8 91.8 %copy-start.26 = (f32[2,16]{1,0:T(2,128)S(1)}, f32[2,16]{1,0:T(2,128)}, u32[]{:S(2)}) copy-start(f32[2,16]{1,0:T(2,128)} %param.12) | copy-start | bytes 388
  193.5 12.9 %copy-start.6 = (f32[6,128,2,16]{3,2,1,0:T(2,128)}, f32[6,128,2,16]{3,2,1,0:T(2,128)S(1)}, u32[]{:S(2)}) copy-start(f32[6,128,2,16]{3,2,1,0:T(2,128)S(1)} %fusion.57) | copy-start | bytes 294916
  195.5 11.8 %collective-permute-start.4 = (bf16[3,2,1280]{2,1,0:T(2,128)(2,1)S(1)}, bf16[3,2,1280]{2,1,0:T(2,128)(2,1)S(1)}, u32[]{:S(2)}, u32[]{:S(2)}) collective-permute-start(bf16[3,2,1280]{2,1,0:T(2,128)(2,1)S(1)} %copy.48), channel_id=1, source_target_pairs={{0,4},{4,8},{8,12},{12,16},{16,20},{20,24},{24,28},{28,32},{32,36}... | collective-permute-start | bytes 46088 | tf_op jit(solution)/shard_map/ppermute | solution.py:22
  202.1 19.9 %copy-start.23 = (f32[6,2,16]{2,1,0:T(2,128)}, f32[6,2,16]{2,1,0:T(2,128)S(1)}, u32[]{:S(2)}) copy-start(f32[6,2,16]{2,1,0:T(2,128)S(1)} %get-tuple-element.30) | copy-start | bytes 2308
  240.0 9.4 %copy-start.13 = (f32[6,128,2,16]{1,0,3,2:T(8,128)S(1)}, f32[6,128,2,16]{1,0,3,2:T(8,128)}, u32[]{:S(2)}) copy-start(f32[6,128,2,16]{1,0,3,2:T(8,128)} %copy-done.12) | copy-start | bytes 294916
  240.0 10.1 %copy-start.25 = (f32[2,16,1,1]{1,0,3,2:T(2,128)S(1)}, f32[2,16,1,1]{1,0,3,2:T(2,128)}, u32[]{:S(2)}) copy-start(f32[2,16,1,1]{1,0,3,2:T(2,128)} %get-tuple-element.31) | copy-start | bytes 388
  242.6 29.6 %copy-start.18 = (f32[2,16]{1,0:T(2,128)S(1)}, f32[2,16]{1,0:T(2,128)}, u32[]{:S(2)}) copy-start(f32[2,16]{1,0:T(2,128)} %get-tuple-element.36) | copy-start | bytes 388
  244.4 27.6 %collective-permute-start.5 = (f32[2,16,72,128]{3,2,1,0:T(8,128)}, f32[2,16,72,128]{3,2,1,0:T(8,128)S(1)}, u32[]{:S(2)}, u32[]{:S(2)}) collective-permute-start(f32[2,16,72,128]{3,2,1,0:T(8,128)} %pad_maximum_fusion.1), channel_id=1, source_target_pairs={{0,4},{4,0},{1,5},{5,1},{2,6},{6,2},{3,7},{7,3},{8,12},{12,8},{9,1... | collective-permute-start | bytes 3538952 | tf_op jit(solution)/shard_map/ppermute | solution.py:43
  248.0 31.1 %slice-start = ((s8[6291456]{0:T(1024)(128)(4,1)}), s8[2097152]{0:T(1024)(128)(4,1)S(1)}, s32[]{:S(2)}) async-start(s8[6291456]{0:T(1024)(128)(4,1)} %bitcast.143), calls=%async_computation.1 | async-start | bytes 4194304
  251.5 27.7 %copy-start.3 = (f32[6,2,16,64,128]{4,3,2,1,0:T(8,128)S(1)}, f32[6,2,16,64,128]{4,3,2,1,0:T(8,128)}, u32[]{:S(2)}) copy-start(f32[6,2,16,64,128]{4,3,2,1,0:T(8,128)} %broadcast_dynamic-update-slice_fusion) | copy-start | bytes 18874372
  275.9 52.5 %collective-permute-start.6 = (f32[2,16,72,128]{3,2,1,0:T(8,128)S(1)}, f32[2,16,72,128]{3,2,1,0:T(8,128)S(1)}, u32[]{:S(2)}, u32[]{:S(2)}) collective-permute-start(f32[2,16,72,128]{3,2,1,0:T(8,128)S(1)} %pad_maximum_fusion.2), channel_id=1, source_target_pairs={{0,24},{8,0},{16,8},{24,16},{1,25},{9,1},{17,9},{25,17},{2,26},{10... | collective-permute-start | bytes 3538952 | tf_op jit(solution)/shard_map/ppermute | solution.py:43
  276.0 52.4 %collective-permute-start.7 = (f32[2,16,72,128]{3,2,1,0:T(8,128)S(1)}, f32[2,16,72,128]{3,2,1,0:T(8,128)S(1)}, u32[]{:S(2)}, u32[]{:S(2)}) collective-permute-start(f32[2,16,72,128]{3,2,1,0:T(8,128)S(1)} %pad_maximum_fusion.2), channel_id=1, source_target_pairs={{0,16},{8,24},{16,0},{24,8},{1,17},{9,25},{17,1},{25,9},{2,18},{10... | collective-permute-start | bytes 3538952 | tf_op jit(solution)/shard_map/ppermute | solution.py:43
  277.4 51.5 %collective-permute-start.8 = (f32[2,16,72,128]{3,2,1,0:T(8,128)S(1)}, f32[2,16,72,128]{3,2,1,0:T(8,128)S(1)}, u32[]{:S(2)}, u32[]{:S(2)}) collective-permute-start(f32[2,16,72,128]{3,2,1,0:T(8,128)S(1)} %pad_maximum_fusion.2), channel_id=1, source_target_pairs={{0,8},{8,16},{16,24},{24,0},{1,9},{9,17},{17,25},{25,1},{2,10},{10... | collective-permute-start | bytes 3538952 | tf_op jit(solution)/shard_map/ppermute | solution.py:43
  280.1 55.0 %copy-start.9 = (bf16[6,128,2,128]{3,1,0,2:T(8,128)(2,1)S(1)}, bf16[6,128,2,128]{3,1,0,2:T(8,128)(2,1)}, u32[]{:S(2)}) copy-start(bf16[6,128,2,128]{3,1,0,2:T(8,128)(2,1)} %copy-done.8) | copy-start | bytes 1179652
  280.1 55.0 %copy-start.10 = (bf16[6,128,2,128]{3,1,0,2:T(8,128)(2,1)S(1)}, bf16[6,128,2,128]{3,1,0,2:T(8,128)(2,1)}, u32[]{:S(2)}) copy-start(bf16[6,128,2,128]{3,1,0,2:T(8,128)(2,1)} %get-tuple-element.20) | copy-start | bytes 1179652
  280.1 55.4 %copy-start.2 = (bf16[6,128,2,1024]{1,3,2,0:T(8,128)(2,1)S(1)}, bf16[6,128,2,1024]{1,3,2,0:T(8,128)(2,1)}, u32[]{:S(2)}) copy-start(bf16[6,128,2,1024]{1,3,2,0:T(8,128)(2,1)} %copy-done.1) | copy-start | bytes 9437188
  280.1 55.4 %copy-start.15 = (f32[6,2,16,128]{3,2,1,0:T(8,128)S(1)}, f32[6,2,16,128]{3,2,1,0:T(8,128)}, u32[]{:S(2)}) copy-start(f32[6,2,16,128]{3,2,1,0:T(8,128)} %copy.57) | copy-start | bytes 294916
  330.4 32.4 %collective-permute-start.10 = (f32[2,16,72,128]{3,2,1,0:T(8,128)S(1)}, f32[2,16,72,128]{3,2,1,0:T(8,128)S(1)}, u32[]{:S(2)}, u32[]{:S(2)}) collective-permute-start(f32[2,16,72,128]{3,2,1,0:T(8,128)S(1)} %pad_maximum_fusion.3), channel_id=1, source_target_pairs={{0,64},{32,96},{1,65},{33,97},{2,66},{34,98},{3,67},{35,99},{4,68}... | collective-permute-start | bytes 3538952 | tf_op jit(solution)/shard_map/ppermute | solution.py:43
  331.9 12.5 %copy-start.4 = (f32[6,2,16,64,128]{4,3,2,1,0:T(8,128)}, f32[6,2,16,64,128]{4,3,2,1,0:T(8,128)S(1)}, u32[]{:S(2)}) copy-start(f32[6,2,16,64,128]{4,3,2,1,0:T(8,128)S(1)} %add_dynamic-update-slice_fusion) | copy-start | bytes 18874372
  331.9 31.0 %collective-permute-start.11 = (f32[2,16,72,128]{3,2,1,0:T(8,128)S(1)}, f32[2,16,72,128]{3,2,1,0:T(8,128)S(1)}, u32[]{:S(2)}, u32[]{:S(2)}) collective-permute-start(f32[2,16,72,128]{3,2,1,0:T(8,128)S(1)} %pad_maximum_fusion.3), channel_id=1, source_target_pairs={{0,96},{1,97},{2,98},{3,99},{4,100},{5,101},{6,102},{7,103},{8,104... | collective-permute-start | bytes 3538952 | tf_op jit(solution)/shard_map/ppermute | solution.py:43
  332.6 52.6 %collective-permute-start.9 = (f32[2,16,72,128]{3,2,1,0:T(8,128)S(1)}, f32[2,16,72,128]{3,2,1,0:T(8,128)S(1)}, u32[]{:S(2)}, u32[]{:S(2)}) collective-permute-start(f32[2,16,72,128]{3,2,1,0:T(8,128)S(1)} %pad_maximum_fusion.3), channel_id=1, source_target_pairs={{0,32},{32,64},{64,96},{1,33},{33,65},{65,97},{2,34},{34,66},{66,9... | collective-permute-start | bytes 3538952 | tf_op jit(solution)/shard_map/ppermute | solution.py:43
  344.3 43.4 %copy-start.11 = (bf16[6,128,2,128]{3,1,0,2:T(8,128)(2,1)S(1)}, bf16[6,128,2,128]{3,1,0,2:T(8,128)(2,1)}, u32[]{:S(2)}) copy-start(bf16[6,128,2,128]{3,1,0,2:T(8,128)(2,1)} %get-tuple-element.20) | copy-start | bytes 1179652
  344.3 43.4 %copy-start.24 = (f32[6,2,16]{2,1,0:T(2,128)S(1)}, f32[6,2,16]{2,1,0:T(2,128)}, u32[]{:S(2)}) copy-start(f32[6,2,16]{2,1,0:T(2,128)} %copy-done.23) | copy-start | bytes 2308
  344.3 43.4 %copy-start.27 = (f32[2,16]{1,0:T(2,128)S(1)}, f32[2,16]{1,0:T(2,128)}, u32[]{:S(2)}) copy-start(f32[2,16]{1,0:T(2,128)} %param.14) | copy-start | bytes 388
  362.7 25.0 %copy-start.5 = (f32[6,2,16,64,128]{4,3,2,1,0:T(8,128)S(1)}, f32[6,2,16,64,128]{4,3,2,1,0:T(8,128)}, u32[]{:S(2)}) copy-start(f32[6,2,16,64,128]{4,3,2,1,0:T(8,128)} %copy-done.4) | copy-start | bytes 18874372
  (11 other events, 54.0 us)
Sparse Core Ops, SparseCore 0:
  26.1 143.7 all-gather.1

commit v6 on v5

--- a/solution.py
+++ b/solution.py
@@ -69,7 +69,7 @@
     return result[1]
 
 
-def mix_groups(gathered, w_in, conv_w, conv_b, dt_bias, a_log, d_skip, norm_gain):
+def mix_groups(gathered, w_in, conv_w, conv_b, dt_bias, a_log, d_skip, norm_gain, after):
     groups = w_in.shape[0]
     row_count = gathered.shape[0]
     rows_first = jnp.transpose(w_in, (1, 0, 2))
@@ -90,6 +90,8 @@
         full_w = lax.all_gather(pair_w, SEQ[:2], axis=0, tiled=True)
     else:
         full_w = lax.all_gather(rows_first, SEQ, axis=0, tiled=True)
+    if after is not None:
+        full_w, _ = lax.optimization_barrier((full_w, after))
     projected = jnp.einsum(
         "td,dgc->tgc",
         gathered,
@@ -157,7 +159,7 @@
     flat_act = activity.reshape(row_count, groups, GW)
     inv_rms = lax.rsqrt(jnp.mean(flat_act * flat_act, axis=-1, keepdims=True) + epsilon)
     normed = (flat_act * inv_rms * norm_gain[None]).astype(jnp.bfloat16)
-    return normed.reshape(row_count, groups * GW)
+    return normed.reshape(row_count, groups * GW), state_now
 
 
 def per_device(tokens, w_in, conv_w, conv_b, dt_bias, a_log, d_skip, norm_gain):
@@ -174,7 +176,16 @@
             piece = tokens
         source = (place - distance) % size
         gathered = lax.dynamic_update_slice(gathered, piece, (0, source * width))
-    return mix_groups(gathered, w_in, conv_w, conv_b, dt_bias, a_log, d_skip, norm_gain)
+    outputs = []
+    after = None
+    for g in range(w_in.shape[0]):
+        one = slice(g, g + 1)
+        normed, after = mix_groups(
+            gathered, w_in[one], conv_w[one], conv_b[one], dt_bias[one],
+            a_log[one], d_skip[one], norm_gain[one], after,
+        )
+        outputs.append(normed)
+    return jnp.concatenate(outputs, axis=1)
 
 
 def split_mesh(mesh):

time: 413 us -> 405 us (0.981)
  waiting for transfers between devices: 247 us -> 170 us
  other arithmetic: 29.7 us -> 56.4 us
  starting transfers between devices: 22.6 us -> 37 us
  local copies, waits for them, and re-layouts: 57 us -> 69.4 us
  matrix products: 38.2 us -> 50.1 us
    ppermute x7 -> x14, waiting for transfers between devices: 110 us -> 56 us  [gather_level(): got = lax.ppermute(packed, axis, route)]
    all_gather x1 -> x2, waiting for transfers between devices: 69.1 us -> 45.6 us  [mix_groups(): full_w = lax.all_gather(pair_w, SEQ[:2], axis=0, tiled=True)]
    ppermute x7 -> x14, starting transfers between devices: 10.3 us -> 20.5 us  [gather_level(): got = lax.ppermute(packed, axis, route)]
    convert_element_type x0 -> x2, other arithmetic: none -> 6.36 us  [mix_groups(): partial_y = partial_y + d_skip[None, None, :, :, None] * x_all]
    unnamed x8 -> x11, other arithmetic: 0.89 us -> 7.19 us
    slice x2 -> x12, local copies, waits for them, and re-layouts: 0.41 us -> 5.95 us  [gather_level(): received.append((got[:, :, -8, 0], got[:, :, :-8]))]
    ppermute x1 -> x2, waiting for transfers between devices: 0.01 us -> 4.93 us  [shifted(): return lax.ppermute(block, axis, route)]
    unnamed x66 -> x128, local copies, waits for them, and re-layouts: 4.92 us -> 9.65 us
  transfers between devices with their start and end apart: 13 -> 23, of which waited for: 9 -> 11; matrix products, arithmetic and copies ran while one was open for 9% -> 34% of each run, Pallas kernels for 0% -> 0%
where the time goes in v6:
time: 405 us; the launch traced here: 397 us
  waiting for transfers between devices  170 us (42%)
  local copies, waits for them, and re-layouts  69.4 us (17%)
  other arithmetic  56.4 us (14%)
  matrix products  50.1 us (12%)
  starting transfers between devices  37 us (9%)
  between operations  14.8 us (4%)
    ppermute x14, waiting for transfers between devices, gather_level(): got = lax.ppermute(packed, axis, route)  56 us
    ppermute x3, waiting for transfers between devices, per_device(): lax.ppermute(tokens, 'chan', [(i, (i + distance) % size) for i in range(s...  49.5 us
    all_gather x2, waiting for transfers between devices, mix_groups(): full_w = lax.all_gather(pair_w, SEQ[:2], axis=0, tiled=True)  45.6 us
    dot_general x2, matrix products, mix_groups(): jnp.einsum('td,dgc->tgc', gathered, full_w, preferred_element_type=jnp.fl...  26.1 us
    ppermute x14, starting transfers between devices, gather_level(): got = lax.ppermute(packed, axis, route)  20.5 us
    convert_element_type x2, other arithmetic, mix_groups(): inputs = jax.nn.silu(pre_act).astype(jnp.bfloat16)  15.4 us
    ppermute x2, waiting for transfers between devices, mix_groups(): lax.ppermute(rows_first, SEQ[2], [(i, (i + distance) % pair) for i in ran...  13.7 us
    dot_general x2, matrix products, mix_groups(): jnp.einsum('qghij,qjghp->qighp', weights, x_all, preferred_element_type=j...  10.8 us
  transfers between devices with their start and end apart: 23, of which 11 were waited for; matrix products, arithmetic and copies ran while one was open for 34% of the time, Pallas kernels for 0%

profile of v6, /device:TPU:22, one launch (start us, length us, event | category | flops | bytes accessed | tf_op | source)
XLA Modules:
  0.0 397.4 jit_solution(4341952973254259718)
XLA Ops:
  10.8 6.7 %collective-permute-done.3 = bf16[128,1,1296]{0,2,1:T(8,128)(2,1)S(1)} collective-permute-done((bf16[128,1,1296]{0,2,1:T(8,128)(2,1)S(1)}, bf16[128,1,1296]{0,2,1:T(8,128)(2,1)S(1)}, u32[]{:S(2)}, u32[]{:S(2)}) %collective-permute-start.3) | collective-permute-done | bytes 331808 | tf_op jit(solution)/shard_map/ppermute | solution.py:83
  20.5 7.0 %collective-permute-done.12 = bf16[128,1,1296]{0,2,1:T(8,128)(2,1)S(1)} collective-permute-done((bf16[128,1,1296]{0,2,1:T(8,128)(2,1)S(1)}, bf16[128,1,1296]{0,2,1:T(8,128)(2,1)S(1)}, u32[]{:S(2)}, u32[]{:S(2)}) %collective-permute-start.12) | collective-permute-done | bytes 331808 | tf_op jit(solution)/shard_map/ppermute | solution.py:83
  28.5 3.6 collective-permute-start.1
  32.1 2.9 collective-permute-start.2
  39.6 3.5 broadcast_in_dim.42
  46.7 19.7 %collective-permute-done = bf16[768,1024]{1,0:T(8,128)(2,1)} collective-permute-done((bf16[768,1024]{1,0:T(8,128)(2,1)}, bf16[768,1024]{1,0:T(8,128)(2,1)}, u32[]{:S(2)}, u32[]{:S(2)}) %collective-permute-start) | collective-permute-done | bytes 1572896 | tf_op jit(solution)/shard_map/ppermute | solution.py:172
  66.4 2.7 constant_dynamic-update-slice_fusion.26
  70.4 29.8 %collective-permute-done.2 = bf16[768,1024]{1,0:T(8,128)(2,1)S(1)} collective-permute-done((bf16[768,1024]{1,0:T(8,128)(2,1)}, bf16[768,1024]{1,0:T(8,128)(2,1)S(1)}, u32[]{:S(2)}, u32[]{:S(2)}) %collective-permute-start.2) | collective-permute-done | bytes 1572896 | tf_op jit(solution)/shard_map/ppermute | solution.py:172
  101.6 6.7 %all-gather.3.cloned.1.call-done = bf16[4096,1,1296]{0,2,1:T(8,128)(2,1)} async-done(((bf16[256,1,1296]{0,2,1:T(8,128)(2,1)}), bf16[4096,1,1296]{0,2,1:T(8,128)(2,1)}) %all-gather.3.cloned.1.call-update) | async-done | bytes 10616848 | tf_op jit(solution)/shard_map/all_gather | solution.py:90
  108.3 13.0 %fusion.101 = (bf16[768,1,1296]{0,2,1:T(8,128)(2,1)S(1)}, f32[768,1,1296]{0,2,1:T(8,128)S(1)}) fusion(bf16[768,4096]{1,0:T(8,128)(2,1)} %constant_dynamic-update-slice_fusion.24, bf16[4096,1,1296]{0,2,1:T(8,128)(2,1)} %all-gather.3.cloned.1.call-done), kind=kOutput, calls=%fused_computation.281 | convolution fusion | flops 8154722304 | bytes 22880256 | tf_op jit(solution)/shard_map/td,dgc->tgc/dot_general | solution.py:95
  121.7 3.6 collective-permute-start.4
  134.4 4.5 %collective-permute-done.4 = bf16[3,1,1280]{0,2,1:T(8,128)(2,1)S(1)} collective-permute-done((bf16[3,1,1280]{0,2,1:T(8,128)(2,1)S(1)}, bf16[3,1,1280]{0,2,1:T(8,128)(2,1)S(1)}, u32[]{:S(2)}, u32[]{:S(2)}) %collective-permute-start.4) | collective-permute-done | bytes 7712 | tf_op jit(solution)/shard_map/ppermute | solution.py:22
  138.9 6.1 %multiply_convert_fusion.3 = bf16[768,1,1280]{0,2,1:T(8,128)(2,1)} fusion(bf16[768,1,1280]{0,2,1:T(8,128)(2,1)S(1)} %slice.449, bf16[3,1,1280]{0,2,1:T(8,128)(2,1)S(1)} %collective-permute-done.4, f32[1280]{0:T(1024)} %get-tuple-element.9, f32[1280]{0:T(1024)} %get-tuple-element.10, f32[1280]{0:T(1024)} %get-tuple-element.11, f32[1280]{0:T(1024)} %get-tuple-element.12, ...), kind=kLoop, calls=%fused_computation.7 | loop fusion | flops 25559040 | bytes 3965440 | tf_op jit(solution)/shard_map/convert_element_type | solution.py:108
  145.1 4.0 copy.109
  149.0 3.1 slice_convert_fusion.1
  152.2 2.6 copy.110
  164.0 38.9 %all-gather.5.cloned.1.call-done = bf16[4096,1,1296]{0,2,1:T(8,128)(2,1)} async-done(((bf16[256,1,1296]{0,2,1:T(8,128)(2,1)}), bf16[4096,1,1296]{0,2,1:T(8,128)(2,1)}) %all-gather.5.cloned.1.call-update) | async-done | bytes 10616848 | tf_op jit(solution)/shard_map/all_gather | solution.py:90
  202.8 13.0 %fusion.102 = (bf16[768,1,1296]{0,2,1:T(8,128)(2,1)S(1)}, f32[768,1,1296]{0,2,1:T(8,128)S(1)}) fusion(bf16[768,4096]{1,0:T(8,128)(2,1)} %constant_dynamic-update-slice_fusion.24, bf16[4096,1,1296]{0,2,1:T(8,128)(2,1)} %all-gather.5.cloned.1.call-done), kind=kOutput, calls=%fused_computation.282 | convolution fusion | flops 8154722304 | bytes 22880256 | tf_op jit(solution)/shard_map/td,dgc->tgc/dot_general | solution.py:95
  229.6 2.5 collective-permute-start.13
  236.5 5.4 %fusion.10 = f32[6,16,64,128]{3,2,1,0:T(8,128)} fusion(bf16[6,128,16,64]{1,3,2,0:T(8,128)(2,1)} %bitcast.379, f32[6,16,128]{2,1,0:T(8,128)} %copy.114, f32[6,16,128]{2,1,0:T(8,128)} %copy.112, f32[6,128,128]{2,1,0:T(8,128)} %fusion.67, pred[128,128]{1,0:T(8,128)(4,1)} %iota_compare_fusion), kind=kOutput, calls=%fused_computation.10 | convolution fusion | flops 210763776 | bytes 5226496 | tf_op jit(solution)/shard_map/qghij,qjghp->qighp/dot_general | solution.py:147
  248.7 9.2 %multiply_convert_fusion.2 = bf16[768,1,1280]{0,2,1:T(8,128)(2,1)S(1)} fusion(bf16[768,1,1280]{0,2,1:T(8,128)(2,1)} %slice.486, bf16[3,1,1280]{0,2,1:T(8,128)(2,1)} %collective-permute-done.13, f32[1280]{0:T(1024)} %get-tuple-element.13, f32[1280]{0:T(1024)} %get-tuple-element.14, f32[1280]{0:T(1024)} %get-tuple-element.8, f32[1280]{0:T(1024)} %get-tuple-element.7, ...), kind=kLoop, calls=%fused_computation.6 | loop fusion | flops 25559040 | bytes 3965440 | tf_op jit(solution)/shard_map/convert_element_type | solution.py:108
  260.2 3.2 slice_convert_fusion
  263.4 2.6 copy.126
  269.8 3.2 collective-permute-start.14
  277.6 5.4 %fusion.11 = f32[6,16,64,128]{3,2,1,0:T(8,128)} fusion(bf16[6,128,16,64]{1,3,2,0:T(8,128)(2,1)} %bitcast.381, f32[6,16,128]{2,1,0:T(8,128)} %copy.130, f32[6,16,128]{2,1,0:T(8,128)} %copy.128, f32[6,128,128]{2,1,0:T(8,128)S(1)} %fusion.64, pred[128,128]{1,0:T(8,128)(4,1)} %iota_compare_fusion), kind=kOutput, calls=%fused_computation.11 | convolution fusion | flops 210763776 | bytes 5226496 | tf_op jit(solution)/shard_map/qghij,qjghp->qighp/dot_general | solution.py:147
  286.4 3.2 collective-permute-start.8
  296.0 20.7 %collective-permute-done.6 = f32[1,16,72,128]{3,2,1,0:T(8,128)S(1)} collective-permute-done((f32[1,16,72,128]{3,2,1,0:T(8,128)}, f32[1,16,72,128]{3,2,1,0:T(8,128)S(1)}, u32[]{:S(2)}, u32[]{:S(2)}) %collective-permute-start.6) | collective-permute-done | bytes 589856 | tf_op jit(solution)/shard_map/ppermute | solution.py:43
  324.0 15.0 %collective-permute-done.15 = f32[1,16,72,128]{3,2,1,0:T(8,128)S(1)} collective-permute-done((f32[1,16,72,128]{3,2,1,0:T(8,128)}, f32[1,16,72,128]{3,2,1,0:T(8,128)S(1)}, u32[]{:S(2)}, u32[]{:S(2)}) %collective-permute-start.15) | collective-permute-done | bytes 589856 | tf_op jit(solution)/shard_map/ppermute | solution.py:43
  348.5 20.2 %collective-permute-done.9 = f32[1,16,72,128]{3,2,1,0:T(8,128)} collective-permute-done((f32[1,16,72,128]{3,2,1,0:T(8,128)}, f32[1,16,72,128]{3,2,1,0:T(8,128)}, u32[]{:S(2)}, u32[]{:S(2)}) %collective-permute-start.9) | collective-permute-done | bytes 589856 | tf_op jit(solution)/shard_map/ppermute | solution.py:43
  369.7 2.9 fusion.55
  372.7 3.1 multiply_reduce_fusion.1
  387.3 2.9 copy.141
  (276 shorter events, 111.5 us)
Async XLA Ops:
  6.5 13.9 %copy-start.10 = (bf16[2,128,1296]{1,2,0:T(8,128)(2,1)S(1)}, bf16[2,128,1296]{1,2,0:T(8,128)(2,1)}, u32[]{:S(2)}) copy-start(bf16[2,128,1296]{1,2,0:T(8,128)(2,1)} %param.9) | copy-start | bytes 1990660
  6.5 28.4 %copy-start.26 = (f32[2,1280]{1,0:T(2,128)S(1)}, f32[2,1280]{1,0:T(2,128)}, u32[]{:S(2)}) copy-start(f32[2,1280]{1,0:T(2,128)} %param.11) | copy-start | bytes 30724
  6.5 29.1 %copy-start.21 = (f32[2,4,1280]{2,1,0:T(4,128)S(1)}, f32[2,4,1280]{2,1,0:T(4,128)}, u32[]{:S(2)}) copy-start(f32[2,4,1280]{2,1,0:T(4,128)} %param.10) | copy-start | bytes 122884
  6.5 101.7 %all-gather.3.cloned.1.call-start = ((), (), s32[]{:S(2)}) async-start(), calls=%async_computation | async-start | bytes 11280384 | tf_op jit(solution)/shard_map/all_gather | solution.py:90
  7.7 9.8 %collective-permute-start.3 = (bf16[128,1,1296]{0,2,1:T(8,128)(2,1)S(1)}, bf16[128,1,1296]{0,2,1:T(8,128)(2,1)S(1)}, u32[]{:S(2)}, u32[]{:S(2)}) collective-permute-start(bf16[128,1,1296]{0,2,1:T(8,128)(2,1)S(1)} %get-tuple-element.39), channel_id=1, source_target_pairs={{0,4},{4,0},{1,5},{5,1},{2,6},{6,2},{3,7},{7,3},{8,12},{12,8},{9,1... | collective-permute-start | bytes 995336 | tf_op jit(solution)/shard_map/ppermute | solution.py:83
  18.5 184.3 %all-gather.5.cloned.1.call-start = ((), (), s32[]{:S(2)}) async-start(), calls=%async_computation.1 | async-start | bytes 11280384 | tf_op jit(solution)/shard_map/all_gather | solution.py:90
  18.5 8.9 %collective-permute-start.12 = (bf16[128,1,1296]{0,2,1:T(8,128)(2,1)S(1)}, bf16[128,1,1296]{0,2,1:T(8,128)(2,1)S(1)}, u32[]{:S(2)}, u32[]{:S(2)}) collective-permute-start(bf16[128,1,1296]{0,2,1:T(8,128)(2,1)S(1)} %get-tuple-element.40), channel_id=1, source_target_pairs={{0,4},{4,0},{1,5},{5,1},{2,6},{6,2},{3,7},{7,3},{8,12},{12,8},{9,1... | collective-permute-start | bytes 995336 | tf_op jit(solution)/shard_map/ppermute | solution.py:83
  28.4 38.0 %collective-permute-start = (bf16[768,1024]{1,0:T(8,128)(2,1)}, bf16[768,1024]{1,0:T(8,128)(2,1)}, u32[]{:S(2)}, u32[]{:S(2)}) collective-permute-start(bf16[768,1024]{1,0:T(8,128)(2,1)} %param.8), channel_id=1, source_target_pairs={{0,1},{1,2},{2,3},{3,0},{4,5},{5,6},{6,7},{7,4},{8,9},{9,10},{10,1... | collective-permute-start | bytes 4718600 | tf_op jit(solution)/shard_map/ppermute | solution.py:172
  28.5 40.6 %collective-permute-start.1 = (bf16[768,1024]{1,0:T(8,128)(2,1)}, bf16[768,1024]{1,0:T(8,128)(2,1)S(1)}, u32[]{:S(2)}, u32[]{:S(2)}) collective-permute-start(bf16[768,1024]{1,0:T(8,128)(2,1)} %param.8), channel_id=1, source_target_pairs={{0,2},{1,3},{2,0},{3,1},{4,6},{5,7},{6,4},{7,5},{8,10},{9,11},{10,... | collective-permute-start | bytes 4718600 | tf_op jit(solution)/shard_map/ppermute | solution.py:172
  32.1 68.1 %collective-permute-start.2 = (bf16[768,1024]{1,0:T(8,128)(2,1)}, bf16[768,1024]{1,0:T(8,128)(2,1)S(1)}, u32[]{:S(2)}, u32[]{:S(2)}) collective-permute-start(bf16[768,1024]{1,0:T(8,128)(2,1)} %param.8), channel_id=1, source_target_pairs={{0,3},{1,0},{2,1},{3,2},{4,7},{5,4},{6,5},{7,6},{8,11},{9,8},{10,9... | collective-permute-start | bytes 4718600 | tf_op jit(solution)/shard_map/ppermute | solution.py:172
  121.7 17.3 %collective-permute-start.4 = (bf16[3,1,1280]{0,2,1:T(8,128)(2,1)S(1)}, bf16[3,1,1280]{0,2,1:T(8,128)(2,1)S(1)}, u32[]{:S(2)}, u32[]{:S(2)}) collective-permute-start(bf16[3,1,1280]{0,2,1:T(8,128)(2,1)S(1)} %slice.448), channel_id=1, source_target_pairs={{0,4},{4,8},{8,12},{12,16},{16,20},{20,24},{24,28},{28,32},{32,36}... | collective-permute-start | bytes 23048 | tf_op jit(solution)/shard_map/ppermute | solution.py:22
  127.8 17.3 %copy-start.28 = (f32[1,1,16]{2,1,0:T(1,128)}, f32[1,1,16]{2,1,0:T(1,128)S(1)}, u32[]{:S(2)}) copy-start(f32[1,1,16]{2,1,0:T(1,128)S(1)} %get-tuple-element.18) | copy-start | bytes 196
  227.9 55.2 %collective-permute-start.5 = (f32[1,16,72,128]{3,2,1,0:T(8,128)}, f32[1,16,72,128]{3,2,1,0:T(8,128)}, u32[]{:S(2)}, u32[]{:S(2)}) collective-permute-start(f32[1,16,72,128]{3,2,1,0:T(8,128)} %pad_maximum_fusion.3), channel_id=1, source_target_pairs={{0,4},{4,0},{1,5},{5,1},{2,6},{6,2},{3,7},{7,3},{8,12},{12,8},{9,1... | collective-permute-start | bytes 1769480 | tf_op jit(solution)/shard_map/ppermute | solution.py:43
  229.6 19.1 %collective-permute-start.13 = (bf16[3,1,1280]{0,2,1:T(8,128)(2,1)}, bf16[3,1,1280]{0,2,1:T(8,128)(2,1)}, u32[]{:S(2)}, u32[]{:S(2)}) collective-permute-start(bf16[3,1,1280]{0,2,1:T(8,128)(2,1)} %slice.485), channel_id=1, source_target_pairs={{0,4},{4,8},{8,12},{12,16},{16,20},{20,24},{24,28},{28,32},{32,36}... | collective-permute-start | bytes 23048 | tf_op jit(solution)/shard_map/ppermute | solution.py:22
  269.8 19.8 %collective-permute-start.14 = (f32[1,16,72,128]{3,2,1,0:T(8,128)}, f32[1,16,72,128]{3,2,1,0:T(8,128)}, u32[]{:S(2)}, u32[]{:S(2)}) collective-permute-start(f32[1,16,72,128]{3,2,1,0:T(8,128)} %pad_maximum_fusion.6), channel_id=1, source_target_pairs={{0,4},{4,0},{1,5},{5,1},{2,6},{6,2},{3,7},{7,3},{8,12},{12,8},{9,1... | collective-permute-start | bytes 1769480 | tf_op jit(solution)/shard_map/ppermute | solution.py:43
  286.4 30.3 %collective-permute-start.6 = (f32[1,16,72,128]{3,2,1,0:T(8,128)}, f32[1,16,72,128]{3,2,1,0:T(8,128)S(1)}, u32[]{:S(2)}, u32[]{:S(2)}) collective-permute-start(f32[1,16,72,128]{3,2,1,0:T(8,128)} %pad_maximum_fusion.4), channel_id=1, source_target_pairs={{0,24},{8,0},{16,8},{24,16},{1,25},{9,1},{17,9},{25,17},{2,26},{10... | collective-permute-start | bytes 1769480 | tf_op jit(solution)/shard_map/ppermute | solution.py:43
  286.4 30.4 %collective-permute-start.8 = (f32[1,16,72,128]{3,2,1,0:T(8,128)}, f32[1,16,72,128]{3,2,1,0:T(8,128)}, u32[]{:S(2)}, u32[]{:S(2)}) collective-permute-start(f32[1,16,72,128]{3,2,1,0:T(8,128)} %pad_maximum_fusion.4), channel_id=1, source_target_pairs={{0,8},{8,16},{16,24},{24,0},{1,9},{9,17},{17,25},{25,1},{2,10},{10... | collective-permute-start | bytes 1769480 | tf_op jit(solution)/shard_map/ppermute | solution.py:43
  289.6 28.1 %collective-permute-start.7 = (f32[1,16,72,128]{3,2,1,0:T(8,128)}, f32[1,16,72,128]{3,2,1,0:T(8,128)}, u32[]{:S(2)}, u32[]{:S(2)}) collective-permute-start(f32[1,16,72,128]{3,2,1,0:T(8,128)} %pad_maximum_fusion.4), channel_id=1, source_target_pairs={{0,16},{8,24},{16,0},{24,8},{1,17},{9,25},{17,1},{25,9},{2,18},{10... | collective-permute-start | bytes 1769480 | tf_op jit(solution)/shard_map/ppermute | solution.py:43
  292.8 46.3 %collective-permute-start.15 = (f32[1,16,72,128]{3,2,1,0:T(8,128)}, f32[1,16,72,128]{3,2,1,0:T(8,128)S(1)}, u32[]{:S(2)}, u32[]{:S(2)}) collective-permute-start(f32[1,16,72,128]{3,2,1,0:T(8,128)} %pad_maximum_fusion.7), channel_id=1, source_target_pairs={{0,24},{8,0},{16,8},{24,16},{1,25},{9,1},{17,9},{25,17},{2,26},{10... | collective-permute-start | bytes 1769480 | tf_op jit(solution)/shard_map/ppermute | solution.py:43
  293.7 47.4 %collective-permute-start.17 = (f32[1,16,72,128]{3,2,1,0:T(8,128)}, f32[1,16,72,128]{3,2,1,0:T(8,128)S(1)}, u32[]{:S(2)}, u32[]{:S(2)}) collective-permute-start(f32[1,16,72,128]{3,2,1,0:T(8,128)} %pad_maximum_fusion.7), channel_id=1, source_target_pairs={{0,8},{8,16},{16,24},{24,0},{1,9},{9,17},{17,25},{25,1},{2,10},{10... | collective-permute-start | bytes 1769480 | tf_op jit(solution)/shard_map/ppermute | solution.py:43
  316.7 24.5 %collective-permute-start.16 = (f32[1,16,72,128]{3,2,1,0:T(8,128)}, f32[1,16,72,128]{3,2,1,0:T(8,128)S(1)}, u32[]{:S(2)}, u32[]{:S(2)}) collective-permute-start(f32[1,16,72,128]{3,2,1,0:T(8,128)} %pad_maximum_fusion.7), channel_id=1, source_target_pairs={{0,16},{8,24},{16,0},{24,8},{1,17},{9,25},{17,1},{25,9},{2,18},{10... | collective-permute-start | bytes 1769480 | tf_op jit(solution)/shard_map/ppermute | solution.py:43
  321.3 26.2 %collective-permute-start.11 = (f32[1,16,72,128]{3,2,1,0:T(8,128)}, f32[1,16,72,128]{3,2,1,0:T(8,128)}, u32[]{:S(2)}, u32[]{:S(2)}) collective-permute-start(f32[1,16,72,128]{3,2,1,0:T(8,128)} %pad_maximum_fusion.5), channel_id=1, source_target_pairs={{0,96},{1,97},{2,98},{3,99},{4,100},{5,101},{6,102},{7,103},{8,104... | collective-permute-start | bytes 1769480 | tf_op jit(solution)/shard_map/ppermute | solution.py:43
  322.8 21.4 %collective-permute-start.10 = (f32[1,16,72,128]{3,2,1,0:T(8,128)}, f32[1,16,72,128]{3,2,1,0:T(8,128)}, u32[]{:S(2)}, u32[]{:S(2)}) collective-permute-start(f32[1,16,72,128]{3,2,1,0:T(8,128)} %pad_maximum_fusion.5), channel_id=1, source_target_pairs={{0,64},{32,96},{1,65},{33,97},{2,66},{34,98},{3,67},{35,99},{4,68}... | collective-permute-start | bytes 1769480 | tf_op jit(solution)/shard_map/ppermute | solution.py:43
  339.1 29.6 %collective-permute-start.9 = (f32[1,16,72,128]{3,2,1,0:T(8,128)}, f32[1,16,72,128]{3,2,1,0:T(8,128)}, u32[]{:S(2)}, u32[]{:S(2)}) collective-permute-start(f32[1,16,72,128]{3,2,1,0:T(8,128)} %pad_maximum_fusion.5), channel_id=1, source_target_pairs={{0,32},{32,64},{64,96},{1,33},{33,65},{65,97},{2,34},{34,66},{66,9... | collective-permute-start | bytes 1769480 | tf_op jit(solution)/shard_map/ppermute | solution.py:43
  341.3 31.4 %copy-start.8 = (f32[6,16,64,128]{3,2,1,0:T(8,128)S(1)}, f32[6,16,64,128]{3,2,1,0:T(8,128)}, u32[]{:S(2)}) copy-start(f32[6,16,64,128]{3,2,1,0:T(8,128)} %fusion.10) | copy-start | bytes 9437188
  341.7 30.9 %copy-start = (f32[6,128,1,1024]{1,3,0,2:T(8,128)S(1)}, f32[6,128,1,1024]{1,3,0,2:T(8,128)}, u32[]{:S(2)}) copy-start(f32[6,128,1,1024]{1,3,0,2:T(8,128)} %copy.115) | copy-start | bytes 9437188
  341.7 30.9 %copy-start.17 = (f32[6,128,16]{1,2,0:T(8,128)S(1)}, f32[6,128,16]{1,2,0:T(8,128)}, u32[]{:S(2)}) copy-start(f32[6,128,16]{1,2,0:T(8,128)} %get-tuple-element.45) | copy-start | bytes 147460
  341.8 30.9 %copy-start.22 = (f32[6,1,16]{2,0,1:T(8,128)S(1)}, f32[6,1,16]{2,0,1:T(8,128)}, u32[]{:S(2)}) copy-start(f32[6,1,16]{2,0,1:T(8,128)} %copy.174) | copy-start | bytes 1156
  341.8 30.9 %copy-start.43 = (f32[16]{0:T(128)S(1)}, f32[16]{0:T(128)}, u32[]{:S(2)}) copy-start(f32[16]{0:T(128)} %get-tuple-element.65) | copy-start | bytes 196
  341.9 36.5 %collective-permute-start.20 = (f32[1,16,72,128]{3,2,1,0:T(8,128)S(1)}, f32[1,16,72,128]{3,2,1,0:T(8,128)S(1)}, u32[]{:S(2)}, u32[]{:S(2)}) collective-permute-start(f32[1,16,72,128]{3,2,1,0:T(8,128)S(1)} %pad_maximum_fusion.8), channel_id=1, source_target_pairs={{0,96},{1,97},{2,98},{3,99},{4,100},{5,101},{6,102},{7,103},{8,104... | collective-permute-start | bytes 1769480 | tf_op jit(solution)/shard_map/ppermute | solution.py:43
  342.8 35.4 %collective-permute-start.19 = (f32[1,16,72,128]{3,2,1,0:T(8,128)S(1)}, f32[1,16,72,128]{3,2,1,0:T(8,128)S(1)}, u32[]{:S(2)}, u32[]{:S(2)}) collective-permute-start(f32[1,16,72,128]{3,2,1,0:T(8,128)S(1)} %pad_maximum_fusion.8), channel_id=1, source_target_pairs={{0,64},{32,96},{1,65},{33,97},{2,66},{34,98},{3,67},{35,99},{4,68}... | collective-permute-start | bytes 1769480 | tf_op jit(solution)/shard_map/ppermute | solution.py:43
  344.2 34.4 %collective-permute-start.18 = (f32[1,16,72,128]{3,2,1,0:T(8,128)S(1)}, f32[1,16,72,128]{3,2,1,0:T(8,128)S(1)}, u32[]{:S(2)}, u32[]{:S(2)}) collective-permute-start(f32[1,16,72,128]{3,2,1,0:T(8,128)S(1)} %pad_maximum_fusion.8), channel_id=1, source_target_pairs={{0,32},{32,64},{64,96},{1,33},{33,65},{65,97},{2,34},{34,66},{66,9... | collective-permute-start | bytes 1769480 | tf_op jit(solution)/shard_map/ppermute | solution.py:43
  (45 other events, 150.4 us)
Sparse Core Ops, SparseCore 0:
  18.6 89.6 all-gather.2
  110.4 92.3 all-gather.4

commit v7 on v6

--- a/solution.py
+++ b/solution.py
@@ -30,10 +30,12 @@
     size = lax.axis_size(axis)
     place = lax.axis_index(axis)
     groups, heads = own[0].shape
-    tail = own[1].shape[-1]
-    packed = jnp.concatenate(
-        [own[1], jnp.broadcast_to(own[0][..., None, None], (groups, heads, 8, tail))], axis=2
-    )
+    shape = own[1].shape
+    tail = shape[-1]
+    rows = own[1].reshape(groups, -1, tail)
+    keep_rows = jnp.pad(own[0][:, None, :], ((0, 0), (0, 7), (0, tail - heads)))
+    packed = jnp.concatenate([rows, keep_rows], axis=1)
+    body = rows.shape[1]
     received = [None]
     for distance in range(1, size):
         if need_total:
@@ -41,7 +43,7 @@
         else:
             route = [(i, i + distance) for i in range(size - distance)]
         got = lax.ppermute(packed, axis, route)
-        received.append((got[:, :, -8, 0], got[:, :, :-8]))
+        received.append((got[:, body, :heads], got[:, :body].reshape(shape)))
     prefix = (jnp.ones_like(own[0]), jnp.zeros_like(own[1]))
     for distance in range(size - 1, 0, -1):
         joined = combine(prefix, received[distance])

time: 405 us -> 394 us (0.973)
  waiting for transfers between devices: 170 us -> 155 us
  starting transfers between devices: 37 us -> 50.8 us
  other arithmetic: 56.4 us -> 49.5 us
    ppermute x14, waiting for transfers between devices: 56 us -> 41.2 us  [gather_level(): got = lax.ppermute(packed, axis, route)]
    ppermute x14, starting transfers between devices: 20.5 us -> 34.1 us  [gather_level(): got = lax.ppermute(packed, axis, route)]
    mul x4 -> x2, other arithmetic: 6.45 us -> 0.54 us  [mix_groups(): state_now = keep_all[q][..., None, None] * state_now + fresh_all[q]]
    unnamed x128 -> x116, local copies, waits for them, and re-layouts: 9.65 us -> 10.3 us
where the time goes in v7:
time: 394 us; the launch traced here: 387 us
  waiting for transfers between devices  155 us (39%)
  local copies, waits for them, and re-layouts  67 us (17%)
  starting transfers between devices  50.8 us (13%)
  matrix products  50.1 us (13%)
  other arithmetic  49.5 us (13%)
  between operations  14.9 us (4%)
    ppermute x3, waiting for transfers between devices, per_device(): lax.ppermute(tokens, 'chan', [(i, (i + distance) % size) for i in range(s...  49.4 us
    all_gather x2, waiting for transfers between devices, mix_groups(): full_w = lax.all_gather(pair_w, SEQ[:2], axis=0, tiled=True)  45.7 us
    ppermute x14, waiting for transfers between devices, gather_level(): got = lax.ppermute(packed, axis, route)  41.2 us
    ppermute x14, starting transfers between devices, gather_level(): got = lax.ppermute(packed, axis, route)  34.1 us
    dot_general x2, matrix products, mix_groups(): jnp.einsum('td,dgc->tgc', gathered, full_w, preferred_element_type=jnp.fl...  27 us
    convert_element_type x2, other arithmetic, mix_groups(): inputs = jax.nn.silu(pre_act).astype(jnp.bfloat16)  16.1 us
    ppermute x2, waiting for transfers between devices, mix_groups(): lax.ppermute(rows_first, SEQ[2], [(i, (i + distance) % pair) for i in ran...  13.7 us
    dot_general x2, matrix products, mix_groups(): jnp.einsum('qghij,qjghp->qighp', weights, x_all, preferred_element_type=j...  10.8 us
  transfers between devices with their start and end apart: 23, of which 11 were waited for; matrix products, arithmetic and copies ran while one was open for 34% of the time, Pallas kernels for 0%

profile of v7, /device:TPU:22, one launch (start us, length us, event | category | flops | bytes accessed | tf_op | source)
XLA Modules:
  0.0 387.4 jit_solution(5249604030271814485)
XLA Ops:
  10.8 6.7 %collective-permute-done.3 = bf16[128,1,1296]{0,2,1:T(8,128)(2,1)S(1)} collective-permute-done((bf16[128,1,1296]{0,2,1:T(8,128)(2,1)S(1)}, bf16[128,1,1296]{0,2,1:T(8,128)(2,1)S(1)}, u32[]{:S(2)}, u32[]{:S(2)}) %collective-permute-start.3) | collective-permute-done | bytes 331808 | tf_op jit(solution)/shard_map/ppermute | solution.py:85
  20.5 7.0 %collective-permute-done.12 = bf16[128,1,1296]{0,2,1:T(8,128)(2,1)S(1)} collective-permute-done((bf16[128,1,1296]{0,2,1:T(8,128)(2,1)S(1)}, bf16[128,1,1296]{0,2,1:T(8,128)(2,1)S(1)}, u32[]{:S(2)}, u32[]{:S(2)}) %collective-permute-start.12) | collective-permute-done | bytes 331808 | tf_op jit(solution)/shard_map/ppermute | solution.py:85
  28.5 3.6 collective-permute-start.1
  32.1 2.9 collective-permute-start.2
  39.6 3.5 broadcast_in_dim.20
  46.7 19.7 %collective-permute-done = bf16[768,1024]{1,0:T(8,128)(2,1)} collective-permute-done((bf16[768,1024]{1,0:T(8,128)(2,1)}, bf16[768,1024]{1,0:T(8,128)(2,1)}, u32[]{:S(2)}, u32[]{:S(2)}) %collective-permute-start) | collective-permute-done | bytes 1572896 | tf_op jit(solution)/shard_map/ppermute | solution.py:174
  66.4 2.7 constant_dynamic-update-slice_fusion.26
  70.4 29.8 %collective-permute-done.2 = bf16[768,1024]{1,0:T(8,128)(2,1)S(1)} collective-permute-done((bf16[768,1024]{1,0:T(8,128)(2,1)}, bf16[768,1024]{1,0:T(8,128)(2,1)S(1)}, u32[]{:S(2)}, u32[]{:S(2)}) %collective-permute-start.2) | collective-permute-done | bytes 1572896 | tf_op jit(solution)/shard_map/ppermute | solution.py:174
  101.5 6.8 %all-gather.3.cloned.1.call-done = bf16[4096,1,1296]{0,2,1:T(8,128)(2,1)} async-done(((bf16[256,1,1296]{0,2,1:T(8,128)(2,1)}), bf16[4096,1,1296]{0,2,1:T(8,128)(2,1)}) %all-gather.3.cloned.1.call-update) | async-done | bytes 10616848 | tf_op jit(solution)/shard_map/all_gather | solution.py:92
  108.3 13.0 %fusion.85 = (bf16[768,1,1296]{0,2,1:T(8,128)(2,1)S(1)}, f32[768,1,1296]{0,2,1:T(8,128)S(1)}) fusion(bf16[768,4096]{1,0:T(8,128)(2,1)} %constant_dynamic-update-slice_fusion.24, bf16[4096,1,1296]{0,2,1:T(8,128)(2,1)} %all-gather.3.cloned.1.call-done), kind=kOutput, calls=%fused_computation.268 | convolution fusion | flops 8154722304 | bytes 22880256 | tf_op jit(solution)/shard_map/td,dgc->tgc/dot_general | solution.py:97
  121.7 3.6 collective-permute-start.4
  133.9 5.1 %collective-permute-done.4 = bf16[3,1,1280]{0,2,1:T(8,128)(2,1)S(1)} collective-permute-done((bf16[3,1,1280]{0,2,1:T(8,128)(2,1)S(1)}, bf16[3,1,1280]{0,2,1:T(8,128)(2,1)S(1)}, u32[]{:S(2)}, u32[]{:S(2)}) %collective-permute-start.4) | collective-permute-done | bytes 7712 | tf_op jit(solution)/shard_map/ppermute | solution.py:22
  138.9 6.1 %multiply_convert_fusion.3 = bf16[768,1,1280]{0,2,1:T(8,128)(2,1)} fusion(bf16[768,1,1280]{0,2,1:T(8,128)(2,1)S(1)} %slice.455, bf16[3,1,1280]{0,2,1:T(8,128)(2,1)S(1)} %collective-permute-done.4, f32[1280]{0:T(1024)} %get-tuple-element.9, f32[1280]{0:T(1024)} %get-tuple-element.10, f32[1280]{0:T(1024)} %get-tuple-element.11, f32[1280]{0:T(1024)} %get-tuple-element.12, ...), kind=kLoop, calls=%fused_computation.7 | loop fusion | flops 25559040 | bytes 3965440 | tf_op jit(solution)/shard_map/convert_element_type | solution.py:110
  145.0 4.0 %copy.54 = bf16[768,1,1280]{2,0,1:T(8,128)(2,1)} copy(bf16[768,1,1280]{0,2,1:T(8,128)(2,1)} %multiply_convert_fusion.3) | data formatting | bytes 3932160 | tf_op jit(solution)/shard_map/convert_element_type | solution.py:110
  149.0 3.1 slice_convert_fusion.1
  152.2 2.6 copy.55
  163.9 38.9 %all-gather.5.cloned.1.call-done = bf16[4096,1,1296]{0,2,1:T(8,128)(2,1)} async-done(((bf16[256,1,1296]{0,2,1:T(8,128)(2,1)}), bf16[4096,1,1296]{0,2,1:T(8,128)(2,1)}) %all-gather.5.cloned.1.call-update) | async-done | bytes 10616848 | tf_op jit(solution)/shard_map/all_gather | solution.py:92
  202.8 14.0 %fusion.86 = (bf16[768,1,1296]{0,2,1:T(8,128)(2,1)}, f32[768,1,1296]{0,2,1:T(8,128)S(1)}) fusion(bf16[768,4096]{1,0:T(8,128)(2,1)} %constant_dynamic-update-slice_fusion.24, bf16[4096,1,1296]{0,2,1:T(8,128)(2,1)} %all-gather.5.cloned.1.call-done), kind=kOutput, calls=%fused_computation.269 | convolution fusion | flops 8154722304 | bytes 22880256 | tf_op jit(solution)/shard_map/td,dgc->tgc/dot_general | solution.py:97
  227.9 2.6 collective-permute-start.13
  236.2 5.6 %fusion.10 = f32[6,16,64,128]{3,2,1,0:T(8,128)} fusion(bf16[6,128,16,64]{1,3,2,0:T(8,128)(2,1)} %bitcast.427, f32[6,16,128]{2,1,0:T(8,128)} %copy.59, f32[6,16,128]{2,1,0:T(8,128)} %copy.57, f32[6,128,128]{2,1,0:T(8,128)} %fusion.51, pred[128,128]{1,0:T(8,128)(4,1)} %iota_compare_fusion.1), kind=kOutput, calls=%fused_computation.10 | convolution fusion | flops 210763776 | bytes 5226496 | tf_op jit(solution)/shard_map/qghij,qjghp->qighp/dot_general | solution.py:149
  249.6 10.0 %multiply_convert_fusion.2 = bf16[768,1,1280]{0,2,1:T(8,128)(2,1)} fusion(bf16[768,1,1280]{0,2,1:T(8,128)(2,1)} %slice.492, bf16[3,1,1280]{0,2,1:T(8,128)(2,1)} %collective-permute-done.13, f32[1280]{0:T(1024)} %get-tuple-element.13, f32[1280]{0:T(1024)} %get-tuple-element.14, f32[1280]{0:T(1024)} %get-tuple-element.8, f32[1280]{0:T(1024)} %get-tuple-element.7, ...), kind=kLoop, calls=%fused_computation.6 | loop fusion | flops 25559040 | bytes 3965440 | tf_op jit(solution)/shard_map/convert_element_type | solution.py:110
  259.6 2.7 copy.64
  271.4 3.6 collective-permute-start.14
  275.9 3.6 copy.70
  279.6 5.2 %fusion.11 = f32[6,16,64,128]{3,2,1,0:T(8,128)S(1)} fusion(bf16[6,128,16,64]{1,3,2,0:T(8,128)(2,1)} %bitcast.429, f32[6,16,128]{2,1,0:T(8,128)} %copy.69, f32[6,16,128]{2,1,0:T(8,128)} %copy.67, f32[6,128,128]{2,1,0:T(8,128)S(1)} %copy-done.19, pred[128,128]{1,0:T(8,128)(4,1)} %iota_compare_fusion.1), kind=kOutput, calls=%fused_computation.11 | convolution fusion | flops 210763776 | bytes 5226496 | tf_op jit(solution)/shard_map/qghij,qjghp->qighp/dot_general | solution.py:149
  289.1 2.4 collective-permute-start.8
  297.6 18.1 %collective-permute-done.6 = f32[1,1032,128]{2,1,0:T(8,128)S(1)} collective-permute-done((f32[1,1032,128]{2,1,0:T(8,128)S(1)}, f32[1,1032,128]{2,1,0:T(8,128)S(1)}, u32[]{:S(2)}, u32[]{:S(2)}) %collective-permute-start.6) | collective-permute-done | bytes 528416 | tf_op jit(solution)/shard_map/ppermute | solution.py:45
  319.2 16.3 %collective-permute-done.15 = f32[1,1032,128]{2,1,0:T(8,128)S(1)} collective-permute-done((f32[1,1032,128]{2,1,0:T(8,128)S(1)}, f32[1,1032,128]{2,1,0:T(8,128)S(1)}, u32[]{:S(2)}, u32[]{:S(2)}) %collective-permute-start.15) | collective-permute-done | bytes 528416 | tf_op jit(solution)/shard_map/ppermute | solution.py:45
  340.1 16.7 %collective-permute-start.18 = (f32[1,1032,128]{2,1,0:T(8,128)S(1)}, f32[1,1032,128]{2,1,0:T(8,128)S(1)}, u32[]{:S(2)}, u32[]{:S(2)}) collective-permute-start(f32[1,1032,128]{2,1,0:T(8,128)S(1)} %select_maximum_fusion), channel_id=1, source_target_pairs={{0,32},{32,64},{64,96},{1,33},{33,65},{65,97},{2,34},{34,66},{66,9... | collective-permute-start | bytes 1585160 | tf_op jit(solution)/shard_map/ppermute | solution.py:45
  357.0 6.0 %collective-permute-done.9 = f32[1,1032,128]{2,1,0:T(8,128)S(1)} collective-permute-done((f32[1,1032,128]{2,1,0:T(8,128)S(1)}, f32[1,1032,128]{2,1,0:T(8,128)S(1)}, u32[]{:S(2)}, u32[]{:S(2)}) %collective-permute-start.9) | collective-permute-done | bytes 528416 | tf_op jit(solution)/shard_map/ppermute | solution.py:45
  364.2 3.1 multiply_reduce_fusion.1
  377.3 2.9 copy.74
  (264 shorter events, 100.7 us)
Async XLA Ops:
  6.5 13.9 %copy-start.11 = (bf16[2,128,1296]{1,2,0:T(8,128)(2,1)S(1)}, bf16[2,128,1296]{1,2,0:T(8,128)(2,1)}, u32[]{:S(2)}) copy-start(bf16[2,128,1296]{1,2,0:T(8,128)(2,1)} %param.9) | copy-start | bytes 1990660
  6.5 28.4 %copy-start.28 = (f32[2,1280]{1,0:T(2,128)S(1)}, f32[2,1280]{1,0:T(2,128)}, u32[]{:S(2)}) copy-start(f32[2,1280]{1,0:T(2,128)} %param.11) | copy-start | bytes 30724
  6.5 29.0 %copy-start.23 = (f32[2,4,1280]{2,1,0:T(4,128)S(1)}, f32[2,4,1280]{2,1,0:T(4,128)}, u32[]{:S(2)}) copy-start(f32[2,4,1280]{2,1,0:T(4,128)} %param.10) | copy-start | bytes 122884
  6.5 101.8 %all-gather.3.cloned.1.call-start = ((), (), s32[]{:S(2)}) async-start(), calls=%async_computation | async-start | bytes 11280384 | tf_op jit(solution)/shard_map/all_gather | solution.py:92
  7.7 9.8 %collective-permute-start.3 = (bf16[128,1,1296]{0,2,1:T(8,128)(2,1)S(1)}, bf16[128,1,1296]{0,2,1:T(8,128)(2,1)S(1)}, u32[]{:S(2)}, u32[]{:S(2)}) collective-permute-start(bf16[128,1,1296]{0,2,1:T(8,128)(2,1)S(1)} %get-tuple-element.39), channel_id=1, source_target_pairs={{0,4},{4,0},{1,5},{5,1},{2,6},{6,2},{3,7},{7,3},{8,12},{12,8},{9,1... | collective-permute-start | bytes 995336 | tf_op jit(solution)/shard_map/ppermute | solution.py:85
  18.5 184.3 %all-gather.5.cloned.1.call-start = ((), (), s32[]{:S(2)}) async-start(), calls=%async_computation.1 | async-start | bytes 11280384 | tf_op jit(solution)/shard_map/all_gather | solution.py:92
  18.5 8.9 %collective-permute-start.12 = (bf16[128,1,1296]{0,2,1:T(8,128)(2,1)S(1)}, bf16[128,1,1296]{0,2,1:T(8,128)(2,1)S(1)}, u32[]{:S(2)}, u32[]{:S(2)}) collective-permute-start(bf16[128,1,1296]{0,2,1:T(8,128)(2,1)S(1)} %get-tuple-element.40), channel_id=1, source_target_pairs={{0,4},{4,0},{1,5},{5,1},{2,6},{6,2},{3,7},{7,3},{8,12},{12,8},{9,1... | collective-permute-start | bytes 995336 | tf_op jit(solution)/shard_map/ppermute | solution.py:85
  28.4 38.0 %collective-permute-start = (bf16[768,1024]{1,0:T(8,128)(2,1)}, bf16[768,1024]{1,0:T(8,128)(2,1)}, u32[]{:S(2)}, u32[]{:S(2)}) collective-permute-start(bf16[768,1024]{1,0:T(8,128)(2,1)} %param.8), channel_id=1, source_target_pairs={{0,1},{1,2},{2,3},{3,0},{4,5},{5,6},{6,7},{7,4},{8,9},{9,10},{10,1... | collective-permute-start | bytes 4718600 | tf_op jit(solution)/shard_map/ppermute | solution.py:174
  28.5 40.6 %collective-permute-start.1 = (bf16[768,1024]{1,0:T(8,128)(2,1)}, bf16[768,1024]{1,0:T(8,128)(2,1)S(1)}, u32[]{:S(2)}, u32[]{:S(2)}) collective-permute-start(bf16[768,1024]{1,0:T(8,128)(2,1)} %param.8), channel_id=1, source_target_pairs={{0,2},{1,3},{2,0},{3,1},{4,6},{5,7},{6,4},{7,5},{8,10},{9,11},{10,... | collective-permute-start | bytes 4718600 | tf_op jit(solution)/shard_map/ppermute | solution.py:174
  32.1 68.1 %collective-permute-start.2 = (bf16[768,1024]{1,0:T(8,128)(2,1)}, bf16[768,1024]{1,0:T(8,128)(2,1)S(1)}, u32[]{:S(2)}, u32[]{:S(2)}) collective-permute-start(bf16[768,1024]{1,0:T(8,128)(2,1)} %param.8), channel_id=1, source_target_pairs={{0,3},{1,0},{2,1},{3,2},{4,7},{5,4},{6,5},{7,6},{8,11},{9,8},{10,9... | collective-permute-start | bytes 4718600 | tf_op jit(solution)/shard_map/ppermute | solution.py:174
  121.7 17.3 %collective-permute-start.4 = (bf16[3,1,1280]{0,2,1:T(8,128)(2,1)S(1)}, bf16[3,1,1280]{0,2,1:T(8,128)(2,1)S(1)}, u32[]{:S(2)}, u32[]{:S(2)}) collective-permute-start(bf16[3,1,1280]{0,2,1:T(8,128)(2,1)S(1)} %slice.454), channel_id=1, source_target_pairs={{0,4},{4,8},{8,12},{12,16},{16,20},{20,24},{24,28},{28,32},{32,36}... | collective-permute-start | bytes 23048 | tf_op jit(solution)/shard_map/ppermute | solution.py:22
  202.8 14.0 %copy-start.43 = (f32[16]{0:T(128)S(1)}, f32[16]{0:T(128)}, u32[]{:S(2)}) copy-start(f32[16]{0:T(128)} %get-tuple-element.93) | copy-start | bytes 196
  202.8 14.1 %copy-start.42 = (f32[16]{0:T(128)S(1)}, f32[16]{0:T(128)}, u32[]{:S(2)}) copy-start(f32[16]{0:T(128)} %get-tuple-element.91) | copy-start | bytes 196
  224.5 60.4 %collective-permute-start.5 = (f32[1,1032,128]{2,1,0:T(8,128)}, f32[1,1032,128]{2,1,0:T(8,128)}, u32[]{:S(2)}, u32[]{:S(2)}) collective-permute-start(f32[1,1032,128]{2,1,0:T(8,128)} %select_maximum_fusion.5), channel_id=1, source_target_pairs={{0,4},{4,0},{1,5},{5,1},{2,6},{6,2},{3,7},{7,3},{8,12},{12,8},{9,1... | collective-permute-start | bytes 1585160 | tf_op jit(solution)/shard_map/ppermute | solution.py:45
  227.9 21.7 %collective-permute-start.13 = (bf16[3,1,1280]{0,2,1:T(8,128)(2,1)}, bf16[3,1,1280]{0,2,1:T(8,128)(2,1)}, u32[]{:S(2)}, u32[]{:S(2)}) collective-permute-start(bf16[3,1,1280]{0,2,1:T(8,128)(2,1)} %slice.491), channel_id=1, source_target_pairs={{0,4},{4,8},{8,12},{12,16},{16,20},{20,24},{24,28},{28,32},{32,36}... | collective-permute-start | bytes 23048 | tf_op jit(solution)/shard_map/ppermute | solution.py:22
  271.4 20.1 %collective-permute-start.14 = (f32[1,1032,128]{2,1,0:T(8,128)}, f32[1,1032,128]{2,1,0:T(8,128)}, u32[]{:S(2)}, u32[]{:S(2)}) collective-permute-start(f32[1,1032,128]{2,1,0:T(8,128)} %select_maximum_fusion.2), channel_id=1, source_target_pairs={{0,4},{4,0},{1,5},{5,1},{2,6},{6,2},{3,7},{7,3},{8,12},{12,8},{9,1... | collective-permute-start | bytes 1585160 | tf_op jit(solution)/shard_map/ppermute | solution.py:45
  284.8 9.1 %copy-start.5 = (f32[1,16,64,128]{3,2,1,0:T(8,128)S(1)}, f32[1,16,64,128]{3,2,1,0:T(8,128)}, u32[]{:S(2)}) copy-start(f32[1,16,64,128]{3,2,1,0:T(8,128)} %copy-done.4) | copy-start | bytes 1572868
  284.8 9.1 %copy-start.8 = (f32[1,16,64,128]{3,2,1,0:T(8,128)S(1)}, f32[1,16,64,128]{3,2,1,0:T(8,128)}, u32[]{:S(2)}) copy-start(f32[1,16,64,128]{3,2,1,0:T(8,128)} %copy-done.7) | copy-start | bytes 1572868
  284.9 9.1 %copy-start.9 = (f32[6,16,64,128]{3,2,1,0:T(8,128)S(1)}, f32[6,16,64,128]{3,2,1,0:T(8,128)}, u32[]{:S(2)}) copy-start(f32[6,16,64,128]{3,2,1,0:T(8,128)} %constant_dynamic-update-slice_fusion.13) | copy-start | bytes 9437188
  288.1 9.3 %copy-start.6 = (f32[1,16,64,128]{3,2,1,0:T(8,128)S(1)}, f32[1,16,64,128]{3,2,1,0:T(8,128)}, u32[]{:S(2)}) copy-start(f32[1,16,64,128]{3,2,1,0:T(8,128)} %get-tuple-element.30) | copy-start | bytes 1572868
  288.2 27.6 %collective-permute-start.6 = (f32[1,1032,128]{2,1,0:T(8,128)S(1)}, f32[1,1032,128]{2,1,0:T(8,128)S(1)}, u32[]{:S(2)}, u32[]{:S(2)}) collective-permute-start(f32[1,1032,128]{2,1,0:T(8,128)S(1)} %select_maximum_fusion.4), channel_id=1, source_target_pairs={{0,24},{8,0},{16,8},{24,16},{1,25},{9,1},{17,9},{25,17},{2,26},{10... | collective-permute-start | bytes 1585160 | tf_op jit(solution)/shard_map/ppermute | solution.py:45
  288.2 27.5 %collective-permute-start.7 = (f32[1,1032,128]{2,1,0:T(8,128)S(1)}, f32[1,1032,128]{2,1,0:T(8,128)S(1)}, u32[]{:S(2)}, u32[]{:S(2)}) collective-permute-start(f32[1,1032,128]{2,1,0:T(8,128)S(1)} %select_maximum_fusion.4), channel_id=1, source_target_pairs={{0,16},{8,24},{16,0},{24,8},{1,17},{9,25},{17,1},{25,9},{2,18},{10... | collective-permute-start | bytes 1585160 | tf_op jit(solution)/shard_map/ppermute | solution.py:45
  289.1 27.5 %collective-permute-start.8 = (f32[1,1032,128]{2,1,0:T(8,128)S(1)}, f32[1,1032,128]{2,1,0:T(8,128)S(1)}, u32[]{:S(2)}, u32[]{:S(2)}) collective-permute-start(f32[1,1032,128]{2,1,0:T(8,128)S(1)} %select_maximum_fusion.4), channel_id=1, source_target_pairs={{0,8},{8,16},{16,24},{24,0},{1,9},{9,17},{17,25},{25,1},{2,10},{10... | collective-permute-start | bytes 1585160 | tf_op jit(solution)/shard_map/ppermute | solution.py:45
  294.3 41.2 %collective-permute-start.15 = (f32[1,1032,128]{2,1,0:T(8,128)S(1)}, f32[1,1032,128]{2,1,0:T(8,128)S(1)}, u32[]{:S(2)}, u32[]{:S(2)}) collective-permute-start(f32[1,1032,128]{2,1,0:T(8,128)S(1)} %select_maximum_fusion.1), channel_id=1, source_target_pairs={{0,24},{8,0},{16,8},{24,16},{1,25},{9,1},{17,9},{25,17},{2,26},{10... | collective-permute-start | bytes 1585160 | tf_op jit(solution)/shard_map/ppermute | solution.py:45
  295.2 42.1 %collective-permute-start.16 = (f32[1,1032,128]{2,1,0:T(8,128)S(1)}, f32[1,1032,128]{2,1,0:T(8,128)S(1)}, u32[]{:S(2)}, u32[]{:S(2)}) collective-permute-start(f32[1,1032,128]{2,1,0:T(8,128)S(1)} %select_maximum_fusion.1), channel_id=1, source_target_pairs={{0,16},{8,24},{16,0},{24,8},{1,17},{9,25},{17,1},{25,9},{2,18},{10... | collective-permute-start | bytes 1585160 | tf_op jit(solution)/shard_map/ppermute | solution.py:45
  315.7 21.7 %collective-permute-start.17 = (f32[1,1032,128]{2,1,0:T(8,128)S(1)}, f32[1,1032,128]{2,1,0:T(8,128)S(1)}, u32[]{:S(2)}, u32[]{:S(2)}) collective-permute-start(f32[1,1032,128]{2,1,0:T(8,128)S(1)} %select_maximum_fusion.1), channel_id=1, source_target_pairs={{0,8},{8,16},{16,24},{24,0},{1,9},{9,17},{17,25},{25,1},{2,10},{10... | collective-permute-start | bytes 1585160 | tf_op jit(solution)/shard_map/ppermute | solution.py:45
  317.2 22.9 %collective-permute-start.11 = (f32[1,1032,128]{2,1,0:T(8,128)S(1)}, f32[1,1032,128]{2,1,0:T(8,128)S(1)}, u32[]{:S(2)}, u32[]{:S(2)}) collective-permute-start(f32[1,1032,128]{2,1,0:T(8,128)S(1)} %select_maximum_fusion.3), channel_id=1, source_target_pairs={{0,96},{1,97},{2,98},{3,99},{4,100},{5,101},{6,102},{7,103},{8,104... | collective-permute-start | bytes 1585160 | tf_op jit(solution)/shard_map/ppermute | solution.py:45
  317.9 39.0 %collective-permute-start.10 = (f32[1,1032,128]{2,1,0:T(8,128)S(1)}, f32[1,1032,128]{2,1,0:T(8,128)S(1)}, u32[]{:S(2)}, u32[]{:S(2)}) collective-permute-start(f32[1,1032,128]{2,1,0:T(8,128)S(1)} %select_maximum_fusion.3), channel_id=1, source_target_pairs={{0,64},{32,96},{1,65},{33,97},{2,66},{34,98},{3,67},{35,99},{4,68}... | collective-permute-start | bytes 1585160 | tf_op jit(solution)/shard_map/ppermute | solution.py:45
  335.4 27.5 %collective-permute-start.9 = (f32[1,1032,128]{2,1,0:T(8,128)S(1)}, f32[1,1032,128]{2,1,0:T(8,128)S(1)}, u32[]{:S(2)}, u32[]{:S(2)}) collective-permute-start(f32[1,1032,128]{2,1,0:T(8,128)S(1)} %select_maximum_fusion.3), channel_id=1, source_target_pairs={{0,32},{32,64},{64,96},{1,33},{33,65},{65,97},{2,34},{34,66},{66,9... | collective-permute-start | bytes 1585160 | tf_op jit(solution)/shard_map/ppermute | solution.py:45
  338.1 32.1 %collective-permute-start.20 = (f32[1,1032,128]{2,1,0:T(8,128)S(1)}, f32[1,1032,128]{2,1,0:T(8,128)S(1)}, u32[]{:S(2)}, u32[]{:S(2)}) collective-permute-start(f32[1,1032,128]{2,1,0:T(8,128)S(1)} %select_maximum_fusion), channel_id=1, source_target_pairs={{0,96},{1,97},{2,98},{3,99},{4,100},{5,101},{6,102},{7,103},{8,104... | collective-permute-start | bytes 1585160 | tf_op jit(solution)/shard_map/ppermute | solution.py:45
  338.8 31.5 %collective-permute-start.19 = (f32[1,1032,128]{2,1,0:T(8,128)S(1)}, f32[1,1032,128]{2,1,0:T(8,128)S(1)}, u32[]{:S(2)}, u32[]{:S(2)}) collective-permute-start(f32[1,1032,128]{2,1,0:T(8,128)S(1)} %select_maximum_fusion), channel_id=1, source_target_pairs={{0,64},{32,96},{1,65},{33,97},{2,66},{34,98},{3,67},{35,99},{4,68}... | collective-permute-start | bytes 1585160 | tf_op jit(solution)/shard_map/ppermute | solution.py:45
  340.1 30.2 %collective-permute-start.18 = (f32[1,1032,128]{2,1,0:T(8,128)S(1)}, f32[1,1032,128]{2,1,0:T(8,128)S(1)}, u32[]{:S(2)}, u32[]{:S(2)}) collective-permute-start(f32[1,1032,128]{2,1,0:T(8,128)S(1)} %select_maximum_fusion), channel_id=1, source_target_pairs={{0,32},{32,64},{64,96},{1,33},{33,65},{65,97},{2,34},{34,66},{66,9... | collective-permute-start | bytes 1585160 | tf_op jit(solution)/shard_map/ppermute | solution.py:45
  (43 other events, 151.6 us)
Sparse Core Ops, SparseCore 0:
  18.6 89.6 all-gather.2
  110.4 92.3 all-gather.4

commit v8 on v7

--- a/solution.py
+++ b/solution.py
@@ -68,7 +68,7 @@
     result = prefixes[-1]
     for prefix in reversed(prefixes[:-1]):
         result = combine(result, prefix)
-    return result[1]
+    return result[1], prefixes[0][1]
 
 
 def mix_groups(gathered, w_in, conv_w, conv_b, dt_bias, a_log, d_skip, norm_gain, after):
@@ -137,10 +137,11 @@
         keep_before.append(keep_now)
         state_now = keep_all[q][..., None, None] * state_now + fresh_all[q]
         keep_now = keep_now * keep_all[q]
-    incoming = entering(keep_now, state_now, SEQ if isinstance(SEQ, tuple) else (SEQ,))
+    incoming, first_level = entering(keep_now, state_now, SEQ if isinstance(SEQ, tuple) else (SEQ,))
     states = jnp.stack(local_states) + jnp.stack(keep_before)[..., None, None] * incoming[None]
 
     scores = jnp.einsum("qign,qjgn->qgij", c_all, b_all, preferred_element_type=jnp.float32)
+    scores = scores + first_level.reshape(-1)[0] * 0
     cum_cols = jnp.transpose(cumulative, (0, 2, 3, 1))
     dt_cols = jnp.transpose(step_dt, (0, 2, 3, 1))
     spread = cum_cols[..., :, None] - cum_cols[..., None, :]

time: 394 us -> 395 us (level)
  the two profiles are of different devices: /device:TPU:22 before, /device:TPU:24 now
where the time goes in v8:
time: 395 us; the launch traced here: 388 us
  waiting for transfers between devices  172 us (44%)
  local copies, waits for them, and re-layouts  69.7 us (18%)
  matrix products  47.4 us (12%)
  other arithmetic  44.3 us (11%)
  starting transfers between devices  36.7 us (9%)
  between operations  17.5 us (4%)
    ppermute x3, waiting for transfers between devices, per_device(): lax.ppermute(tokens, 'chan', [(i, (i + distance) % size) for i in range(s...  51.5 us
    ppermute x14, waiting for transfers between devices, gather_level(): got = lax.ppermute(packed, axis, route)  51.2 us
    all_gather x2, waiting for transfers between devices, mix_groups(): full_w = lax.all_gather(pair_w, SEQ[:2], axis=0, tiled=True)  44.3 us
    dot_general x2, matrix products, mix_groups(): jnp.einsum('td,dgc->tgc', gathered, full_w, preferred_element_type=jnp.fl...  28 us
    ppermute x14, starting transfers between devices, gather_level(): got = lax.ppermute(packed, axis, route)  20.1 us
    convert_element_type x2, other arithmetic, mix_groups(): inputs = jax.nn.silu(pre_act).astype(jnp.bfloat16)  14 us
    ppermute x2, waiting for transfers between devices, mix_groups(): lax.ppermute(rows_first, SEQ[2], [(i, (i + distance) % pair) for i in ran...  13.7 us
    ppermute x2, waiting for transfers between devices, shifted(): return lax.ppermute(block, axis, route)  11.3 us
  transfers between devices with their start and end apart: 23, of which 16 were waited for; matrix products, arithmetic and copies ran while one was open for 31% of the time, Pallas kernels for 0%

profile of v8, /device:TPU:24, one launch (start us, length us, event | category | flops | bytes accessed | tf_op | source)
XLA Modules:
  0.0 387.6 jit_solution(10164798829692934990)
XLA Ops:
  10.8 6.7 %collective-permute-done.3 = bf16[128,1,1296]{0,2,1:T(8,128)(2,1)S(1)} collective-permute-done((bf16[128,1,1296]{0,2,1:T(8,128)(2,1)S(1)}, bf16[128,1,1296]{0,2,1:T(8,128)(2,1)S(1)}, u32[]{:S(2)}, u32[]{:S(2)}) %collective-permute-start.3) | collective-permute-done | bytes 331808 | tf_op jit(solution)/shard_map/ppermute | solution.py:85
  20.5 7.0 %collective-permute-done.12 = bf16[128,1,1296]{0,2,1:T(8,128)(2,1)S(1)} collective-permute-done((bf16[128,1,1296]{0,2,1:T(8,128)(2,1)S(1)}, bf16[128,1,1296]{0,2,1:T(8,128)(2,1)S(1)}, u32[]{:S(2)}, u32[]{:S(2)}) %collective-permute-start.12) | collective-permute-done | bytes 331808 | tf_op jit(solution)/shard_map/ppermute | solution.py:85
  28.5 3.6 collective-permute-start.1
  32.1 2.9 collective-permute-start.2
  38.6 3.5 broadcast_in_dim.20
  44.7 21.7 %collective-permute-done = bf16[768,1024]{1,0:T(8,128)(2,1)} collective-permute-done((bf16[768,1024]{1,0:T(8,128)(2,1)}, bf16[768,1024]{1,0:T(8,128)(2,1)}, u32[]{:S(2)}, u32[]{:S(2)}) %collective-permute-start) | collective-permute-done | bytes 1572896 | tf_op jit(solution)/shard_map/ppermute | solution.py:175
  66.4 2.7 constant_dynamic-update-slice_fusion.26
  70.4 29.8 %collective-permute-done.2 = bf16[768,1024]{1,0:T(8,128)(2,1)S(1)} collective-permute-done((bf16[768,1024]{1,0:T(8,128)(2,1)}, bf16[768,1024]{1,0:T(8,128)(2,1)S(1)}, u32[]{:S(2)}, u32[]{:S(2)}) %collective-permute-start.2) | collective-permute-done | bytes 1572896 | tf_op jit(solution)/shard_map/ppermute | solution.py:175
  101.5 8.2 %all-gather.3.cloned.1.call-done = bf16[4096,1,1296]{0,2,1:T(8,128)(2,1)} async-done(((bf16[256,1,1296]{0,2,1:T(8,128)(2,1)}), bf16[4096,1,1296]{0,2,1:T(8,128)(2,1)}) %all-gather.3.cloned.1.call-update) | async-done | bytes 10616848 | tf_op jit(solution)/shard_map/all_gather | solution.py:92
  109.7 14.0 %fusion.86 = (bf16[768,1,1296]{0,2,1:T(8,128)(2,1)}, f32[768,1,1296]{0,2,1:T(8,128)S(1)}) fusion(bf16[768,4096]{1,0:T(8,128)(2,1)} %constant_dynamic-update-slice_fusion.24, bf16[4096,1,1296]{0,2,1:T(8,128)(2,1)} %all-gather.3.cloned.1.call-done), kind=kOutput, calls=%fused_computation.273 | convolution fusion | flops 8154722304 | bytes 22880256 | tf_op jit(solution)/shard_map/td,dgc->tgc/dot_general | solution.py:97
  125.8 3.6 collective-permute-start.4
  134.5 10.6 %collective-permute-done.4 = bf16[3,1,1280]{0,2,1:T(8,128)(2,1)S(1)} collective-permute-done((bf16[3,1,1280]{0,2,1:T(8,128)(2,1)S(1)}, bf16[3,1,1280]{0,2,1:T(8,128)(2,1)S(1)}, u32[]{:S(2)}, u32[]{:S(2)}) %collective-permute-start.4) | collective-permute-done | bytes 7712 | tf_op jit(solution)/shard_map/ppermute | solution.py:22
  145.1 5.2 %multiply_convert_fusion.3 = bf16[768,1,1280]{0,2,1:T(8,128)(2,1)} fusion(bf16[768,1,1280]{0,2,1:T(8,128)(2,1)S(1)} %slice.463, bf16[3,1,1280]{0,2,1:T(8,128)(2,1)S(1)} %collective-permute-done.4, f32[1280]{0:T(1024)S(1)} %get-tuple-element.9, f32[1280]{0:T(1024)S(1)} %get-tuple-element.10, f32[1280]{0:T(1024)S(1)} %get-tuple-element.11, ...), kind=kLoop, calls=%fused_computation.7 | loop fusion | flops 25559040 | bytes 3965440 | tf_op jit(solution)/shard_map/convert_element_type | solution.py:110
  150.3 4.0 %copy.54 = bf16[768,1,1280]{2,0,1:T(8,128)(2,1)} copy(bf16[768,1,1280]{0,2,1:T(8,128)(2,1)} %multiply_convert_fusion.3) | data formatting | bytes 3932160 | tf_op jit(solution)/shard_map/convert_element_type | solution.py:110
  154.3 3.3 slice_convert_fusion.1
  157.6 2.6 copy.55
  167.2 36.1 %all-gather.5.cloned.1.call-done = bf16[4096,1,1296]{0,2,1:T(8,128)(2,1)} async-done(((bf16[256,1,1296]{0,2,1:T(8,128)(2,1)}), bf16[4096,1,1296]{0,2,1:T(8,128)(2,1)}) %all-gather.5.cloned.1.call-update) | async-done | bytes 10616848 | tf_op jit(solution)/shard_map/all_gather | solution.py:92
  203.3 14.0 %fusion.87 = (bf16[768,1,1296]{0,2,1:T(8,128)(2,1)}, f32[768,1,1296]{0,2,1:T(8,128)S(1)}) fusion(bf16[768,4096]{1,0:T(8,128)(2,1)} %constant_dynamic-update-slice_fusion.24, bf16[4096,1,1296]{0,2,1:T(8,128)(2,1)} %all-gather.5.cloned.1.call-done), kind=kOutput, calls=%fused_computation.274 | convolution fusion | flops 8154722304 | bytes 22880256 | tf_op jit(solution)/shard_map/td,dgc->tgc/dot_general | solution.py:97
  237.2 3.0 slice.502
  245.5 8.9 %multiply_convert_fusion.2 = bf16[768,1,1280]{0,2,1:T(8,128)(2,1)S(1)} fusion(bf16[768,1,1280]{0,2,1:T(8,128)(2,1)} %slice.502, bf16[3,1,1280]{0,2,1:T(8,128)(2,1)} %collective-permute-done.13, f32[1280]{0:T(1024)} %get-tuple-element.13, f32[1280]{0:T(1024)} %get-tuple-element.14, f32[1280]{0:T(1024)} %get-tuple-element.8, f32[1280]{0:T(1024)} %get-tuple-element.7, ...), kind=kLoop, calls=%fused_computation.6 | loop fusion | flops 25559040 | bytes 3965440 | tf_op jit(solution)/shard_map/convert_element_type | solution.py:110
  256.7 3.1 slice_convert_fusion
  259.8 2.6 copy.65
  278.1 5.2 %fusion.10 = f32[6,16,64,128]{3,2,1,0:T(8,128)S(1)} fusion(bf16[6,128,16,64]{1,3,2,0:T(8,128)(2,1)} %bitcast.437, f32[6,16,128]{2,1,0:T(8,128)S(1)} %copy-done.19, f32[6,16,128]{2,1,0:T(8,128)S(1)} %copy-done.18, f32[6,128,128]{2,1,0:T(8,128)S(1)} %convolution_add_fusion.1, pred[128,128]{1,0:T(8,128)(4,1)S(1)} %copy-done.23), kind=kOutput, calls=%fused_computation.10 | convolution fusion | flops 210763776 | bytes 5226496 | tf_op jit(solution)/shard_map/qghij,qjghp->qighp/dot_general | solution.py:150
  289.3 2.9 collective-permute-start.15
  299.1 10.8 %collective-permute-done.6 = f32[1,1032,128]{2,1,0:T(8,128)S(1)} collective-permute-done((f32[1,1032,128]{2,1,0:T(8,128)S(1)}, f32[1,1032,128]{2,1,0:T(8,128)S(1)}, u32[]{:S(2)}, u32[]{:S(2)}) %collective-permute-start.6) | collective-permute-done | bytes 528416 | tf_op jit(solution)/shard_map/ppermute | solution.py:45
  309.9 2.6 collective-permute-start.17
  318.2 5.7 %collective-permute-done.15 = f32[1,1032,128]{2,1,0:T(8,128)S(1)} collective-permute-done((f32[1,1032,128]{2,1,0:T(8,128)S(1)}, f32[1,1032,128]{2,1,0:T(8,128)S(1)}, u32[]{:S(2)}, u32[]{:S(2)}) %collective-permute-start.15) | collective-permute-done | bytes 528416 | tf_op jit(solution)/shard_map/ppermute | solution.py:45
  326.4 7.7 %collective-permute-done.17 = f32[1,1032,128]{2,1,0:T(8,128)S(1)} collective-permute-done((f32[1,1032,128]{2,1,0:T(8,128)S(1)}, f32[1,1032,128]{2,1,0:T(8,128)S(1)}, u32[]{:S(2)}, u32[]{:S(2)}) %collective-permute-start.17) | collective-permute-done | bytes 528416 | tf_op jit(solution)/shard_map/ppermute | solution.py:45
  337.6 18.7 %collective-permute-done.11 = f32[1,1032,128]{2,1,0:T(8,128)S(1)} collective-permute-done((f32[1,1032,128]{2,1,0:T(8,128)S(1)}, f32[1,1032,128]{2,1,0:T(8,128)S(1)}, u32[]{:S(2)}, u32[]{:S(2)}) %collective-permute-start.11) | collective-permute-done | bytes 528416 | tf_op jit(solution)/shard_map/ppermute | solution.py:45
  359.5 3.1 multiply_reduce_fusion.1
  362.6 3.8 collective-permute-done.20
  377.4 2.9 copy.74
  (248 shorter events, 109.7 us)
Async XLA Ops:
  6.5 13.9 %copy-start.9 = (bf16[2,128,1296]{1,2,0:T(8,128)(2,1)S(1)}, bf16[2,128,1296]{1,2,0:T(8,128)(2,1)}, u32[]{:S(2)}) copy-start(bf16[2,128,1296]{1,2,0:T(8,128)(2,1)} %param.9) | copy-start | bytes 1990660
  6.5 28.4 %copy-start.26 = (f32[2,1280]{1,0:T(2,128)S(1)}, f32[2,1280]{1,0:T(2,128)}, u32[]{:S(2)}) copy-start(f32[2,1280]{1,0:T(2,128)} %param.11) | copy-start | bytes 30724
  6.5 28.4 %copy-start.21 = (f32[2,4,1280]{2,1,0:T(4,128)S(1)}, f32[2,4,1280]{2,1,0:T(4,128)}, u32[]{:S(2)}) copy-start(f32[2,4,1280]{2,1,0:T(4,128)} %param.10) | copy-start | bytes 122884
  6.5 103.2 %all-gather.3.cloned.1.call-start = ((), (), s32[]{:S(2)}) async-start(), calls=%async_computation | async-start | bytes 11280384 | tf_op jit(solution)/shard_map/all_gather | solution.py:92
  7.7 9.8 %collective-permute-start.3 = (bf16[128,1,1296]{0,2,1:T(8,128)(2,1)S(1)}, bf16[128,1,1296]{0,2,1:T(8,128)(2,1)S(1)}, u32[]{:S(2)}, u32[]{:S(2)}) collective-permute-start(bf16[128,1,1296]{0,2,1:T(8,128)(2,1)S(1)} %get-tuple-element.41), channel_id=1, source_target_pairs={{0,4},{4,0},{1,5},{5,1},{2,6},{6,2},{3,7},{7,3},{8,12},{12,8},{9,1... | collective-permute-start | bytes 995336 | tf_op jit(solution)/shard_map/ppermute | solution.py:85
  18.5 184.8 %all-gather.5.cloned.1.call-start = ((), (), s32[]{:S(2)}) async-start(), calls=%async_computation.1 | async-start | bytes 11280384 | tf_op jit(solution)/shard_map/all_gather | solution.py:92
  18.5 8.9 %collective-permute-start.12 = (bf16[128,1,1296]{0,2,1:T(8,128)(2,1)S(1)}, bf16[128,1,1296]{0,2,1:T(8,128)(2,1)S(1)}, u32[]{:S(2)}, u32[]{:S(2)}) collective-permute-start(bf16[128,1,1296]{0,2,1:T(8,128)(2,1)S(1)} %get-tuple-element.42), channel_id=1, source_target_pairs={{0,4},{4,0},{1,5},{5,1},{2,6},{6,2},{3,7},{7,3},{8,12},{12,8},{9,1... | collective-permute-start | bytes 995336 | tf_op jit(solution)/shard_map/ppermute | solution.py:85
  28.4 38.0 %collective-permute-start = (bf16[768,1024]{1,0:T(8,128)(2,1)}, bf16[768,1024]{1,0:T(8,128)(2,1)}, u32[]{:S(2)}, u32[]{:S(2)}) collective-permute-start(bf16[768,1024]{1,0:T(8,128)(2,1)} %param.8), channel_id=1, source_target_pairs={{0,1},{1,2},{2,3},{3,0},{4,5},{5,6},{6,7},{7,4},{8,9},{9,10},{10,1... | collective-permute-start | bytes 4718600 | tf_op jit(solution)/shard_map/ppermute | solution.py:175
  28.5 40.6 %collective-permute-start.1 = (bf16[768,1024]{1,0:T(8,128)(2,1)}, bf16[768,1024]{1,0:T(8,128)(2,1)S(1)}, u32[]{:S(2)}, u32[]{:S(2)}) collective-permute-start(bf16[768,1024]{1,0:T(8,128)(2,1)} %param.8), channel_id=1, source_target_pairs={{0,2},{1,3},{2,0},{3,1},{4,6},{5,7},{6,4},{7,5},{8,10},{9,11},{10,... | collective-permute-start | bytes 4718600 | tf_op jit(solution)/shard_map/ppermute | solution.py:175
  32.1 68.1 %collective-permute-start.2 = (bf16[768,1024]{1,0:T(8,128)(2,1)}, bf16[768,1024]{1,0:T(8,128)(2,1)S(1)}, u32[]{:S(2)}, u32[]{:S(2)}) collective-permute-start(bf16[768,1024]{1,0:T(8,128)(2,1)} %param.8), channel_id=1, source_target_pairs={{0,3},{1,0},{2,1},{3,2},{4,7},{5,4},{6,5},{7,6},{8,11},{9,8},{10,9... | collective-permute-start | bytes 4718600 | tf_op jit(solution)/shard_map/ppermute | solution.py:175
  125.8 19.3 %collective-permute-start.4 = (bf16[3,1,1280]{0,2,1:T(8,128)(2,1)S(1)}, bf16[3,1,1280]{0,2,1:T(8,128)(2,1)S(1)}, u32[]{:S(2)}, u32[]{:S(2)}) collective-permute-start(bf16[3,1,1280]{0,2,1:T(8,128)(2,1)S(1)} %slice.462), channel_id=1, source_target_pairs={{0,4},{4,8},{8,12},{12,16},{16,20},{20,24},{24,28},{28,32},{32,36}... | collective-permute-start | bytes 23048 | tf_op jit(solution)/shard_map/ppermute | solution.py:22
  225.1 46.6 %collective-permute-start.5 = (f32[1,1032,128]{2,1,0:T(8,128)}, f32[1,1032,128]{2,1,0:T(8,128)}, u32[]{:S(2)}, u32[]{:S(2)}) collective-permute-start(f32[1,1032,128]{2,1,0:T(8,128)} %select_maximum_fusion.5), channel_id=1, source_target_pairs={{0,4},{4,0},{1,5},{5,1},{2,6},{6,2},{3,7},{7,3},{8,12},{12,8},{9,1... | collective-permute-start | bytes 1585160 | tf_op jit(solution)/shard_map/ppermute | solution.py:45
  232.0 13.5 %collective-permute-start.13 = (bf16[3,1,1280]{0,2,1:T(8,128)(2,1)}, bf16[3,1,1280]{0,2,1:T(8,128)(2,1)}, u32[]{:S(2)}, u32[]{:S(2)}) collective-permute-start(bf16[3,1,1280]{0,2,1:T(8,128)(2,1)} %slice.501), channel_id=1, source_target_pairs={{0,4},{4,8},{8,12},{12,16},{16,20},{20,24},{24,28},{28,32},{32,36}... | collective-permute-start | bytes 23048 | tf_op jit(solution)/shard_map/ppermute | solution.py:22
  267.9 15.4 %collective-permute-start.14 = (f32[1,1032,128]{2,1,0:T(8,128)}, f32[1,1032,128]{2,1,0:T(8,128)}, u32[]{:S(2)}, u32[]{:S(2)}) collective-permute-start(f32[1,1032,128]{2,1,0:T(8,128)} %select_maximum_fusion.2), channel_id=1, source_target_pairs={{0,4},{4,0},{1,5},{5,1},{2,6},{6,2},{3,7},{7,3},{8,12},{12,8},{9,1... | collective-permute-start | bytes 1585160 | tf_op jit(solution)/shard_map/ppermute | solution.py:45
  269.3 8.1 %copy-start.29 = (f32[1,1,16]{2,1,0:T(1,128)S(1)}, f32[1,1,16]{2,1,0:T(1,128)}, u32[]{:S(2)}) copy-start(f32[1,1,16]{2,1,0:T(1,128)} %get-tuple-element.82) | copy-start | bytes 196
  269.3 8.8 %copy-start.18 = (f32[6,16,128]{2,1,0:T(8,128)S(1)}, f32[6,16,128]{2,1,0:T(8,128)}, u32[]{:S(2)}) copy-start(f32[6,16,128]{2,1,0:T(8,128)} %copy.59) | copy-start | bytes 147460
  269.3 8.8 %copy-start.19 = (f32[6,16,128]{2,1,0:T(8,128)S(1)}, f32[6,16,128]{2,1,0:T(8,128)}, u32[]{:S(2)}) copy-start(f32[6,16,128]{2,1,0:T(8,128)} %copy.61) | copy-start | bytes 147460
  269.3 8.8 %copy-start.23 = (pred[128,128]{1,0:T(8,128)(4,1)S(1)}, pred[128,128]{1,0:T(8,128)(4,1)}, u32[]{:S(2)}) copy-start(pred[128,128]{1,0:T(8,128)(4,1)} %iota_compare_fusion.1) | copy-start | bytes 49156
  285.8 10.9 %copy-start.2 = (bf16[6,128,1,1024]{1,3,0,2:T(8,128)(2,1)S(1)}, bf16[6,128,1,1024]{1,3,0,2:T(8,128)(2,1)}, u32[]{:S(2)}) copy-start(bf16[6,128,1,1024]{1,3,0,2:T(8,128)(2,1)} %copy.65) | copy-start | bytes 4718596
  285.9 10.9 %copy-start.20 = (f32[6,16,128]{2,1,0:T(8,128)S(1)}, f32[6,16,128]{2,1,0:T(8,128)}, u32[]{:S(2)}) copy-start(f32[6,16,128]{2,1,0:T(8,128)} %copy.69) | copy-start | bytes 147460
  286.3 23.6 %collective-permute-start.6 = (f32[1,1032,128]{2,1,0:T(8,128)S(1)}, f32[1,1032,128]{2,1,0:T(8,128)S(1)}, u32[]{:S(2)}, u32[]{:S(2)}) collective-permute-start(f32[1,1032,128]{2,1,0:T(8,128)S(1)} %select_maximum_fusion.4), channel_id=1, source_target_pairs={{0,24},{8,0},{16,8},{24,16},{1,25},{9,1},{17,9},{25,17},{2,26},{10... | collective-permute-start | bytes 1585160 | tf_op jit(solution)/shard_map/ppermute | solution.py:45
  287.2 25.3 %collective-permute-start.7 = (f32[1,1032,128]{2,1,0:T(8,128)S(1)}, f32[1,1032,128]{2,1,0:T(8,128)S(1)}, u32[]{:S(2)}, u32[]{:S(2)}) collective-permute-start(f32[1,1032,128]{2,1,0:T(8,128)S(1)} %select_maximum_fusion.4), channel_id=1, source_target_pairs={{0,16},{8,24},{16,0},{24,8},{1,17},{9,25},{17,1},{25,9},{2,18},{10... | collective-permute-start | bytes 1585160 | tf_op jit(solution)/shard_map/ppermute | solution.py:45
  288.8 26.3 %collective-permute-start.8 = (f32[1,1032,128]{2,1,0:T(8,128)S(1)}, f32[1,1032,128]{2,1,0:T(8,128)S(1)}, u32[]{:S(2)}, u32[]{:S(2)}) collective-permute-start(f32[1,1032,128]{2,1,0:T(8,128)S(1)} %select_maximum_fusion.4), channel_id=1, source_target_pairs={{0,8},{8,16},{16,24},{24,0},{1,9},{9,17},{17,25},{25,1},{2,10},{10... | collective-permute-start | bytes 1585160 | tf_op jit(solution)/shard_map/ppermute | solution.py:45
  289.3 34.7 %collective-permute-start.15 = (f32[1,1032,128]{2,1,0:T(8,128)S(1)}, f32[1,1032,128]{2,1,0:T(8,128)S(1)}, u32[]{:S(2)}, u32[]{:S(2)}) collective-permute-start(f32[1,1032,128]{2,1,0:T(8,128)S(1)} %select_maximum_fusion.1), channel_id=1, source_target_pairs={{0,24},{8,0},{16,8},{24,16},{1,25},{9,1},{17,9},{25,17},{2,26},{10... | collective-permute-start | bytes 1585160 | tf_op jit(solution)/shard_map/ppermute | solution.py:45
  292.1 34.2 %collective-permute-start.16 = (f32[1,1032,128]{2,1,0:T(8,128)S(1)}, f32[1,1032,128]{2,1,0:T(8,128)S(1)}, u32[]{:S(2)}, u32[]{:S(2)}) collective-permute-start(f32[1,1032,128]{2,1,0:T(8,128)S(1)} %select_maximum_fusion.1), channel_id=1, source_target_pairs={{0,16},{8,24},{16,0},{24,8},{1,17},{9,25},{17,1},{25,9},{2,18},{10... | collective-permute-start | bytes 1585160 | tf_op jit(solution)/shard_map/ppermute | solution.py:45
  309.9 24.2 %collective-permute-start.17 = (f32[1,1032,128]{2,1,0:T(8,128)S(1)}, f32[1,1032,128]{2,1,0:T(8,128)S(1)}, u32[]{:S(2)}, u32[]{:S(2)}) collective-permute-start(f32[1,1032,128]{2,1,0:T(8,128)S(1)} %select_maximum_fusion.1), channel_id=1, source_target_pairs={{0,8},{8,16},{16,24},{24,0},{1,9},{9,17},{17,25},{25,1},{2,10},{10... | collective-permute-start | bytes 1585160 | tf_op jit(solution)/shard_map/ppermute | solution.py:45
  315.6 40.7 %collective-permute-start.11 = (f32[1,1032,128]{2,1,0:T(8,128)S(1)}, f32[1,1032,128]{2,1,0:T(8,128)S(1)}, u32[]{:S(2)}, u32[]{:S(2)}) collective-permute-start(f32[1,1032,128]{2,1,0:T(8,128)S(1)} %select_maximum_fusion.3), channel_id=1, source_target_pairs={{0,96},{1,97},{2,98},{3,99},{4,100},{5,101},{6,102},{7,103},{8,104... | collective-permute-start | bytes 1585160 | tf_op jit(solution)/shard_map/ppermute | solution.py:45
  316.9 40.7 %collective-permute-start.10 = (f32[1,1032,128]{2,1,0:T(8,128)S(1)}, f32[1,1032,128]{2,1,0:T(8,128)S(1)}, u32[]{:S(2)}, u32[]{:S(2)}) collective-permute-start(f32[1,1032,128]{2,1,0:T(8,128)S(1)} %select_maximum_fusion.3), channel_id=1, source_target_pairs={{0,64},{32,96},{1,65},{33,97},{2,66},{34,98},{3,67},{35,99},{4,68}... | collective-permute-start | bytes 1585160 | tf_op jit(solution)/shard_map/ppermute | solution.py:45
  324.0 33.8 %collective-permute-start.9 = (f32[1,1032,128]{2,1,0:T(8,128)S(1)}, f32[1,1032,128]{2,1,0:T(8,128)S(1)}, u32[]{:S(2)}, u32[]{:S(2)}) collective-permute-start(f32[1,1032,128]{2,1,0:T(8,128)S(1)} %select_maximum_fusion.3), channel_id=1, source_target_pairs={{0,32},{32,64},{64,96},{1,33},{33,65},{65,97},{2,34},{34,66},{66,9... | collective-permute-start | bytes 1585160 | tf_op jit(solution)/shard_map/ppermute | solution.py:45
  334.8 31.6 %collective-permute-start.20 = (f32[1,1032,128]{2,1,0:T(8,128)S(1)}, f32[1,1032,128]{2,1,0:T(8,128)S(1)}, u32[]{:S(2)}, u32[]{:S(2)}) collective-permute-start(f32[1,1032,128]{2,1,0:T(8,128)S(1)} %select_maximum_fusion), channel_id=1, source_target_pairs={{0,96},{1,97},{2,98},{3,99},{4,100},{5,101},{6,102},{7,103},{8,104... | collective-permute-start | bytes 1585160 | tf_op jit(solution)/shard_map/ppermute | solution.py:45
  336.3 32.5 %collective-permute-start.19 = (f32[1,1032,128]{2,1,0:T(8,128)S(1)}, f32[1,1032,128]{2,1,0:T(8,128)S(1)}, u32[]{:S(2)}, u32[]{:S(2)}) collective-permute-start(f32[1,1032,128]{2,1,0:T(8,128)S(1)} %select_maximum_fusion), channel_id=1, source_target_pairs={{0,64},{32,96},{1,65},{33,97},{2,66},{34,98},{3,67},{35,99},{4,68}... | collective-permute-start | bytes 1585160 | tf_op jit(solution)/shard_map/ppermute | solution.py:45
  356.3 13.5 %collective-permute-start.18 = (f32[1,1032,128]{2,1,0:T(8,128)S(1)}, f32[1,1032,128]{2,1,0:T(8,128)S(1)}, u32[]{:S(2)}, u32[]{:S(2)}) collective-permute-start(f32[1,1032,128]{2,1,0:T(8,128)S(1)} %select_maximum_fusion), channel_id=1, source_target_pairs={{0,32},{32,64},{64,96},{1,33},{33,65},{65,97},{2,34},{34,66},{66,9... | collective-permute-start | bytes 1585160 | tf_op jit(solution)/shard_map/ppermute | solution.py:45
  (32 other events, 66.9 us)
Sparse Core Ops, SparseCore 0:
  18.6 91.0 all-gather.2
  111.8 91.3 all-gather.4

commit v9 on v7

--- a/solution.py
+++ b/solution.py
@@ -149,7 +149,6 @@
     partial_y = jnp.einsum(
         "qghij,qjghp->qighp", weights, x_all, preferred_element_type=jnp.float32
     )
-    partial_y = partial_y + d_skip[None, None, :, :, None] * x_all
 
     across = jnp.einsum(
         "qign,qghpn->qighp",
@@ -157,7 +156,7 @@
         states.astype(jnp.bfloat16),
         preferred_element_type=jnp.float32,
     )
-    activity = partial_y + jnp.exp(cumulative)[..., None] * across
+    activity = partial_y + jnp.exp(cumulative)[..., None] * across + d_skip[None, None, :, :, None] * x_all
     flat_act = activity.reshape(row_count, groups, GW)
     inv_rms = lax.rsqrt(jnp.mean(flat_act * flat_act, axis=-1, keepdims=True) + epsilon)
     normed = (flat_act * inv_rms * norm_gain[None]).astype(jnp.bfloat16)

time: 394 us -> 394 us (level)
  no operation moved by 1% of the time
where the time goes in v9:
time: 394 us; the launch traced here: 387 us
  waiting for transfers between devices  155 us (39%)
  local copies, waits for them, and re-layouts  67 us (17%)
  starting transfers between devices  50.8 us (13%)
  matrix products  50.1 us (13%)
  other arithmetic  49.5 us (13%)
  between operations  14.9 us (4%)
    ppermute x3, waiting for transfers between devices, per_device(): lax.ppermute(tokens, 'chan', [(i, (i + distance) % size) for i in range(s...  49.4 us
    all_gather x2, waiting for transfers between devices, mix_groups(): full_w = lax.all_gather(pair_w, SEQ[:2], axis=0, tiled=True)  45.7 us
    ppermute x14, waiting for transfers between devices, gather_level(): got = lax.ppermute(packed, axis, route)  41.2 us
    ppermute x14, starting transfers between devices, gather_level(): got = lax.ppermute(packed, axis, route)  34.1 us
    dot_general x2, matrix products, mix_groups(): jnp.einsum('td,dgc->tgc', gathered, full_w, preferred_element_type=jnp.fl...  27 us
    convert_element_type x2, other arithmetic, mix_groups(): inputs = jax.nn.silu(pre_act).astype(jnp.bfloat16)  16.1 us
    ppermute x2, waiting for transfers between devices, mix_groups(): lax.ppermute(rows_first, SEQ[2], [(i, (i + distance) % pair) for i in ran...  13.7 us
    dot_general x2, matrix products, mix_groups(): jnp.einsum('qghij,qjghp->qighp', weights, x_all, preferred_element_type=j...  10.8 us
  transfers between devices with their start and end apart: 23, of which 11 were waited for; matrix products, arithmetic and copies ran while one was open for 34% of the time, Pallas kernels for 0%

profile of v9, /device:TPU:22, one launch (start us, length us, event | category | flops | bytes accessed | tf_op | source)
XLA Modules:
  0.0 387.4 jit_solution(18386568598531957623)
XLA Ops:
  10.8 6.7 %collective-permute-done.3 = bf16[128,1,1296]{0,2,1:T(8,128)(2,1)S(1)} collective-permute-done((bf16[128,1,1296]{0,2,1:T(8,128)(2,1)S(1)}, bf16[128,1,1296]{0,2,1:T(8,128)(2,1)S(1)}, u32[]{:S(2)}, u32[]{:S(2)}) %collective-permute-start.3) | collective-permute-done | bytes 331808 | tf_op jit(solution)/shard_map/ppermute | solution.py:85
  20.5 7.0 %collective-permute-done.12 = bf16[128,1,1296]{0,2,1:T(8,128)(2,1)S(1)} collective-permute-done((bf16[128,1,1296]{0,2,1:T(8,128)(2,1)S(1)}, bf16[128,1,1296]{0,2,1:T(8,128)(2,1)S(1)}, u32[]{:S(2)}, u32[]{:S(2)}) %collective-permute-start.12) | collective-permute-done | bytes 331808 | tf_op jit(solution)/shard_map/ppermute | solution.py:85
  28.5 3.6 collective-permute-start.1
  32.1 2.9 collective-permute-start.2
  39.6 3.5 broadcast_in_dim.20
  46.7 19.7 %collective-permute-done = bf16[768,1024]{1,0:T(8,128)(2,1)} collective-permute-done((bf16[768,1024]{1,0:T(8,128)(2,1)}, bf16[768,1024]{1,0:T(8,128)(2,1)}, u32[]{:S(2)}, u32[]{:S(2)}) %collective-permute-start) | collective-permute-done | bytes 1572896 | tf_op jit(solution)/shard_map/ppermute | solution.py:173
  66.4 2.7 constant_dynamic-update-slice_fusion.26
  70.4 29.8 %collective-permute-done.2 = bf16[768,1024]{1,0:T(8,128)(2,1)S(1)} collective-permute-done((bf16[768,1024]{1,0:T(8,128)(2,1)}, bf16[768,1024]{1,0:T(8,128)(2,1)S(1)}, u32[]{:S(2)}, u32[]{:S(2)}) %collective-permute-start.2) | collective-permute-done | bytes 1572896 | tf_op jit(solution)/shard_map/ppermute | solution.py:173
  101.5 6.8 %all-gather.3.cloned.1.call-done = bf16[4096,1,1296]{0,2,1:T(8,128)(2,1)} async-done(((bf16[256,1,1296]{0,2,1:T(8,128)(2,1)}), bf16[4096,1,1296]{0,2,1:T(8,128)(2,1)}) %all-gather.3.cloned.1.call-update) | async-done | bytes 10616848 | tf_op jit(solution)/shard_map/all_gather | solution.py:92
  108.3 13.0 %fusion.87 = (bf16[768,1,1296]{0,2,1:T(8,128)(2,1)S(1)}, f32[768,1,1296]{0,2,1:T(8,128)S(1)}) fusion(bf16[768,4096]{1,0:T(8,128)(2,1)} %constant_dynamic-update-slice_fusion.24, bf16[4096,1,1296]{0,2,1:T(8,128)(2,1)} %all-gather.3.cloned.1.call-done), kind=kOutput, calls=%fused_computation.268 | convolution fusion | flops 8154722304 | bytes 22880256 | tf_op jit(solution)/shard_map/td,dgc->tgc/dot_general | solution.py:97
  121.7 3.6 collective-permute-start.4
  133.9 5.1 %collective-permute-done.4 = bf16[3,1,1280]{0,2,1:T(8,128)(2,1)S(1)} collective-permute-done((bf16[3,1,1280]{0,2,1:T(8,128)(2,1)S(1)}, bf16[3,1,1280]{0,2,1:T(8,128)(2,1)S(1)}, u32[]{:S(2)}, u32[]{:S(2)}) %collective-permute-start.4) | collective-permute-done | bytes 7712 | tf_op jit(solution)/shard_map/ppermute | solution.py:22
  138.9 6.1 %multiply_convert_fusion.3 = bf16[768,1,1280]{0,2,1:T(8,128)(2,1)} fusion(bf16[768,1,1280]{0,2,1:T(8,128)(2,1)S(1)} %slice.455, bf16[3,1,1280]{0,2,1:T(8,128)(2,1)S(1)} %collective-permute-done.4, f32[1280]{0:T(1024)} %get-tuple-element.9, f32[1280]{0:T(1024)} %get-tuple-element.10, f32[1280]{0:T(1024)} %get-tuple-element.11, f32[1280]{0:T(1024)} %get-tuple-element.12, ...), kind=kLoop, calls=%fused_computation.7 | loop fusion | flops 25559040 | bytes 3965440 | tf_op jit(solution)/shard_map/convert_element_type | solution.py:110
  145.0 4.0 %copy.54 = bf16[768,1,1280]{2,0,1:T(8,128)(2,1)} copy(bf16[768,1,1280]{0,2,1:T(8,128)(2,1)} %multiply_convert_fusion.3) | data formatting | bytes 3932160 | tf_op jit(solution)/shard_map/convert_element_type | solution.py:110
  149.0 3.1 slice_convert_fusion.1
  152.2 2.6 copy.55
  163.9 38.9 %all-gather.5.cloned.1.call-done = bf16[4096,1,1296]{0,2,1:T(8,128)(2,1)} async-done(((bf16[256,1,1296]{0,2,1:T(8,128)(2,1)}), bf16[4096,1,1296]{0,2,1:T(8,128)(2,1)}) %all-gather.5.cloned.1.call-update) | async-done | bytes 10616848 | tf_op jit(solution)/shard_map/all_gather | solution.py:92
  202.8 14.0 %fusion.88 = (bf16[768,1,1296]{0,2,1:T(8,128)(2,1)}, f32[768,1,1296]{0,2,1:T(8,128)S(1)}) fusion(bf16[768,4096]{1,0:T(8,128)(2,1)} %constant_dynamic-update-slice_fusion.24, bf16[4096,1,1296]{0,2,1:T(8,128)(2,1)} %all-gather.5.cloned.1.call-done), kind=kOutput, calls=%fused_computation.269 | convolution fusion | flops 8154722304 | bytes 22880256 | tf_op jit(solution)/shard_map/td,dgc->tgc/dot_general | solution.py:97
  227.9 2.6 collective-permute-start.13
  236.2 5.6 %fusion.10 = f32[6,16,64,128]{3,2,1,0:T(8,128)} fusion(bf16[6,128,16,64]{1,3,2,0:T(8,128)(2,1)} %bitcast.427, f32[6,16,128]{2,1,0:T(8,128)} %copy.59, f32[6,16,128]{2,1,0:T(8,128)} %copy.57, f32[6,128,128]{2,1,0:T(8,128)} %fusion.53, pred[128,128]{1,0:T(8,128)(4,1)} %iota_compare_fusion.1), kind=kOutput, calls=%fused_computation.10 | convolution fusion | flops 210763776 | bytes 5226496 | tf_op jit(solution)/shard_map/qghij,qjghp->qighp/dot_general | solution.py:149
  249.6 10.0 %multiply_convert_fusion.2 = bf16[768,1,1280]{0,2,1:T(8,128)(2,1)} fusion(bf16[768,1,1280]{0,2,1:T(8,128)(2,1)} %slice.492, bf16[3,1,1280]{0,2,1:T(8,128)(2,1)} %collective-permute-done.13, f32[1280]{0:T(1024)} %get-tuple-element.13, f32[1280]{0:T(1024)} %get-tuple-element.14, f32[1280]{0:T(1024)} %get-tuple-element.8, f32[1280]{0:T(1024)} %get-tuple-element.7, ...), kind=kLoop, calls=%fused_computation.6 | loop fusion | flops 25559040 | bytes 3965440 | tf_op jit(solution)/shard_map/convert_element_type | solution.py:110
  259.6 2.7 copy.64
  271.4 3.6 collective-permute-start.14
  275.9 3.6 copy.72
  279.6 5.2 %fusion.11 = f32[6,16,64,128]{3,2,1,0:T(8,128)S(1)} fusion(bf16[6,128,16,64]{1,3,2,0:T(8,128)(2,1)} %bitcast.429, f32[6,16,128]{2,1,0:T(8,128)} %copy.69, f32[6,16,128]{2,1,0:T(8,128)} %copy.67, f32[6,128,128]{2,1,0:T(8,128)S(1)} %copy-done.19, pred[128,128]{1,0:T(8,128)(4,1)} %iota_compare_fusion.1), kind=kOutput, calls=%fused_computation.11 | convolution fusion | flops 210763776 | bytes 5226496 | tf_op jit(solution)/shard_map/qghij,qjghp->qighp/dot_general | solution.py:149
  289.1 2.4 collective-permute-start.8
  297.6 18.1 %collective-permute-done.6 = f32[1,1032,128]{2,1,0:T(8,128)S(1)} collective-permute-done((f32[1,1032,128]{2,1,0:T(8,128)S(1)}, f32[1,1032,128]{2,1,0:T(8,128)S(1)}, u32[]{:S(2)}, u32[]{:S(2)}) %collective-permute-start.6) | collective-permute-done | bytes 528416 | tf_op jit(solution)/shard_map/ppermute | solution.py:45
  319.2 16.3 %collective-permute-done.15 = f32[1,1032,128]{2,1,0:T(8,128)S(1)} collective-permute-done((f32[1,1032,128]{2,1,0:T(8,128)S(1)}, f32[1,1032,128]{2,1,0:T(8,128)S(1)}, u32[]{:S(2)}, u32[]{:S(2)}) %collective-permute-start.15) | collective-permute-done | bytes 528416 | tf_op jit(solution)/shard_map/ppermute | solution.py:45
  340.1 16.7 %collective-permute-start.18 = (f32[1,1032,128]{2,1,0:T(8,128)S(1)}, f32[1,1032,128]{2,1,0:T(8,128)S(1)}, u32[]{:S(2)}, u32[]{:S(2)}) collective-permute-start(f32[1,1032,128]{2,1,0:T(8,128)S(1)} %select_maximum_fusion), channel_id=1, source_target_pairs={{0,32},{32,64},{64,96},{1,33},{33,65},{65,97},{2,34},{34,66},{66,9... | collective-permute-start | bytes 1585160 | tf_op jit(solution)/shard_map/ppermute | solution.py:45
  357.0 6.0 %collective-permute-done.9 = f32[1,1032,128]{2,1,0:T(8,128)S(1)} collective-permute-done((f32[1,1032,128]{2,1,0:T(8,128)S(1)}, f32[1,1032,128]{2,1,0:T(8,128)S(1)}, u32[]{:S(2)}, u32[]{:S(2)}) %collective-permute-start.9) | collective-permute-done | bytes 528416 | tf_op jit(solution)/shard_map/ppermute | solution.py:45
  364.2 3.1 multiply_reduce_fusion.1
  377.3 2.9 copy.74
  (264 shorter events, 100.7 us)
Async XLA Ops:
  6.5 13.9 %copy-start.11 = (bf16[2,128,1296]{1,2,0:T(8,128)(2,1)S(1)}, bf16[2,128,1296]{1,2,0:T(8,128)(2,1)}, u32[]{:S(2)}) copy-start(bf16[2,128,1296]{1,2,0:T(8,128)(2,1)} %param.9) | copy-start | bytes 1990660
  6.5 28.4 %copy-start.28 = (f32[2,1280]{1,0:T(2,128)S(1)}, f32[2,1280]{1,0:T(2,128)}, u32[]{:S(2)}) copy-start(f32[2,1280]{1,0:T(2,128)} %param.11) | copy-start | bytes 30724
  6.5 29.0 %copy-start.23 = (f32[2,4,1280]{2,1,0:T(4,128)S(1)}, f32[2,4,1280]{2,1,0:T(4,128)}, u32[]{:S(2)}) copy-start(f32[2,4,1280]{2,1,0:T(4,128)} %param.10) | copy-start | bytes 122884
  6.5 101.8 %all-gather.3.cloned.1.call-start = ((), (), s32[]{:S(2)}) async-start(), calls=%async_computation | async-start | bytes 11280384 | tf_op jit(solution)/shard_map/all_gather | solution.py:92
  7.7 9.8 %collective-permute-start.3 = (bf16[128,1,1296]{0,2,1:T(8,128)(2,1)S(1)}, bf16[128,1,1296]{0,2,1:T(8,128)(2,1)S(1)}, u32[]{:S(2)}, u32[]{:S(2)}) collective-permute-start(bf16[128,1,1296]{0,2,1:T(8,128)(2,1)S(1)} %get-tuple-element.39), channel_id=1, source_target_pairs={{0,4},{4,0},{1,5},{5,1},{2,6},{6,2},{3,7},{7,3},{8,12},{12,8},{9,1... | collective-permute-start | bytes 995336 | tf_op jit(solution)/shard_map/ppermute | solution.py:85
  18.5 184.3 %all-gather.5.cloned.1.call-start = ((), (), s32[]{:S(2)}) async-start(), calls=%async_computation.1 | async-start | bytes 11280384 | tf_op jit(solution)/shard_map/all_gather | solution.py:92
  18.5 8.9 %collective-permute-start.12 = (bf16[128,1,1296]{0,2,1:T(8,128)(2,1)S(1)}, bf16[128,1,1296]{0,2,1:T(8,128)(2,1)S(1)}, u32[]{:S(2)}, u32[]{:S(2)}) collective-permute-start(bf16[128,1,1296]{0,2,1:T(8,128)(2,1)S(1)} %get-tuple-element.40), channel_id=1, source_target_pairs={{0,4},{4,0},{1,5},{5,1},{2,6},{6,2},{3,7},{7,3},{8,12},{12,8},{9,1... | collective-permute-start | bytes 995336 | tf_op jit(solution)/shard_map/ppermute | solution.py:85
  28.4 38.0 %collective-permute-start = (bf16[768,1024]{1,0:T(8,128)(2,1)}, bf16[768,1024]{1,0:T(8,128)(2,1)}, u32[]{:S(2)}, u32[]{:S(2)}) collective-permute-start(bf16[768,1024]{1,0:T(8,128)(2,1)} %param.8), channel_id=1, source_target_pairs={{0,1},{1,2},{2,3},{3,0},{4,5},{5,6},{6,7},{7,4},{8,9},{9,10},{10,1... | collective-permute-start | bytes 4718600 | tf_op jit(solution)/shard_map/ppermute | solution.py:173
  28.5 40.6 %collective-permute-start.1 = (bf16[768,1024]{1,0:T(8,128)(2,1)}, bf16[768,1024]{1,0:T(8,128)(2,1)S(1)}, u32[]{:S(2)}, u32[]{:S(2)}) collective-permute-start(bf16[768,1024]{1,0:T(8,128)(2,1)} %param.8), channel_id=1, source_target_pairs={{0,2},{1,3},{2,0},{3,1},{4,6},{5,7},{6,4},{7,5},{8,10},{9,11},{10,... | collective-permute-start | bytes 4718600 | tf_op jit(solution)/shard_map/ppermute | solution.py:173
  32.1 68.1 %collective-permute-start.2 = (bf16[768,1024]{1,0:T(8,128)(2,1)}, bf16[768,1024]{1,0:T(8,128)(2,1)S(1)}, u32[]{:S(2)}, u32[]{:S(2)}) collective-permute-start(bf16[768,1024]{1,0:T(8,128)(2,1)} %param.8), channel_id=1, source_target_pairs={{0,3},{1,0},{2,1},{3,2},{4,7},{5,4},{6,5},{7,6},{8,11},{9,8},{10,9... | collective-permute-start | bytes 4718600 | tf_op jit(solution)/shard_map/ppermute | solution.py:173
  121.7 17.3 %collective-permute-start.4 = (bf16[3,1,1280]{0,2,1:T(8,128)(2,1)S(1)}, bf16[3,1,1280]{0,2,1:T(8,128)(2,1)S(1)}, u32[]{:S(2)}, u32[]{:S(2)}) collective-permute-start(bf16[3,1,1280]{0,2,1:T(8,128)(2,1)S(1)} %slice.454), channel_id=1, source_target_pairs={{0,4},{4,8},{8,12},{12,16},{16,20},{20,24},{24,28},{28,32},{32,36}... | collective-permute-start | bytes 23048 | tf_op jit(solution)/shard_map/ppermute | solution.py:22
  202.8 14.0 %copy-start.43 = (f32[16]{0:T(128)S(1)}, f32[16]{0:T(128)}, u32[]{:S(2)}) copy-start(f32[16]{0:T(128)} %get-tuple-element.93) | copy-start | bytes 196
  202.8 14.1 %copy-start.42 = (f32[16]{0:T(128)S(1)}, f32[16]{0:T(128)}, u32[]{:S(2)}) copy-start(f32[16]{0:T(128)} %get-tuple-element.91) | copy-start | bytes 196
  224.5 60.4 %collective-permute-start.5 = (f32[1,1032,128]{2,1,0:T(8,128)}, f32[1,1032,128]{2,1,0:T(8,128)}, u32[]{:S(2)}, u32[]{:S(2)}) collective-permute-start(f32[1,1032,128]{2,1,0:T(8,128)} %select_maximum_fusion.5), channel_id=1, source_target_pairs={{0,4},{4,0},{1,5},{5,1},{2,6},{6,2},{3,7},{7,3},{8,12},{12,8},{9,1... | collective-permute-start | bytes 1585160 | tf_op jit(solution)/shard_map/ppermute | solution.py:45
  227.9 21.7 %collective-permute-start.13 = (bf16[3,1,1280]{0,2,1:T(8,128)(2,1)}, bf16[3,1,1280]{0,2,1:T(8,128)(2,1)}, u32[]{:S(2)}, u32[]{:S(2)}) collective-permute-start(bf16[3,1,1280]{0,2,1:T(8,128)(2,1)} %slice.491), channel_id=1, source_target_pairs={{0,4},{4,8},{8,12},{12,16},{16,20},{20,24},{24,28},{28,32},{32,36}... | collective-permute-start | bytes 23048 | tf_op jit(solution)/shard_map/ppermute | solution.py:22
  271.4 20.1 %collective-permute-start.14 = (f32[1,1032,128]{2,1,0:T(8,128)}, f32[1,1032,128]{2,1,0:T(8,128)}, u32[]{:S(2)}, u32[]{:S(2)}) collective-permute-start(f32[1,1032,128]{2,1,0:T(8,128)} %select_maximum_fusion.2), channel_id=1, source_target_pairs={{0,4},{4,0},{1,5},{5,1},{2,6},{6,2},{3,7},{7,3},{8,12},{12,8},{9,1... | collective-permute-start | bytes 1585160 | tf_op jit(solution)/shard_map/ppermute | solution.py:45
  284.8 9.1 %copy-start.5 = (f32[1,16,64,128]{3,2,1,0:T(8,128)S(1)}, f32[1,16,64,128]{3,2,1,0:T(8,128)}, u32[]{:S(2)}) copy-start(f32[1,16,64,128]{3,2,1,0:T(8,128)} %copy-done.4) | copy-start | bytes 1572868
  284.8 9.1 %copy-start.8 = (f32[1,16,64,128]{3,2,1,0:T(8,128)S(1)}, f32[1,16,64,128]{3,2,1,0:T(8,128)}, u32[]{:S(2)}) copy-start(f32[1,16,64,128]{3,2,1,0:T(8,128)} %copy-done.7) | copy-start | bytes 1572868
  284.9 9.1 %copy-start.9 = (f32[6,16,64,128]{3,2,1,0:T(8,128)S(1)}, f32[6,16,64,128]{3,2,1,0:T(8,128)}, u32[]{:S(2)}) copy-start(f32[6,16,64,128]{3,2,1,0:T(8,128)} %constant_dynamic-update-slice_fusion.13) | copy-start | bytes 9437188
  288.1 9.3 %copy-start.6 = (f32[1,16,64,128]{3,2,1,0:T(8,128)S(1)}, f32[1,16,64,128]{3,2,1,0:T(8,128)}, u32[]{:S(2)}) copy-start(f32[1,16,64,128]{3,2,1,0:T(8,128)} %get-tuple-element.30) | copy-start | bytes 1572868
  288.2 27.6 %collective-permute-start.6 = (f32[1,1032,128]{2,1,0:T(8,128)S(1)}, f32[1,1032,128]{2,1,0:T(8,128)S(1)}, u32[]{:S(2)}, u32[]{:S(2)}) collective-permute-start(f32[1,1032,128]{2,1,0:T(8,128)S(1)} %select_maximum_fusion.4), channel_id=1, source_target_pairs={{0,24},{8,0},{16,8},{24,16},{1,25},{9,1},{17,9},{25,17},{2,26},{10... | collective-permute-start | bytes 1585160 | tf_op jit(solution)/shard_map/ppermute | solution.py:45
  288.2 27.5 %collective-permute-start.7 = (f32[1,1032,128]{2,1,0:T(8,128)S(1)}, f32[1,1032,128]{2,1,0:T(8,128)S(1)}, u32[]{:S(2)}, u32[]{:S(2)}) collective-permute-start(f32[1,1032,128]{2,1,0:T(8,128)S(1)} %select_maximum_fusion.4), channel_id=1, source_target_pairs={{0,16},{8,24},{16,0},{24,8},{1,17},{9,25},{17,1},{25,9},{2,18},{10... | collective-permute-start | bytes 1585160 | tf_op jit(solution)/shard_map/ppermute | solution.py:45
  289.1 27.5 %collective-permute-start.8 = (f32[1,1032,128]{2,1,0:T(8,128)S(1)}, f32[1,1032,128]{2,1,0:T(8,128)S(1)}, u32[]{:S(2)}, u32[]{:S(2)}) collective-permute-start(f32[1,1032,128]{2,1,0:T(8,128)S(1)} %select_maximum_fusion.4), channel_id=1, source_target_pairs={{0,8},{8,16},{16,24},{24,0},{1,9},{9,17},{17,25},{25,1},{2,10},{10... | collective-permute-start | bytes 1585160 | tf_op jit(solution)/shard_map/ppermute | solution.py:45
  294.3 41.2 %collective-permute-start.15 = (f32[1,1032,128]{2,1,0:T(8,128)S(1)}, f32[1,1032,128]{2,1,0:T(8,128)S(1)}, u32[]{:S(2)}, u32[]{:S(2)}) collective-permute-start(f32[1,1032,128]{2,1,0:T(8,128)S(1)} %select_maximum_fusion.1), channel_id=1, source_target_pairs={{0,24},{8,0},{16,8},{24,16},{1,25},{9,1},{17,9},{25,17},{2,26},{10... | collective-permute-start | bytes 1585160 | tf_op jit(solution)/shard_map/ppermute | solution.py:45
  295.2 42.1 %collective-permute-start.16 = (f32[1,1032,128]{2,1,0:T(8,128)S(1)}, f32[1,1032,128]{2,1,0:T(8,128)S(1)}, u32[]{:S(2)}, u32[]{:S(2)}) collective-permute-start(f32[1,1032,128]{2,1,0:T(8,128)S(1)} %select_maximum_fusion.1), channel_id=1, source_target_pairs={{0,16},{8,24},{16,0},{24,8},{1,17},{9,25},{17,1},{25,9},{2,18},{10... | collective-permute-start | bytes 1585160 | tf_op jit(solution)/shard_map/ppermute | solution.py:45
  315.7 21.7 %collective-permute-start.17 = (f32[1,1032,128]{2,1,0:T(8,128)S(1)}, f32[1,1032,128]{2,1,0:T(8,128)S(1)}, u32[]{:S(2)}, u32[]{:S(2)}) collective-permute-start(f32[1,1032,128]{2,1,0:T(8,128)S(1)} %select_maximum_fusion.1), channel_id=1, source_target_pairs={{0,8},{8,16},{16,24},{24,0},{1,9},{9,17},{17,25},{25,1},{2,10},{10... | collective-permute-start | bytes 1585160 | tf_op jit(solution)/shard_map/ppermute | solution.py:45
  317.2 22.9 %collective-permute-start.11 = (f32[1,1032,128]{2,1,0:T(8,128)S(1)}, f32[1,1032,128]{2,1,0:T(8,128)S(1)}, u32[]{:S(2)}, u32[]{:S(2)}) collective-permute-start(f32[1,1032,128]{2,1,0:T(8,128)S(1)} %select_maximum_fusion.3), channel_id=1, source_target_pairs={{0,96},{1,97},{2,98},{3,99},{4,100},{5,101},{6,102},{7,103},{8,104... | collective-permute-start | bytes 1585160 | tf_op jit(solution)/shard_map/ppermute | solution.py:45
  317.9 39.0 %collective-permute-start.10 = (f32[1,1032,128]{2,1,0:T(8,128)S(1)}, f32[1,1032,128]{2,1,0:T(8,128)S(1)}, u32[]{:S(2)}, u32[]{:S(2)}) collective-permute-start(f32[1,1032,128]{2,1,0:T(8,128)S(1)} %select_maximum_fusion.3), channel_id=1, source_target_pairs={{0,64},{32,96},{1,65},{33,97},{2,66},{34,98},{3,67},{35,99},{4,68}... | collective-permute-start | bytes 1585160 | tf_op jit(solution)/shard_map/ppermute | solution.py:45
  335.4 27.5 %collective-permute-start.9 = (f32[1,1032,128]{2,1,0:T(8,128)S(1)}, f32[1,1032,128]{2,1,0:T(8,128)S(1)}, u32[]{:S(2)}, u32[]{:S(2)}) collective-permute-start(f32[1,1032,128]{2,1,0:T(8,128)S(1)} %select_maximum_fusion.3), channel_id=1, source_target_pairs={{0,32},{32,64},{64,96},{1,33},{33,65},{65,97},{2,34},{34,66},{66,9... | collective-permute-start | bytes 1585160 | tf_op jit(solution)/shard_map/ppermute | solution.py:45
  338.1 32.1 %collective-permute-start.20 = (f32[1,1032,128]{2,1,0:T(8,128)S(1)}, f32[1,1032,128]{2,1,0:T(8,128)S(1)}, u32[]{:S(2)}, u32[]{:S(2)}) collective-permute-start(f32[1,1032,128]{2,1,0:T(8,128)S(1)} %select_maximum_fusion), channel_id=1, source_target_pairs={{0,96},{1,97},{2,98},{3,99},{4,100},{5,101},{6,102},{7,103},{8,104... | collective-permute-start | bytes 1585160 | tf_op jit(solution)/shard_map/ppermute | solution.py:45
  338.8 31.5 %collective-permute-start.19 = (f32[1,1032,128]{2,1,0:T(8,128)S(1)}, f32[1,1032,128]{2,1,0:T(8,128)S(1)}, u32[]{:S(2)}, u32[]{:S(2)}) collective-permute-start(f32[1,1032,128]{2,1,0:T(8,128)S(1)} %select_maximum_fusion), channel_id=1, source_target_pairs={{0,64},{32,96},{1,65},{33,97},{2,66},{34,98},{3,67},{35,99},{4,68}... | collective-permute-start | bytes 1585160 | tf_op jit(solution)/shard_map/ppermute | solution.py:45
  340.1 30.2 %collective-permute-start.18 = (f32[1,1032,128]{2,1,0:T(8,128)S(1)}, f32[1,1032,128]{2,1,0:T(8,128)S(1)}, u32[]{:S(2)}, u32[]{:S(2)}) collective-permute-start(f32[1,1032,128]{2,1,0:T(8,128)S(1)} %select_maximum_fusion), channel_id=1, source_target_pairs={{0,32},{32,64},{64,96},{1,33},{33,65},{65,97},{2,34},{34,66},{66,9... | collective-permute-start | bytes 1585160 | tf_op jit(solution)/shard_map/ppermute | solution.py:45
  (43 other events, 151.6 us)
Sparse Core Ops, SparseCore 0:
  18.6 89.6 all-gather.2
  110.4 92.3 all-gather.4

commit v10 on v7

--- a/solution.py
+++ b/solution.py
@@ -71,27 +71,33 @@
     return result[1]
 
 
-def mix_groups(gathered, w_in, conv_w, conv_b, dt_bias, a_log, d_skip, norm_gain, after):
-    groups = w_in.shape[0]
+def pair_rows(w_in):
+    rows_first = jnp.transpose(w_in, (1, 0, 2))
+    if not isinstance(SEQ, tuple):
+        return rows_first
+    pair = lax.axis_size(SEQ[2])
+    slot = lax.axis_index(SEQ[2])
+    piece = rows_first.shape[0]
+    pair_w = jnp.zeros((piece * pair,) + rows_first.shape[1:], rows_first.dtype)
+    for distance in range(pair):
+        if distance:
+            rows = lax.ppermute(
+                rows_first, SEQ[2], [(i, (i + distance) % pair) for i in range(pair)]
+            )
+        else:
+            rows = rows_first
+        source = (slot - distance) % pair
+        pair_w = lax.dynamic_update_slice(pair_w, rows, (source * piece, 0, 0))
+    return pair_w
+
+
+def mix_groups(gathered, pair_w, conv_w, conv_b, dt_bias, a_log, d_skip, norm_gain, after):
+    groups = pair_w.shape[1]
     row_count = gathered.shape[0]
-    rows_first = jnp.transpose(w_in, (1, 0, 2))
     if isinstance(SEQ, tuple):
-        pair = lax.axis_size(SEQ[2])
-        slot = lax.axis_index(SEQ[2])
-        piece = rows_first.shape[0]
-        pair_w = jnp.zeros((piece * pair,) + rows_first.shape[1:], rows_first.dtype)
-        for distance in range(pair):
-            if distance:
-                rows = lax.ppermute(
-                    rows_first, SEQ[2], [(i, (i + distance) % pair) for i in range(pair)]
-                )
-            else:
-                rows = rows_first
-            source = (slot - distance) % pair
-            pair_w = lax.dynamic_update_slice(pair_w, rows, (source * piece, 0, 0))
         full_w = lax.all_gather(pair_w, SEQ[:2], axis=0, tiled=True)
     else:
-        full_w = lax.all_gather(rows_first, SEQ, axis=0, tiled=True)
+        full_w = lax.all_gather(pair_w, SEQ, axis=0, tiled=True)
     if after is not None:
         full_w, _ = lax.optimization_barrier((full_w, after))
     projected = jnp.einsum(
@@ -180,10 +186,11 @@
         gathered = lax.dynamic_update_slice(gathered, piece, (0, source * width))
     outputs = []
     after = None
+    pair_w = pair_rows(w_in)
     for g in range(w_in.shape[0]):
         one = slice(g, g + 1)
         normed, after = mix_groups(
-            gathered, w_in[one], conv_w[one], conv_b[one], dt_bias[one],
+            gathered, pair_w[:, one], conv_w[one], conv_b[one], dt_bias[one],
             a_log[one], d_skip[one], norm_gain[one], after,
         )
         outputs.append(normed)

time: 394 us -> 401 us (1.018)
  waiting for transfers between devices: 155 us -> 163 us
    all_gather x2, waiting for transfers between devices: 45.7 us -> 55 us  [mix_groups(): full_w = lax.all_gather(pair_w, SEQ[:2], axis=0, tiled=True)]
    unnamed x116 -> x110, local copies, waits for them, and re-layouts: 10.3 us -> 8.6 us
    ppermute x2 -> x1, waiting for transfers between devices: 13.7 us -> 13.6 us  [pair_rows(): lax.ppermute(rows_first, SEQ[2], [(i, (i + distance) % pair) for i in ran...]
  transfers between devices with their start and end apart: 23 -> 22, of which waited for: 11 -> 10; matrix products, arithmetic and copies ran while one was open for 34% -> 34% of each run, Pallas kernels for 0% -> 0%
where the time goes in v10:
time: 401 us; the launch traced here: 394 us
  waiting for transfers between devices  163 us (41%)
  local copies, waits for them, and re-layouts  67.1 us (17%)
  matrix products  50.1 us (12%)
  other arithmetic  49.7 us (12%)
  starting transfers between devices  49 us (12%)
  between operations  14.9 us (4%)
    all_gather x2, waiting for transfers between devices, mix_groups(): full_w = lax.all_gather(pair_w, SEQ[:2], axis=0, tiled=True)  55 us
    ppermute x3, waiting for transfers between devices, per_device(): lax.ppermute(tokens, 'chan', [(i, (i + distance) % size) for i in range(s...  47.6 us
    ppermute x14, waiting for transfers between devices, gather_level(): got = lax.ppermute(packed, axis, route)  41.2 us
    ppermute x14, starting transfers between devices, gather_level(): got = lax.ppermute(packed, axis, route)  34.1 us
    dot_general x2, matrix products, mix_groups(): jnp.einsum('td,dgc->tgc', gathered, full_w, preferred_element_type=jnp.fl...  27 us
    convert_element_type x2, other arithmetic, mix_groups(): inputs = jax.nn.silu(pre_act).astype(jnp.bfloat16)  16.4 us
    ppermute x1, waiting for transfers between devices, pair_rows(): lax.ppermute(rows_first, SEQ[2], [(i, (i + distance) % pair) for i in ran...  13.6 us
    dot_general x2, matrix products, mix_groups(): jnp.einsum('qghij,qjghp->qighp', weights, x_all, preferred_element_type=j...  10.8 us
  transfers between devices with their start and end apart: 22, of which 10 were waited for; matrix products, arithmetic and copies ran while one was open for 34% of the time, Pallas kernels for 0%

profile of v10, /device:TPU:22, one launch (start us, length us, event | category | flops | bytes accessed | tf_op | source)
XLA Modules:
  0.0 394.0 jit_solution(7321338975399936912)
XLA Ops:
  10.0 13.6 %collective-permute-done.3 = bf16[128,2,1296]{0,2,1:T(8,128)(2,1)S(1)} collective-permute-done((bf16[128,2,1296]{0,2,1:T(8,128)(2,1)}, bf16[128,2,1296]{0,2,1:T(8,128)(2,1)S(1)}, u32[]{:S(2)}, u32[]{:S(2)}) %collective-permute-start.3) | collective-permute-done | bytes 663584 | tf_op jit(solution)/shard_map/ppermute | solution.py:84
  25.7 3.8 collective-permute-start.1
  29.5 2.9 collective-permute-start.2
  37.1 3.5 broadcast_in_dim.24
  44.2 19.0 %collective-permute-done = bf16[768,1024]{1,0:T(8,128)(2,1)} collective-permute-done((bf16[768,1024]{1,0:T(8,128)(2,1)S(1)}, bf16[768,1024]{1,0:T(8,128)(2,1)}, u32[]{:S(2)}, u32[]{:S(2)}) %collective-permute-start) | collective-permute-done | bytes 1572896 | tf_op jit(solution)/shard_map/ppermute | solution.py:180
  63.2 2.7 constant_dynamic-update-slice_fusion.24
  65.9 2.8 constant_dynamic-update-slice_fusion.23
  68.7 28.6 %collective-permute-done.2 = bf16[768,1024]{1,0:T(8,128)(2,1)S(1)} collective-permute-done((bf16[768,1024]{1,0:T(8,128)(2,1)S(1)}, bf16[768,1024]{1,0:T(8,128)(2,1)S(1)}, u32[]{:S(2)}, u32[]{:S(2)}) %collective-permute-start.2) | collective-permute-done | bytes 1572896 | tf_op jit(solution)/shard_map/ppermute | solution.py:180
  98.7 16.0 %all-gather.3.cloned.1.call-done = bf16[4096,1,1296]{0,2,1:T(8,128)(2,1)} async-done(((bf16[256,1,1296]{0,2,1:T(8,128)(2,1)}), bf16[4096,1,1296]{0,2,1:T(8,128)(2,1)}) %all-gather.3.cloned.1.call-update) | async-done | bytes 10616848 | tf_op jit(solution)/shard_map/all_gather | solution.py:98
  114.7 13.0 %fusion.86 = (bf16[768,1,1296]{0,2,1:T(8,128)(2,1)S(1)}, f32[768,1,1296]{0,2,1:T(8,128)S(1)}) fusion(bf16[768,4096]{1,0:T(8,128)(2,1)} %constant_dynamic-update-slice_fusion.22, bf16[4096,1,1296]{0,2,1:T(8,128)(2,1)} %all-gather.3.cloned.1.call-done), kind=kOutput, calls=%fused_computation.265 | convolution fusion | flops 8154722304 | bytes 22880256 | tf_op jit(solution)/shard_map/td,dgc->tgc/dot_general | solution.py:103
  128.1 3.6 collective-permute-start.4
  140.3 5.1 %collective-permute-done.4 = bf16[3,1,1280]{0,2,1:T(8,128)(2,1)S(1)} collective-permute-done((bf16[3,1,1280]{0,2,1:T(8,128)(2,1)S(1)}, bf16[3,1,1280]{0,2,1:T(8,128)(2,1)S(1)}, u32[]{:S(2)}, u32[]{:S(2)}) %collective-permute-start.4) | collective-permute-done | bytes 7712 | tf_op jit(solution)/shard_map/ppermute | solution.py:22
  145.4 6.1 %multiply_convert_fusion.3 = bf16[768,1,1280]{0,2,1:T(8,128)(2,1)} fusion(bf16[768,1,1280]{0,2,1:T(8,128)(2,1)S(1)} %slice.456, bf16[3,1,1280]{0,2,1:T(8,128)(2,1)S(1)} %collective-permute-done.4, f32[1280]{0:T(1024)} %get-tuple-element.9, f32[1280]{0:T(1024)} %get-tuple-element.10, f32[1280]{0:T(1024)} %get-tuple-element.11, f32[1280]{0:T(1024)} %get-tuple-element.12, ...), kind=kLoop, calls=%fused_computation.7 | loop fusion | flops 25559040 | bytes 3965440 | tf_op jit(solution)/shard_map/convert_element_type | solution.py:116
  151.5 4.0 %copy.54 = bf16[768,1,1280]{2,0,1:T(8,128)(2,1)} copy(bf16[768,1,1280]{0,2,1:T(8,128)(2,1)} %multiply_convert_fusion.3) | data formatting | bytes 3932160 | tf_op jit(solution)/shard_map/convert_element_type | solution.py:116
  155.5 3.1 slice_convert_fusion.1
  158.6 2.6 copy.55
  170.3 39.0 %all-gather.5.cloned.1.call-done = bf16[4096,1,1296]{0,2,1:T(8,128)(2,1)} async-done(((bf16[256,1,1296]{0,2,1:T(8,128)(2,1)}), bf16[4096,1,1296]{0,2,1:T(8,128)(2,1)}) %all-gather.5.cloned.1.call-update) | async-done | bytes 10616848 | tf_op jit(solution)/shard_map/all_gather | solution.py:98
  209.3 14.0 %fusion.87 = (bf16[768,1,1296]{0,2,1:T(8,128)(2,1)}, f32[768,1,1296]{0,2,1:T(8,128)S(1)}) fusion(bf16[768,4096]{1,0:T(8,128)(2,1)} %constant_dynamic-update-slice_fusion.22, bf16[4096,1,1296]{0,2,1:T(8,128)(2,1)} %all-gather.5.cloned.1.call-done), kind=kOutput, calls=%fused_computation.266 | convolution fusion | flops 8154722304 | bytes 22880256 | tf_op jit(solution)/shard_map/td,dgc->tgc/dot_general | solution.py:103
  234.4 2.6 collective-permute-start.12
  242.6 5.6 %fusion.10 = f32[6,16,64,128]{3,2,1,0:T(8,128)} fusion(bf16[6,128,16,64]{1,3,2,0:T(8,128)(2,1)} %bitcast.421, f32[6,16,128]{2,1,0:T(8,128)} %copy.59, f32[6,16,128]{2,1,0:T(8,128)} %copy.57, f32[6,128,128]{2,1,0:T(8,128)} %fusion.51, pred[128,128]{1,0:T(8,128)(4,1)} %iota_compare_fusion.1), kind=kOutput, calls=%fused_computation.10 | convolution fusion | flops 210763776 | bytes 5226496 | tf_op jit(solution)/shard_map/qghij,qjghp->qighp/dot_general | solution.py:155
  255.9 10.3 %multiply_convert_fusion.2 = bf16[768,1,1280]{0,2,1:T(8,128)(2,1)} fusion(bf16[768,1,1280]{0,2,1:T(8,128)(2,1)} %slice.494, bf16[3,1,1280]{0,2,1:T(8,128)(2,1)} %collective-permute-done.12, f32[1280]{0:T(1024)} %get-tuple-element.13, f32[1280]{0:T(1024)} %get-tuple-element.14, f32[1280]{0:T(1024)} %get-tuple-element.8, f32[1280]{0:T(1024)} %get-tuple-element.7, ...), kind=kLoop, calls=%fused_computation.6 | loop fusion | flops 25559040 | bytes 3965440 | tf_op jit(solution)/shard_map/convert_element_type | solution.py:116
  266.2 2.7 copy.64
  278.1 3.6 collective-permute-start.13
  282.6 3.6 copy.70
  286.3 5.2 %fusion.11 = f32[6,16,64,128]{3,2,1,0:T(8,128)S(1)} fusion(bf16[6,128,16,64]{1,3,2,0:T(8,128)(2,1)} %bitcast.423, f32[6,16,128]{2,1,0:T(8,128)} %copy.69, f32[6,16,128]{2,1,0:T(8,128)} %copy.67, f32[6,128,128]{2,1,0:T(8,128)S(1)} %copy-done.16, pred[128,128]{1,0:T(8,128)(4,1)} %iota_compare_fusion.1), kind=kOutput, calls=%fused_computation.11 | convolution fusion | flops 210763776 | bytes 5226496 | tf_op jit(solution)/shard_map/qghij,qjghp->qighp/dot_general | solution.py:155
  295.7 2.4 collective-permute-start.8
  304.2 18.1 %collective-permute-done.6 = f32[1,1032,128]{2,1,0:T(8,128)S(1)} collective-permute-done((f32[1,1032,128]{2,1,0:T(8,128)S(1)}, f32[1,1032,128]{2,1,0:T(8,128)S(1)}, u32[]{:S(2)}, u32[]{:S(2)}) %collective-permute-start.6) | collective-permute-done | bytes 528416 | tf_op jit(solution)/shard_map/ppermute | solution.py:45
  325.8 16.3 %collective-permute-done.14 = f32[1,1032,128]{2,1,0:T(8,128)S(1)} collective-permute-done((f32[1,1032,128]{2,1,0:T(8,128)S(1)}, f32[1,1032,128]{2,1,0:T(8,128)S(1)}, u32[]{:S(2)}, u32[]{:S(2)}) %collective-permute-start.14) | collective-permute-done | bytes 528416 | tf_op jit(solution)/shard_map/ppermute | solution.py:45
  346.7 16.7 %collective-permute-start.17 = (f32[1,1032,128]{2,1,0:T(8,128)S(1)}, f32[1,1032,128]{2,1,0:T(8,128)S(1)}, u32[]{:S(2)}, u32[]{:S(2)}) collective-permute-start(f32[1,1032,128]{2,1,0:T(8,128)S(1)} %select_maximum_fusion), channel_id=1, source_target_pairs={{0,32},{32,64},{64,96},{1,33},{33,65},{65,97},{2,34},{34,66},{66,9... | collective-permute-start | bytes 1585160 | tf_op jit(solution)/shard_map/ppermute | solution.py:45
  363.6 6.0 %collective-permute-done.9 = f32[1,1032,128]{2,1,0:T(8,128)S(1)} collective-permute-done((f32[1,1032,128]{2,1,0:T(8,128)S(1)}, f32[1,1032,128]{2,1,0:T(8,128)S(1)}, u32[]{:S(2)}, u32[]{:S(2)}) %collective-permute-start.9) | collective-permute-done | bytes 528416 | tf_op jit(solution)/shard_map/ppermute | solution.py:45
  370.8 3.1 multiply_reduce_fusion.1
  383.9 2.9 copy.74
  (253 shorter events, 96.7 us)
Async XLA Ops:
  6.5 108.2 %all-gather.3.cloned.1.call-start = ((), (), s32[]{:S(2)}) async-start(), calls=%async_computation | async-start | bytes 11280384 | tf_op jit(solution)/shard_map/all_gather | solution.py:98
  6.5 17.0 %collective-permute-start.3 = (bf16[128,2,1296]{0,2,1:T(8,128)(2,1)}, bf16[128,2,1296]{0,2,1:T(8,128)(2,1)S(1)}, u32[]{:S(2)}, u32[]{:S(2)}) collective-permute-start(bf16[128,2,1296]{0,2,1:T(8,128)(2,1)} %bitcast.454), channel_id=1, source_target_pairs={{0,4},{4,0},{1,5},{5,1},{2,6},{6,2},{3,7},{7,3},{8,12},{12,8},{9,1... | collective-permute-start | bytes 1990664 | tf_op jit(solution)/shard_map/ppermute | solution.py:84
  8.5 17.1 %copy-start.13 = (bf16[768,1024]{1,0:T(8,128)(2,1)S(1)}, bf16[768,1024]{1,0:T(8,128)(2,1)}, u32[]{:S(2)}) copy-start(bf16[768,1024]{1,0:T(8,128)(2,1)} %param.8) | copy-start | bytes 4718596
  8.6 23.8 %copy-start.25 = (f32[2,1280]{1,0:T(2,128)S(1)}, f32[2,1280]{1,0:T(2,128)}, u32[]{:S(2)}) copy-start(f32[2,1280]{1,0:T(2,128)} %param.11) | copy-start | bytes 30724
  8.6 24.5 %copy-start.20 = (f32[2,4,1280]{2,1,0:T(4,128)S(1)}, f32[2,4,1280]{2,1,0:T(4,128)}, u32[]{:S(2)}) copy-start(f32[2,4,1280]{2,1,0:T(4,128)} %param.10) | copy-start | bytes 122884
  24.9 184.3 %all-gather.5.cloned.1.call-start = ((), (), s32[]{:S(2)}) async-start(), calls=%async_computation.1 | async-start | bytes 11280384 | tf_op jit(solution)/shard_map/all_gather | solution.py:98
  25.7 37.5 %collective-permute-start = (bf16[768,1024]{1,0:T(8,128)(2,1)S(1)}, bf16[768,1024]{1,0:T(8,128)(2,1)}, u32[]{:S(2)}, u32[]{:S(2)}) collective-permute-start(bf16[768,1024]{1,0:T(8,128)(2,1)S(1)} %copy-done.13), channel_id=1, source_target_pairs={{0,1},{1,2},{2,3},{3,0},{4,5},{5,6},{6,7},{7,4},{8,9},{9,10},{10,1... | collective-permute-start | bytes 4718600 | tf_op jit(solution)/shard_map/ppermute | solution.py:180
  25.7 40.2 %collective-permute-start.1 = (bf16[768,1024]{1,0:T(8,128)(2,1)S(1)}, bf16[768,1024]{1,0:T(8,128)(2,1)}, u32[]{:S(2)}, u32[]{:S(2)}) collective-permute-start(bf16[768,1024]{1,0:T(8,128)(2,1)S(1)} %copy-done.13), channel_id=1, source_target_pairs={{0,2},{1,3},{2,0},{3,1},{4,6},{5,7},{6,4},{7,5},{8,10},{9,11},{10,... | collective-permute-start | bytes 4718600 | tf_op jit(solution)/shard_map/ppermute | solution.py:180
  29.5 67.8 %collective-permute-start.2 = (bf16[768,1024]{1,0:T(8,128)(2,1)S(1)}, bf16[768,1024]{1,0:T(8,128)(2,1)S(1)}, u32[]{:S(2)}, u32[]{:S(2)}) collective-permute-start(bf16[768,1024]{1,0:T(8,128)(2,1)S(1)} %copy-done.13), channel_id=1, source_target_pairs={{0,3},{1,0},{2,1},{3,2},{4,7},{5,4},{6,5},{7,6},{8,11},{9,8},{10,9... | collective-permute-start | bytes 4718600 | tf_op jit(solution)/shard_map/ppermute | solution.py:180
  128.1 17.3 %collective-permute-start.4 = (bf16[3,1,1280]{0,2,1:T(8,128)(2,1)S(1)}, bf16[3,1,1280]{0,2,1:T(8,128)(2,1)S(1)}, u32[]{:S(2)}, u32[]{:S(2)}) collective-permute-start(bf16[3,1,1280]{0,2,1:T(8,128)(2,1)S(1)} %slice.455), channel_id=1, source_target_pairs={{0,4},{4,8},{8,12},{12,16},{16,20},{20,24},{24,28},{28,32},{32,36}... | collective-permute-start | bytes 23048 | tf_op jit(solution)/shard_map/ppermute | solution.py:22
  209.2 14.0 %copy-start.40 = (f32[16]{0:T(128)S(1)}, f32[16]{0:T(128)}, u32[]{:S(2)}) copy-start(f32[16]{0:T(128)} %get-tuple-element.93) | copy-start | bytes 196
  209.2 14.1 %copy-start.39 = (f32[16]{0:T(128)S(1)}, f32[16]{0:T(128)}, u32[]{:S(2)}) copy-start(f32[16]{0:T(128)} %get-tuple-element.91) | copy-start | bytes 196
  231.0 60.6 %collective-permute-start.5 = (f32[1,1032,128]{2,1,0:T(8,128)}, f32[1,1032,128]{2,1,0:T(8,128)}, u32[]{:S(2)}, u32[]{:S(2)}) collective-permute-start(f32[1,1032,128]{2,1,0:T(8,128)} %select_maximum_fusion.5), channel_id=1, source_target_pairs={{0,4},{4,0},{1,5},{5,1},{2,6},{6,2},{3,7},{7,3},{8,12},{12,8},{9,1... | collective-permute-start | bytes 1585160 | tf_op jit(solution)/shard_map/ppermute | solution.py:45
  234.4 21.6 %collective-permute-start.12 = (bf16[3,1,1280]{0,2,1:T(8,128)(2,1)}, bf16[3,1,1280]{0,2,1:T(8,128)(2,1)}, u32[]{:S(2)}, u32[]{:S(2)}) collective-permute-start(bf16[3,1,1280]{0,2,1:T(8,128)(2,1)} %slice.493), channel_id=1, source_target_pairs={{0,4},{4,8},{8,12},{12,16},{16,20},{20,24},{24,28},{28,32},{32,36}... | collective-permute-start | bytes 23048 | tf_op jit(solution)/shard_map/ppermute | solution.py:22
  278.1 20.0 %collective-permute-start.13 = (f32[1,1032,128]{2,1,0:T(8,128)}, f32[1,1032,128]{2,1,0:T(8,128)}, u32[]{:S(2)}, u32[]{:S(2)}) collective-permute-start(f32[1,1032,128]{2,1,0:T(8,128)} %select_maximum_fusion.2), channel_id=1, source_target_pairs={{0,4},{4,0},{1,5},{5,1},{2,6},{6,2},{3,7},{7,3},{8,12},{12,8},{9,1... | collective-permute-start | bytes 1585160 | tf_op jit(solution)/shard_map/ppermute | solution.py:45
  291.5 9.1 %copy-start.5 = (f32[1,16,64,128]{3,2,1,0:T(8,128)S(1)}, f32[1,16,64,128]{3,2,1,0:T(8,128)}, u32[]{:S(2)}) copy-start(f32[1,16,64,128]{3,2,1,0:T(8,128)} %copy-done.4) | copy-start | bytes 1572868
  291.5 9.1 %copy-start.8 = (f32[1,16,64,128]{3,2,1,0:T(8,128)S(1)}, f32[1,16,64,128]{3,2,1,0:T(8,128)}, u32[]{:S(2)}) copy-start(f32[1,16,64,128]{3,2,1,0:T(8,128)} %copy-done.7) | copy-start | bytes 1572868
  291.5 9.1 %copy-start.9 = (f32[6,16,64,128]{3,2,1,0:T(8,128)S(1)}, f32[6,16,64,128]{3,2,1,0:T(8,128)}, u32[]{:S(2)}) copy-start(f32[6,16,64,128]{3,2,1,0:T(8,128)} %constant_dynamic-update-slice_fusion.13) | copy-start | bytes 9437188
  291.5 9.1 %copy-start.32 = (f32[16]{0:T(128)S(1)}, f32[16]{0:T(128)}, u32[]{:S(2)}) copy-start(f32[16]{0:T(128)} %get-tuple-element.83) | copy-start | bytes 196
  294.8 9.3 %copy-start.6 = (f32[1,16,64,128]{3,2,1,0:T(8,128)S(1)}, f32[1,16,64,128]{3,2,1,0:T(8,128)}, u32[]{:S(2)}) copy-start(f32[1,16,64,128]{3,2,1,0:T(8,128)} %get-tuple-element.30) | copy-start | bytes 1572868
  294.8 27.6 %collective-permute-start.6 = (f32[1,1032,128]{2,1,0:T(8,128)S(1)}, f32[1,1032,128]{2,1,0:T(8,128)S(1)}, u32[]{:S(2)}, u32[]{:S(2)}) collective-permute-start(f32[1,1032,128]{2,1,0:T(8,128)S(1)} %select_maximum_fusion.4), channel_id=1, source_target_pairs={{0,24},{8,0},{16,8},{24,16},{1,25},{9,1},{17,9},{25,17},{2,26},{10... | collective-permute-start | bytes 1585160 | tf_op jit(solution)/shard_map/ppermute | solution.py:45
  294.9 27.5 %collective-permute-start.7 = (f32[1,1032,128]{2,1,0:T(8,128)S(1)}, f32[1,1032,128]{2,1,0:T(8,128)S(1)}, u32[]{:S(2)}, u32[]{:S(2)}) collective-permute-start(f32[1,1032,128]{2,1,0:T(8,128)S(1)} %select_maximum_fusion.4), channel_id=1, source_target_pairs={{0,16},{8,24},{16,0},{24,8},{1,17},{9,25},{17,1},{25,9},{2,18},{10... | collective-permute-start | bytes 1585160 | tf_op jit(solution)/shard_map/ppermute | solution.py:45
  295.7 27.5 %collective-permute-start.8 = (f32[1,1032,128]{2,1,0:T(8,128)S(1)}, f32[1,1032,128]{2,1,0:T(8,128)S(1)}, u32[]{:S(2)}, u32[]{:S(2)}) collective-permute-start(f32[1,1032,128]{2,1,0:T(8,128)S(1)} %select_maximum_fusion.4), channel_id=1, source_target_pairs={{0,8},{8,16},{16,24},{24,0},{1,9},{9,17},{17,25},{25,1},{2,10},{10... | collective-permute-start | bytes 1585160 | tf_op jit(solution)/shard_map/ppermute | solution.py:45
  301.0 41.2 %collective-permute-start.14 = (f32[1,1032,128]{2,1,0:T(8,128)S(1)}, f32[1,1032,128]{2,1,0:T(8,128)S(1)}, u32[]{:S(2)}, u32[]{:S(2)}) collective-permute-start(f32[1,1032,128]{2,1,0:T(8,128)S(1)} %select_maximum_fusion.1), channel_id=1, source_target_pairs={{0,24},{8,0},{16,8},{24,16},{1,25},{9,1},{17,9},{25,17},{2,26},{10... | collective-permute-start | bytes 1585160 | tf_op jit(solution)/shard_map/ppermute | solution.py:45
  301.9 42.1 %collective-permute-start.15 = (f32[1,1032,128]{2,1,0:T(8,128)S(1)}, f32[1,1032,128]{2,1,0:T(8,128)S(1)}, u32[]{:S(2)}, u32[]{:S(2)}) collective-permute-start(f32[1,1032,128]{2,1,0:T(8,128)S(1)} %select_maximum_fusion.1), channel_id=1, source_target_pairs={{0,16},{8,24},{16,0},{24,8},{1,17},{9,25},{17,1},{25,9},{2,18},{10... | collective-permute-start | bytes 1585160 | tf_op jit(solution)/shard_map/ppermute | solution.py:45
  322.4 21.7 %collective-permute-start.16 = (f32[1,1032,128]{2,1,0:T(8,128)S(1)}, f32[1,1032,128]{2,1,0:T(8,128)S(1)}, u32[]{:S(2)}, u32[]{:S(2)}) collective-permute-start(f32[1,1032,128]{2,1,0:T(8,128)S(1)} %select_maximum_fusion.1), channel_id=1, source_target_pairs={{0,8},{8,16},{16,24},{24,0},{1,9},{9,17},{17,25},{25,1},{2,10},{10... | collective-permute-start | bytes 1585160 | tf_op jit(solution)/shard_map/ppermute | solution.py:45
  323.8 22.9 %collective-permute-start.11 = (f32[1,1032,128]{2,1,0:T(8,128)S(1)}, f32[1,1032,128]{2,1,0:T(8,128)S(1)}, u32[]{:S(2)}, u32[]{:S(2)}) collective-permute-start(f32[1,1032,128]{2,1,0:T(8,128)S(1)} %select_maximum_fusion.3), channel_id=1, source_target_pairs={{0,96},{1,97},{2,98},{3,99},{4,100},{5,101},{6,102},{7,103},{8,104... | collective-permute-start | bytes 1585160 | tf_op jit(solution)/shard_map/ppermute | solution.py:45
  324.5 39.0 %collective-permute-start.10 = (f32[1,1032,128]{2,1,0:T(8,128)S(1)}, f32[1,1032,128]{2,1,0:T(8,128)S(1)}, u32[]{:S(2)}, u32[]{:S(2)}) collective-permute-start(f32[1,1032,128]{2,1,0:T(8,128)S(1)} %select_maximum_fusion.3), channel_id=1, source_target_pairs={{0,64},{32,96},{1,65},{33,97},{2,66},{34,98},{3,67},{35,99},{4,68}... | collective-permute-start | bytes 1585160 | tf_op jit(solution)/shard_map/ppermute | solution.py:45
  342.1 27.5 %collective-permute-start.9 = (f32[1,1032,128]{2,1,0:T(8,128)S(1)}, f32[1,1032,128]{2,1,0:T(8,128)S(1)}, u32[]{:S(2)}, u32[]{:S(2)}) collective-permute-start(f32[1,1032,128]{2,1,0:T(8,128)S(1)} %select_maximum_fusion.3), channel_id=1, source_target_pairs={{0,32},{32,64},{64,96},{1,33},{33,65},{65,97},{2,34},{34,66},{66,9... | collective-permute-start | bytes 1585160 | tf_op jit(solution)/shard_map/ppermute | solution.py:45
  344.7 32.1 %collective-permute-start.19 = (f32[1,1032,128]{2,1,0:T(8,128)S(1)}, f32[1,1032,128]{2,1,0:T(8,128)S(1)}, u32[]{:S(2)}, u32[]{:S(2)}) collective-permute-start(f32[1,1032,128]{2,1,0:T(8,128)S(1)} %select_maximum_fusion), channel_id=1, source_target_pairs={{0,96},{1,97},{2,98},{3,99},{4,100},{5,101},{6,102},{7,103},{8,104... | collective-permute-start | bytes 1585160 | tf_op jit(solution)/shard_map/ppermute | solution.py:45
  345.4 31.5 %collective-permute-start.18 = (f32[1,1032,128]{2,1,0:T(8,128)S(1)}, f32[1,1032,128]{2,1,0:T(8,128)S(1)}, u32[]{:S(2)}, u32[]{:S(2)}) collective-permute-start(f32[1,1032,128]{2,1,0:T(8,128)S(1)} %select_maximum_fusion), channel_id=1, source_target_pairs={{0,64},{32,96},{1,65},{33,97},{2,66},{34,98},{3,67},{35,99},{4,68}... | collective-permute-start | bytes 1585160 | tf_op jit(solution)/shard_map/ppermute | solution.py:45
  346.7 30.2 %collective-permute-start.17 = (f32[1,1032,128]{2,1,0:T(8,128)S(1)}, f32[1,1032,128]{2,1,0:T(8,128)S(1)}, u32[]{:S(2)}, u32[]{:S(2)}) collective-permute-start(f32[1,1032,128]{2,1,0:T(8,128)S(1)} %select_maximum_fusion), channel_id=1, source_target_pairs={{0,32},{32,64},{64,96},{1,33},{33,65},{65,97},{2,34},{34,66},{66,9... | collective-permute-start | bytes 1585160 | tf_op jit(solution)/shard_map/ppermute | solution.py:45
  (39 other events, 137.5 us)
Sparse Core Ops, SparseCore 0:
  25.0 89.6 all-gather.2
  116.8 92.3 all-gather.4

commit v11 on v7

--- a/solution.py
+++ b/solution.py
@@ -89,30 +89,34 @@
                 rows = rows_first
             source = (slot - distance) % pair
             pair_w = lax.dynamic_update_slice(pair_w, rows, (source * piece, 0, 0))
-        full_w = lax.all_gather(pair_w, SEQ[:2], axis=0, tiled=True)
+        plane_axes = SEQ[:2]
     else:
-        full_w = lax.all_gather(rows_first, SEQ, axis=0, tiled=True)
-    if after is not None:
-        full_w, _ = lax.optimization_barrier((full_w, after))
-    projected = jnp.einsum(
-        "td,dgc->tgc",
-        gathered,
-        full_w,
-        preferred_element_type=jnp.float32,
-    )
-    conv_in = projected[:, :, :CW].astype(jnp.bfloat16)
-    raw_dt = projected[:, :, CW:]
-    rim_rows = shifted(conv_in[row_count - (KCONV - 1) :], SEQ, 1)
-    padded = jnp.concatenate([rim_rows, conv_in], axis=0)
-    pre_act = jnp.broadcast_to(conv_b[None], (row_count, groups, CW))
-    for offset in range(KCONV):
-        pre_act = pre_act + conv_w[None, :, offset] * padded[offset : offset + row_count]
-    inputs = jax.nn.silu(pre_act).astype(jnp.bfloat16)
+        pair_w = rows_first
+        plane_axes = SEQ
+    cut = GW + N
+    first_w = jnp.concatenate([pair_w[..., :cut], pair_w[..., CW:]], axis=-1)
+    first_w = lax.all_gather(first_w, plane_axes, axis=0, tiled=True)
+    later_w = lax.all_gather(pair_w[..., cut:CW], plane_axes, axis=0, tiled=True)
+    first = jnp.einsum("td,dgc->tgc", gathered, first_w, preferred_element_type=jnp.float32)
+    later = jnp.einsum("td,dgc->tgc", gathered, later_w, preferred_element_type=jnp.float32)
+
+    def convolved(part, taps, shift):
+        conv_in = part.astype(jnp.bfloat16)
+        rim_rows = shifted(conv_in[row_count - (KCONV - 1) :], SEQ, 1)
+        padded = jnp.concatenate([rim_rows, conv_in], axis=0)
+        pre_act = jnp.broadcast_to(shift[None], (row_count,) + shift.shape)
+        for offset in range(KCONV):
+            pre_act = pre_act + taps[None, :, offset] * padded[offset : offset + row_count]
+        return jax.nn.silu(pre_act).astype(jnp.bfloat16)
+
+    inputs_xb = convolved(first[..., :cut], conv_w[..., :cut], conv_b[..., :cut])
+    raw_dt = first[..., cut:]
+    inputs_c = convolved(later, conv_w[..., cut:], conv_b[..., cut:])
     block_count = row_count // Q
-    blocked = inputs.reshape(block_count, Q, groups, CW)
+    blocked = inputs_xb.reshape(block_count, Q, groups, cut)
     x_all = blocked[..., :GW].reshape(block_count, Q, groups, HG, P_SIZE)
-    b_all = blocked[..., GW : GW + N]
-    c_all = blocked[..., GW + N :]
+    b_all = blocked[..., GW:]
+    c_all = inputs_c.reshape(block_count, Q, groups, N)
     step_dt = jax.nn.softplus(raw_dt + dt_bias[None]).reshape(block_count, Q, groups, HG)
     decay_rate = -jnp.exp(a_log)
     cumulative = jnp.cumsum(decay_rate[None, None] * step_dt, axis=1)
@@ -178,16 +182,10 @@
             piece = tokens
         source = (place - distance) % size
         gathered = lax.dynamic_update_slice(gathered, piece, (0, source * width))
-    outputs = []
-    after = None
-    for g in range(w_in.shape[0]):
-        one = slice(g, g + 1)
-        normed, after = mix_groups(
-            gathered, w_in[one], conv_w[one], conv_b[one], dt_bias[one],
-            a_log[one], d_skip[one], norm_gain[one], after,
-        )
-        outputs.append(normed)
-    return jnp.concatenate(outputs, axis=1)
+    normed, _ = mix_groups(
+        gathered, w_in, conv_w, conv_b, dt_bias, a_log, d_skip, norm_gain, None
+    )
+    return normed
 
 
 def split_mesh(mesh):

time: 394 us -> 454 us (1.15)
  waiting for transfers between devices: 155 us -> 220 us
  starting transfers between devices: 50.8 us -> 25.2 us
  other arithmetic: 49.5 us -> 67.9 us
  local copies, waits for them, and re-layouts: 67 us -> 81.6 us
  matrix products: 50.1 us -> 36.9 us
    ppermute x2, waiting for transfers between devices: 5.09 us -> 33.4 us  [shifted(): return lax.ppermute(block, axis, route)]
    ppermute x14 -> x7, starting transfers between devices: 34.1 us -> 9.01 us  [gather_level(): got = lax.ppermute(packed, axis, route)]
    ppermute x14 -> x7, waiting for transfers between devices: 41.2 us -> 63.4 us  [gather_level(): got = lax.ppermute(packed, axis, route)]
    slice x0 -> x2, other arithmetic: none -> 10.9 us  [the longest x1 8.24 us: gather_level(): received.append((got[:, body, :heads], got[:, :body].reshape(shape)))]
    add x1, other arithmetic: 1.21 us -> 11.8 us  [mix_groups(): state_now = keep_all[q][..., None, None] * state_now + fresh_all[q]]
    all_gather x2, waiting for transfers between devices: 45.7 us -> 55.6 us  [the longest x1 55.6 us: mix_groups(): first_w = lax.all_gather(first_w, plane_axes, axis=0, tiled=True)]
    convert_element_type x4 -> x2, other arithmetic: 21.5 us -> 12.9 us  [convolved(): return jax.nn.silu(pre_act).astype(jnp.bfloat16)]
    mul x4 -> x12, local copies, waits for them, and re-layouts: 0.01 us -> 6.82 us  [combine(): later[0][..., None, None] * earlier[1] + later[1]]
  transfers between devices with their start and end apart: 23 -> 15, of which waited for: 11 -> 8; matrix products, arithmetic and copies ran while one was open for 34% -> 31% of each run, Pallas kernels for 0% -> 0%
where the time goes in v11:
time: 454 us; the launch traced here: 447 us
  waiting for transfers between devices  220 us (48%)
  local copies, waits for them, and re-layouts  81.6 us (18%)
  other arithmetic  67.9 us (15%)
  matrix products  36.9 us (8%)
  starting transfers between devices  25.2 us (6%)
  between operations  14.7 us (3%)
    ppermute x7, waiting for transfers between devices, gather_level(): got = lax.ppermute(packed, axis, route)  63.4 us
    all_gather x1, waiting for transfers between devices, mix_groups(): first_w = lax.all_gather(first_w, plane_axes, axis=0, tiled=True)  55.6 us
    ppermute x3, waiting for transfers between devices, per_device(): lax.ppermute(tokens, 'chan', [(i, (i + distance) % size) for i in range(s...  54 us
    ppermute x2, waiting for transfers between devices, shifted(): return lax.ppermute(block, axis, route)  33.4 us
    dot_general x1, matrix products, mix_groups(): jnp.einsum('td,dgc->tgc', gathered, first_w, preferred_element_type=jnp.f...  20.9 us
    ppermute x1, waiting for transfers between devices, mix_groups(): lax.ppermute(rows_first, SEQ[2], [(i, (i + distance) % pair) for i in ran...  13.9 us
    convert_element_type x2, other arithmetic, convolved(): return jax.nn.silu(pre_act).astype(jnp.bfloat16)  12.9 us
    add x1, other arithmetic, mix_groups(): state_now = keep_all[q][..., None, None] * state_now + fresh_all[q]  11.8 us
  transfers between devices with their start and end apart: 15, of which 8 were waited for; matrix products, arithmetic and copies ran while one was open for 31% of the time, Pallas kernels for 0%

profile of v11, /device:TPU:22, one launch (start us, length us, event | category | flops | bytes accessed | tf_op | source)
XLA Modules:
  0.0 446.5 jit_solution(12456876121992115238)
XLA Ops:
  9.8 13.9 %collective-permute-done.3 = bf16[128,2,1296]{0,2,1:T(8,128)(2,1)} collective-permute-done((bf16[128,2,1296]{0,2,1:T(8,128)(2,1)}, bf16[128,2,1296]{0,2,1:T(8,128)(2,1)}, u32[]{:S(2)}, u32[]{:S(2)}) %collective-permute-start.3) | collective-permute-done | bytes 663584 | tf_op jit(solution)/shard_map/ppermute | solution.py:85
  26.3 3.2 collective-permute-start.2
  29.5 3.7 collective-permute-start.1
  33.8 3.4 broadcast_in_dim.13
  41.5 19.0 %collective-permute-done = bf16[768,1024]{1,0:T(8,128)(2,1)} collective-permute-done((bf16[768,1024]{1,0:T(8,128)(2,1)S(1)}, bf16[768,1024]{1,0:T(8,128)(2,1)}, u32[]{:S(2)}, u32[]{:S(2)}) %collective-permute-start) | collective-permute-done | bytes 1572896 | tf_op jit(solution)/shard_map/ppermute | solution.py:178
  60.5 2.8 constant_dynamic-update-slice_fusion.12
  63.3 35.0 %collective-permute-done.1 = bf16[768,1024]{1,0:T(8,128)(2,1)} collective-permute-done((bf16[768,1024]{1,0:T(8,128)(2,1)S(1)}, bf16[768,1024]{1,0:T(8,128)(2,1)}, u32[]{:S(2)}, u32[]{:S(2)}) %collective-permute-start.1) | collective-permute-done | bytes 1572896 | tf_op jit(solution)/shard_map/ppermute | solution.py:178
  98.3 2.8 constant_dynamic-update-slice_fusion.11
  101.1 2.7 constant_dynamic-update-slice_fusion.10
  103.7 55.6 %all-gather.3.cloned.1.call-done = bf16[4096,2,1168]{0,2,1:T(8,128)(2,1)} async-done(((bf16[256,2,1168]{0,2,1:T(8,128)(2,1)}), bf16[4096,2,1168]{0,2,1:T(8,128)(2,1)}) %all-gather.3.cloned.1.call-update) | async-done | bytes 19136528 | tf_op jit(solution)/shard_map/all_gather | solution.py:98
  159.4 20.9 %fusion.66 = (bf16[768,2,1168]{0,2,1:T(8,128)(2,1)}, f32[768,2,1168]{0,2,1:T(8,128)S(1)}) fusion(bf16[4096,2,1168]{0,2,1:T(8,128)(2,1)} %all-gather.3.cloned.1.call-done, bf16[768,4096]{1,0:T(8,128)(2,1)} %constant_dynamic-update-slice_fusion.10), kind=kOutput, calls=%fused_computation.163 | convolution fusion | flops 14698635264 | bytes 36192256 | tf_op jit(solution)/shard_map/td,dgc->tgc/dot_general | solution.py:100
  184.2 3.6 collective-permute-start.4
  204.2 9.9 %multiply_convert_fusion.1 = bf16[768,2,1152]{0,2,1:T(8,128)(2,1)} fusion(bf16[768,2,1152]{0,2,1:T(8,128)(2,1)S(1)} %slice.229, bf16[3,2,1152]{0,2,1:T(8,128)(2,1)} %copy.131, f32[2,1152]{1,0:T(2,128)} %get-tuple-element.59, f32[2,1152]{1,0:T(2,128)} %get-tuple-element.60, f32[2,1152]{1,0:T(2,128)} %get-tuple-element.61, f32[2,1152]{1,0:T(2,128)} %get-tuple-element.62, ...), kind=kLoop, calls=%fused_computation.3 | loop fusion | flops 46006272 | bytes 7137792 | tf_op jit(solution)/shard_map/convert_element_type | solution.py:110
  214.1 4.4 copy.132
  220.6 4.7 %copy.133 = bf16[6,128,2,1024]{1,3,2,0:T(8,128)(2,1)} copy(bf16[6,128,2,1024]{3,1,0,2:T(8,128)(2,1)} %slice.234) | data formatting | bytes 6291456 | tf_op jit(solution)/shard_map/slice | solution.py:117
  225.3 2.9 fusion.19
  228.2 2.7 fusion.61
  231.7 11.8 %copy_add_fusion.7 = f32[2,1024,128]{2,0,1:T(2,128)S(1)} fusion(f32[2,1024,128]{2,1,0:T(8,128)S(1)} %bitcast.180, f32[2,1024,128]{2,1,0:T(8,128)S(1)} %bitcast.181, f32[2,1024,128]{2,1,0:T(8,128)S(1)} %bitcast.182, f32[2,1024,128]{2,1,0:T(8,128)S(1)} %bitcast.183, f32[2,1024,128]{2,1,0:T(8,128)S(1)} %bitcast.184, f32[2,1024,128]{2,1,0:T(8,128)S(1)} %bitcast.179, ...), kind=kLoop, calls=%fused_computation.60 | loop fusion | flops 2883584 | bytes 7389184 | tf_op jit(solution)/shard_map/add | solution.py:142
  250.8 21.0 %collective-permute-done.6 = f32[2,1032,128]{2,0,1:T(2,128)} collective-permute-done((f32[2,1032,128]{2,0,1:T(2,128)}, f32[2,1032,128]{2,0,1:T(2,128)}, u32[]{:S(2)}, u32[]{:S(2)}) %collective-permute-start.6) | collective-permute-done | bytes 1056800 | tf_op jit(solution)/shard_map/ppermute | solution.py:45
  278.0 8.0 %add_select_fusion.1 = (f32[2,1024,128]{2,0,1:T(2,128)S(1)}, f32[2,1024,128]{2,0,1:T(2,128)}) fusion(f32[2,1024,128]{2,0,1:T(2,128)} %copy-done.4, pred[]{:T(512)S(6)} %ge.25, pred[]{:T(512)S(6)} %lt.68, f32[2,1024]{0,1:T(8,128)S(1)} %bitcast.198, f32[2,1024]{0,1:T(8,128)S(1)} %bitcast.199, f32[2,1024]{0,1:T(8,128)S(1)} %bitcast.200, ...), kind=kLoop, calls=%fused_computation.72 | loop fusion | flops 1835008 | bytes 4218882 | tf_op jit(solution)/shard_map/jit(_where)/select_n | solution.py:58
  291.4 5.2 %fusion.24 = bf16[768,2,128]{2,0,1:T(8,128)(2,1)S(1)} fusion(bf16[4096,2,128]{0,2,1:T(8,128)(2,1)} %all-gather.5.cloned.1.call-done, bf16[768,4096]{1,0:T(8,128)(2,1)} %constant_dynamic-update-slice_fusion.10), kind=kOutput, calls=%fused_computation.36 | convolution fusion | flops 1610809344 | bytes 8781824 | tf_op jit(solution)/shard_map/td,dgc->tgc/dot_general | solution.py:101
  298.0 3.6 collective-permute-start.5
  302.9 33.4 %collective-permute-done.5 = bf16[3,2,128]{2,0,1:T(4,128)(2,1)} collective-permute-done((bf16[3,2,128]{2,0,1:T(4,128)(2,1)}, bf16[3,2,128]{2,0,1:T(4,128)(2,1)}, u32[]{:S(2)}, u32[]{:S(2)}) %collective-permute-start.5) | collective-permute-done | bytes 1568 | tf_op jit(solution)/shard_map/ppermute | solution.py:22
  336.2 3.0 multiply_convert_fusion.5
  344.5 3.2 constant_dynamic-update-slice_fusion.1
  359.9 8.2 %fusion.62 = (f32[2,1024,128]{2,0,1:T(2,128)S(1)}, f32[2,1024,128]{2,0,1:T(2,128)S(1)}, f32[2,1024,128]{2,0,1:T(2,128)S(1)}, f32[2,1024,128]{2,0,1:T(2,128)S(1)}) fusion(f32[2,1032,128]{2,0,1:T(2,128)} %collective-permute-done.7, f32[2,1024,128]{2,0,1:T(2,128)} %copy-done.3, f32[2,1032,128]{2,0,1:T(2,128)} %collective-permute-done.9, ...), kind=kLoop, calls=%fused_computation.159 | loop fusion | flops 4980736 | bytes 8429574 | tf_op jit(solution)/shard_map/slice | solution.py:46
  376.0 24.0 %collective-permute-done.11 = f32[2,1032,128]{2,0,1:T(2,128)S(1)} collective-permute-done((f32[2,1032,128]{2,0,1:T(2,128)S(1)}, f32[2,1032,128]{2,0,1:T(2,128)S(1)}, u32[]{:S(2)}, u32[]{:S(2)}) %collective-permute-start.11) | collective-permute-done | bytes 1056800 | tf_op jit(solution)/shard_map/ppermute | solution.py:45
  400.1 18.4 %collective-permute-done.10 = f32[2,1032,128]{2,0,1:T(2,128)S(1)} collective-permute-done((f32[2,1032,128]{2,0,1:T(2,128)S(1)}, f32[2,1032,128]{2,0,1:T(2,128)S(1)}, u32[]{:S(2)}, u32[]{:S(2)}) %collective-permute-start.10) | collective-permute-done | bytes 1056800 | tf_op jit(solution)/shard_map/ppermute | solution.py:45
  418.7 3.0 fusion.28
  423.8 5.6 %multiply_reduce_fusion = (f32[6,128,2]{1,2,0:T(2,128)S(1)}, f32[6,128,2,16,64]{1,4,3,2,0:T(8,128)S(1)}) fusion(f32[6,2,16,64,128]{4,3,2,1,0:T(8,128)S(1)} %fusion.18, f32[6,128,2,16]{1,3,2,0:T(8,128)S(1)} %copy-done.15, bf16[6,128,2,16,64]{1,4,3,2,0:T(8,128)(2,1)S(1)} %bitcast.170, f32[2,16]{1,0:T(2,128)S(1)} %copy-done.43, ...), kind=kOutput, calls=%fused_computation.16 | convolution fusion | flops 432536064 | bytes 16832640 | tf_op jit(solution)/shard_map/qghij,qjghp->qighp/dot_general | solution.py:153
  429.4 5.8 %copy.172 = f32[6,128,2,16,64]{1,0,4,3,2:T(8,128)S(1)} copy(f32[6,128,2,16,64]{1,4,3,2,0:T(8,128)S(1)} %get-tuple-element.58) | data formatting | bytes 12582912 | tf_op jit(solution)/shard_map/add | solution.py:164
  436.4 2.9 copy.173
  (206 shorter events, 83.7 us)
Async XLA Ops:
  6.5 19.7 %copy-start.10 = (bf16[768,1024]{1,0:T(8,128)(2,1)S(1)}, bf16[768,1024]{1,0:T(8,128)(2,1)}, u32[]{:S(2)}) copy-start(bf16[768,1024]{1,0:T(8,128)(2,1)} %param.8) | copy-start | bytes 4718596
  6.5 26.7 %copy-start.26 = (f32[2,1280]{1,0:T(2,128)S(1)}, f32[2,1280]{1,0:T(2,128)}, u32[]{:S(2)}) copy-start(f32[2,1280]{1,0:T(2,128)} %param.11) | copy-start | bytes 30724
  6.5 152.8 %all-gather.3.cloned.1.call-start = ((), (), s32[]{:S(2)}) async-start(), calls=%async_computation | async-start | bytes 20332544 | tf_op jit(solution)/shard_map/all_gather | solution.py:98
  6.5 17.1 %collective-permute-start.3 = (bf16[128,2,1296]{0,2,1:T(8,128)(2,1)}, bf16[128,2,1296]{0,2,1:T(8,128)(2,1)}, u32[]{:S(2)}, u32[]{:S(2)}) collective-permute-start(bf16[128,2,1296]{0,2,1:T(8,128)(2,1)} %bitcast.202), channel_id=1, source_target_pairs={{0,4},{4,0},{1,5},{5,1},{2,6},{6,2},{3,7},{7,3},{8,12},{12,8},{9,1... | collective-permute-start | bytes 1990664 | tf_op jit(solution)/shard_map/ppermute | solution.py:85
  25.0 13.5 %copy-start.42 = (f32[2,16]{1,0:T(2,128)S(1)}, f32[2,16]{1,0:T(2,128)}, u32[]{:S(2)}) copy-start(f32[2,16]{1,0:T(2,128)} %param.13) | copy-start | bytes 388
  26.2 265.2 %all-gather.5.cloned.1.call-start = ((), (), s32[]{:S(2)}) async-start(), calls=%async_computation.1 | async-start | bytes 2228224 | tf_op jit(solution)/shard_map/all_gather | solution.py:99
  26.2 34.3 %collective-permute-start = (bf16[768,1024]{1,0:T(8,128)(2,1)S(1)}, bf16[768,1024]{1,0:T(8,128)(2,1)}, u32[]{:S(2)}, u32[]{:S(2)}) collective-permute-start(bf16[768,1024]{1,0:T(8,128)(2,1)S(1)} %copy-done.10), channel_id=1, source_target_pairs={{0,1},{1,2},{2,3},{3,0},{4,5},{5,6},{6,7},{7,4},{8,9},{9,10},{10,1... | collective-permute-start | bytes 4718600 | tf_op jit(solution)/shard_map/ppermute | solution.py:178
  26.3 74.8 %collective-permute-start.2 = (bf16[768,1024]{1,0:T(8,128)(2,1)S(1)}, bf16[768,1024]{1,0:T(8,128)(2,1)}, u32[]{:S(2)}, u32[]{:S(2)}) collective-permute-start(bf16[768,1024]{1,0:T(8,128)(2,1)S(1)} %copy-done.10), channel_id=1, source_target_pairs={{0,3},{1,0},{2,1},{3,2},{4,7},{5,4},{6,5},{7,6},{8,11},{9,8},{10,9... | collective-permute-start | bytes 4718600 | tf_op jit(solution)/shard_map/ppermute | solution.py:178
  29.5 68.8 %collective-permute-start.1 = (bf16[768,1024]{1,0:T(8,128)(2,1)S(1)}, bf16[768,1024]{1,0:T(8,128)(2,1)}, u32[]{:S(2)}, u32[]{:S(2)}) collective-permute-start(bf16[768,1024]{1,0:T(8,128)(2,1)S(1)} %copy-done.10), channel_id=1, source_target_pairs={{0,2},{1,3},{2,0},{3,1},{4,6},{5,7},{6,4},{7,5},{8,10},{9,11},{10,... | collective-permute-start | bytes 4718600 | tf_op jit(solution)/shard_map/ppermute | solution.py:178
  103.7 76.5 %copy-start.41 = (f32[2,16]{1,0:T(2,128)S(1)}, f32[2,16]{1,0:T(2,128)}, u32[]{:S(2)}) copy-start(f32[2,16]{1,0:T(2,128)} %param.12) | copy-start | bytes 388
  184.2 18.2 %collective-permute-start.4 = (bf16[3,2,1152]{2,1,0:T(2,128)(2,1)}, bf16[3,2,1152]{2,1,0:T(2,128)(2,1)}, u32[]{:S(2)}, u32[]{:S(2)}) collective-permute-start(bf16[3,2,1152]{2,1,0:T(2,128)(2,1)} %copy.130), channel_id=1, source_target_pairs={{0,4},{4,8},{8,12},{12,16},{16,20},{20,24},{24,28},{28,32},{32,36}... | collective-permute-start | bytes 41480 | tf_op jit(solution)/shard_map/ppermute | solution.py:22
  231.7 40.1 %copy-start.35 = (f32[2,1,16]{2,0,1:T(2,128)S(1)}, f32[2,1,16]{2,0,1:T(2,128)}, u32[]{:S(2)}) copy-start(f32[2,1,16]{2,0,1:T(2,128)} %get-tuple-element.49) | copy-start | bytes 388
  246.8 25.0 %collective-permute-start.6 = (f32[2,1032,128]{2,0,1:T(2,128)}, f32[2,1032,128]{2,0,1:T(2,128)}, u32[]{:S(2)}, u32[]{:S(2)}) collective-permute-start(f32[2,1032,128]{2,0,1:T(2,128)} %select_maximum_fusion.2), channel_id=1, source_target_pairs={{0,4},{4,0},{1,5},{5,1},{2,6},{6,2},{3,7},{7,3},{8,12},{12,8},{9,1... | collective-permute-start | bytes 3170312 | tf_op jit(solution)/shard_map/ppermute | solution.py:45
  289.3 47.0 %slice-start.2 = ((f32[2,1280]{1,0:T(2,128)}), f32[2,128]{1,0:T(2,128)S(1)}, s32[]{:S(2)}) async-start(f32[2,1280]{1,0:T(2,128)} %param.11), calls=%async_computation.4 | async-start | bytes 2048 | tf_op jit(solution)/shard_map/slice | solution.py:114
  289.3 55.2 %copy-start.25 = (f32[2,16]{1,0:T(2,128)S(1)}, f32[2,16]{1,0:T(2,128)}, u32[]{:S(2)}) copy-start(f32[2,16]{1,0:T(2,128)} %bitcast_multiply_fusion.3) | copy-start | bytes 388
  289.3 59.2 %collective-permute-start.9 = (f32[2,1032,128]{2,0,1:T(2,128)}, f32[2,1032,128]{2,0,1:T(2,128)}, u32[]{:S(2)}, u32[]{:S(2)}) collective-permute-start(f32[2,1032,128]{2,0,1:T(2,128)} %select_maximum_fusion.1), channel_id=1, source_target_pairs={{0,8},{8,16},{16,24},{24,0},{1,9},{9,17},{17,25},{25,1},{2,10},{10... | collective-permute-start | bytes 3170312 | tf_op jit(solution)/shard_map/ppermute | solution.py:45
  289.3 59.1 %collective-permute-start.8 = (f32[2,1032,128]{2,0,1:T(2,128)}, f32[2,1032,128]{2,0,1:T(2,128)}, u32[]{:S(2)}, u32[]{:S(2)}) collective-permute-start(f32[2,1032,128]{2,0,1:T(2,128)} %select_maximum_fusion.1), channel_id=1, source_target_pairs={{0,16},{8,24},{16,0},{24,8},{1,17},{9,25},{17,1},{25,9},{2,18},{10... | collective-permute-start | bytes 3170312 | tf_op jit(solution)/shard_map/ppermute | solution.py:45
  291.4 57.1 %collective-permute-start.7 = (f32[2,1032,128]{2,0,1:T(2,128)}, f32[2,1032,128]{2,0,1:T(2,128)}, u32[]{:S(2)}, u32[]{:S(2)}) collective-permute-start(f32[2,1032,128]{2,0,1:T(2,128)} %select_maximum_fusion.1), channel_id=1, source_target_pairs={{0,24},{8,0},{16,8},{24,16},{1,25},{9,1},{17,9},{25,17},{2,26},{10... | collective-permute-start | bytes 3170312 | tf_op jit(solution)/shard_map/ppermute | solution.py:45
  298.0 38.2 %collective-permute-start.5 = (bf16[3,2,128]{2,0,1:T(4,128)(2,1)}, bf16[3,2,128]{2,0,1:T(4,128)(2,1)}, u32[]{:S(2)}, u32[]{:S(2)}) collective-permute-start(bf16[3,2,128]{2,0,1:T(4,128)(2,1)} %slice.236), channel_id=1, source_target_pairs={{0,4},{4,8},{8,12},{12,16},{16,20},{20,24},{24,28},{28,32},{32,36}... | collective-permute-start | bytes 4616 | tf_op jit(solution)/shard_map/ppermute | solution.py:22
  358.0 14.9 %slice-start = ((s8[6291456]{0:T(1024)(128)(4,1)}), s8[4194304]{0:T(1024)(128)(4,1)S(1)}, s32[]{:S(2)}) async-start(s8[6291456]{0:T(1024)(128)(4,1)} %bitcast.163), calls=%async_computation.2 | async-start | bytes 8388608
  359.9 15.6 %copy-start.30 = (f32[2,16]{1,0:T(2,128)S(1)}, f32[2,16]{1,0:T(2,128)}, u32[]{:S(2)}) copy-start(f32[2,16]{1,0:T(2,128)} %get-tuple-element.52) | copy-start | bytes 388
  369.6 6.3 %collective-permute-start.12 = (f32[2,1032,128]{2,0,1:T(2,128)S(1)}, f32[2,1032,128]{2,0,1:T(2,128)S(1)}, u32[]{:S(2)}, u32[]{:S(2)}) collective-permute-start(f32[2,1032,128]{2,0,1:T(2,128)S(1)} %select_maximum_fusion), channel_id=1, source_target_pairs={{0,96},{1,97},{2,98},{3,99},{4,100},{5,101},{6,102},{7,103},{8,104... | collective-permute-start | bytes 3170312 | tf_op jit(solution)/shard_map/ppermute | solution.py:45
  370.3 29.7 %collective-permute-start.11 = (f32[2,1032,128]{2,0,1:T(2,128)S(1)}, f32[2,1032,128]{2,0,1:T(2,128)S(1)}, u32[]{:S(2)}, u32[]{:S(2)}) collective-permute-start(f32[2,1032,128]{2,0,1:T(2,128)S(1)} %select_maximum_fusion), channel_id=1, source_target_pairs={{0,64},{32,96},{1,65},{33,97},{2,66},{34,98},{3,67},{35,99},{4,68}... | collective-permute-start | bytes 3170312 | tf_op jit(solution)/shard_map/ppermute | solution.py:45
  373.1 45.5 %copy-start.7 = (f32[2,1024,128]{2,0,1:T(2,128)S(1)}, f32[2,1024,128]{2,0,1:T(2,128)}, u32[]{:S(2)}) copy-start(f32[2,1024,128]{2,0,1:T(2,128)} %get-tuple-element.35) | copy-start | bytes 3145732
  373.1 45.5 %copy-start.27 = (f32[2,16]{1,0:T(2,128)S(1)}, f32[2,16]{1,0:T(2,128)}, u32[]{:S(2)}) copy-start(f32[2,16]{1,0:T(2,128)} %get-tuple-element.21) | copy-start | bytes 388
  373.1 45.5 %copy-start.28 = (f32[2,16]{1,0:T(2,128)S(1)}, f32[2,16]{1,0:T(2,128)}, u32[]{:S(2)}) copy-start(f32[2,16]{1,0:T(2,128)} %get-tuple-element.25) | copy-start | bytes 388
  373.1 45.5 %copy-start.32 = (f32[2,16]{1,0:T(2,128)S(1)}, f32[2,16]{1,0:T(2,128)}, u32[]{:S(2)}) copy-start(f32[2,16]{1,0:T(2,128)} %get-tuple-element.30) | copy-start | bytes 388
  373.2 45.5 %copy-start.33 = (f32[2,16]{1,0:T(2,128)S(1)}, f32[2,16]{1,0:T(2,128)}, u32[]{:S(2)}) copy-start(f32[2,16]{1,0:T(2,128)} %get-tuple-element.32) | copy-start | bytes 388
  373.2 45.5 %copy-start.38 = (f32[2,16]{1,0:T(2,128)S(1)}, f32[2,16]{1,0:T(2,128)}, u32[]{:S(2)}) copy-start(f32[2,16]{1,0:T(2,128)} %get-tuple-element.20) | copy-start | bytes 388
  373.2 45.5 %copy-start.39 = (f32[2,16]{1,0:T(2,128)S(1)}, f32[2,16]{1,0:T(2,128)}, u32[]{:S(2)}) copy-start(f32[2,16]{1,0:T(2,128)} %get-tuple-element.24) | copy-start | bytes 388
  373.2 45.3 %collective-permute-start.10 = (f32[2,1032,128]{2,0,1:T(2,128)S(1)}, f32[2,1032,128]{2,0,1:T(2,128)S(1)}, u32[]{:S(2)}, u32[]{:S(2)}) collective-permute-start(f32[2,1032,128]{2,0,1:T(2,128)S(1)} %select_maximum_fusion), channel_id=1, source_target_pairs={{0,32},{32,64},{64,96},{1,33},{33,65},{65,97},{2,34},{34,66},{66,9... | collective-permute-start | bytes 3170312 | tf_op jit(solution)/shard_map/ppermute | solution.py:45
  376.0 45.6 %copy-start.37 = (f32[6,2,16]{2,1,0:T(2,128)S(1)}, f32[6,2,16]{2,1,0:T(2,128)}, u32[]{:S(2)}) copy-start(f32[6,2,16]{2,1,0:T(2,128)} %copy-done.36) | copy-start | bytes 2308
  (30 other events, 170.2 us)
Sparse Core Ops, SparseCore 0:
  26.3 133.0 all-gather.2
  161.5 46.9 all-gather.4
